TPU v7x, 128 devices: a whole 4x4x4 slice. The times are simulated.
128 devices in a mesh: az: 16 (over x_hi, z, core), tm: 8 (over x_lo, y).
Axes of the slice: x: 4 (x_hi: 2, x_lo: 2; x = x_hi * 2 + x_lo), y: 4, z: 4, core: 2. Of those that a mesh axis runs over, the one named last changes fastest.
Arguments:
- pressure: bfloat16 [16, 64, 128, 4096], P(None, 'az', 'tm'), may hold values from -6 to 6
- offsets: int32 [128, 16], P('tm'), may hold values from -1 to 0
- frac: float32 [128, 16], P('tm'), may hold values from 0 to 1
Outputs:
- csm: float32 [256, 2, 1024, 1024], P('tm', None, 'az')
All inputs are finite; a program needn't handle non-finite values.
Results may differ from a plain program's by a relative error of at most 0.0065.
Values may be sent and summed in bfloat16 or wider, within the bound.
No kernel may reach another device: no remote copies, remote signals or barrier semaphores. Data moves between devices by JAX's collectives and lax.ppermute only.
A program may use at most 192 MiB of HBM per device.

v0:
```python
import math

import jax
import jax.numpy as jnp
from jax import lax
from jax.sharding import PartitionSpec as P

FREQS = 256


def extended(block, sides, width):
    for axis, dim in sides:
        count = lax.axis_size(axis)
        forward = [(i, i + 1) for i in range(count - 1)]
        forward.append((count - 1, 0))
        backward = [(target, source) for source, target in forward]
        low = lax.ppermute(
            lax.slice_in_dim(block, block.shape[dim] - width, None, axis=dim), axis, forward
        )
        high = lax.ppermute(lax.slice_in_dim(block, 0, width, axis=dim), axis, backward)
        block = jnp.concatenate([low, block, high], axis=dim)
    return block


def dft_table(length, freqs):
    times = jnp.arange(length, dtype=jnp.int32)
    bins = jnp.arange(1, freqs + 1, dtype=jnp.int32)
    phase = (times[:, None] * bins[None, :] % length).astype(jnp.float32) * (2.0 * math.pi / length)
    hann = 0.5 - 0.5 * jnp.cos(times.astype(jnp.float32) * (2.0 * math.pi / length))
    factor = hann[:, None] / math.sqrt(3.0 * length / 8.0)
    return jnp.concatenate([factor * jnp.cos(phase), -factor * jnp.sin(phase)], axis=1).astype(
        jnp.bfloat16
    )


def interp_weights(offsets, frac):
    rows = []
    for shift in range(-1, 2):
        low = (offsets == shift).astype(frac.dtype)
        high = (offsets + 1 == shift).astype(frac.dtype)
        rows.append((1.0 - frac) * low + frac * high)
    return jnp.stack(rows, 0)


def rotated_rows(rows):
    split = rows.reshape(rows.shape[0], rows.shape[1], rows.shape[2] // 2, 2)
    return jnp.stack([split[..., 1], -split[..., 0]], -1).reshape(rows.shape)


def cross_terms(rows, turned, columns):
    real = jnp.einsum("fqk,fpk->fqp", rows, columns, preferred_element_type=jnp.float32)
    imag = jnp.einsum("fqk,fpk->fqp", turned, columns, preferred_element_type=jnp.float32)
    return jnp.stack([real, imag], 1)


def shards(pressure, offsets, frac):
    cycles, sector, blocks, length = pressure.shape
    subs = offsets.shape[1]
    sub_len = length // subs
    padded = extended(pressure, (("az", 1),), 1)
    weights = interp_weights(offsets, frac)
    total = jnp.zeros((cycles, sector, blocks, subs, sub_len), jnp.float32)
    for shift in range(3):
        moved = padded[:, shift : shift + sector].reshape(cycles, sector, blocks, subs, sub_len)
        total = total + weights[shift][None, None, :, :, None] * moved
    virtual = total.astype(jnp.bfloat16).reshape(cycles * sector * blocks, length)
    table = dft_table(length, FREQS)
    freqs = table.shape[1] // 2
    spectra = jnp.dot(virtual, table, preferred_element_type=jnp.float32).astype(jnp.bfloat16)
    spectra = spectra.reshape(cycles, sector, blocks, 2, freqs).transpose(4, 1, 0, 2, 3)
    spectra = spectra.reshape(freqs, sector * cycles, blocks, 2)
    local_rows = sector * cycles
    gathered = lax.all_gather(spectra, "az", axis=1, tiled=True)
    shared = lax.all_to_all(gathered, "tm", split_axis=0, concat_axis=2, tiled=True)
    width = shared.shape[2]
    columns = shared.reshape(shared.shape[0], shared.shape[1], width * 2)
    start = lax.axis_index("az") * local_rows
    rows = lax.dynamic_slice_in_dim(columns, start, local_rows, 1)
    result = cross_terms(rows, rotated_rows(rows), columns)
    return result * (1.0 / width)


def solution(mesh):
    return jax.shard_map(
        shards,
        mesh=mesh,
        in_specs=(P(None, "az", "tm", None), P("tm", None), P("tm", None)),
        out_specs=P("tm", None, "az", None),
        check_vma=False,
    )
```

profile of v0, /device:TPU:1, one launch (start us, length us, event | category | flops | bytes accessed | tf_op | source)
XLA Modules:
  0.0 562.0 jit_solution(8039521140243428556)
XLA Ops:
  6.5 0.0 copy-start
  6.5 0.0 copy-start.1
  6.5 0.0 all-gather.2.cloned.1.call-start
  6.5 4.7 fusion.19
  11.3 3.0 collective-permute-start
  14.3 0.0 collective-permute-start.1
  14.3 0.0 copy-done
  14.3 0.0 copy-done.1
  14.3 2.1 mul.142
  16.5 19.6 %copy.35 = f32[128,8,16,256]{3,1,2,0:T(8,128)} copy(f32[128,8,16,256]{3,2,1,0:T(8,128)S(1)} %bitcast.38) | data formatting | bytes 33554432
  36.1 2.1 mul.137
  38.2 19.0 %copy.34 = f32[128,8,16,256]{3,1,2,0:T(8,128)} copy(f32[128,8,16,256]{3,2,1,0:T(8,128)S(1)} %bitcast.39) | data formatting | bytes 33554432
  57.3 2.1 mul.132
  59.4 0.0 slice-start
  59.4 0.0 slice-start.1
  59.4 19.3 %copy.33 = f32[128,8,16,256]{3,1,2,0:T(8,128)} copy(f32[128,8,16,256]{3,2,1,0:T(8,128)S(1)} %bitcast.40) | data formatting | bytes 33554432
  78.8 0.1 subtract_multiply_fusion
  78.8 0.0 slice-start.2
  78.8 19.2 %multiply_convert_fusion.1 = (bf16[4096,256]{1,0:T(8,128)(2,1)}, bf16[4096,256]{1,0:T(8,128)(2,1)}) fusion(s32[256]{0:T(256)S(1)} %iota_add_fusion, f32[4096]{0:T(1024)S(1)} %get-tuple-element.16, f32[4096]{0:T(1024)S(1)} %get-tuple-element.17), kind=kLoop, calls=%fused_computation.20 | loop fusion | flops 18874368 | bytes 4228096 | tf_op jit(solution)/shard_map/convert.3
  98.0 0.0 slice-start.3
  98.0 0.0 collective-permute-done
  98.0 0.0 collective-permute-done.1
  98.1 0.0 slice-done
  98.1 0.0 slice-done.1
  98.1 8.1 %pad_maximum_fusion.1 = (bf16[16,4,16,4096]{3,2,1,0:T(8,128)(2,1)}, bf16[16,4,16,4096]{3,2,1,0:T(8,128)(2,1)}) fusion(bf16[16,4,16,4096]{3,2,1,0:T(8,128)(2,1)S(1)} %bitcast.43, bf16[16,1,16,4096]{3,2,1,0:T(8,128)(2,1)} %collective-permute-done, bf16[16,1,16,4096]{3,2,1,0:T(8,128)(2,1)} %collective-permute-done.1), kind=kLoop, calls=%fused_computation.8 | loop fusion | flops 8388608 | bytes 29360128 | tf_op jit(solution)/shard_map/concatenate | solution.py:21
  106.1 0.0 slice-done.2
  106.2 0.0 slice-done.3
  106.2 26.0 %fusion.1 = bf16[1024,4096]{1,0:T(8,128)(2,1)} fusion(f32[1024,4096]{1,0:T(8,128)} %bitcast.35, f32[1024,4096]{1,0:T(8,128)} %bitcast.36, f32[1024,4096]{1,0:T(8,128)} %bitcast.37, bf16[16,4,16,4096]{3,2,1,0:T(8,128)(2,1)} %get-tuple-element.6, bf16[16,4,16,4096]{3,2,1,0:T(8,128)(2,1)S(1)} %bitcast.45, bf16[16,4,16,4096]{3,2,1,0:T(8,128)(2,1)} %get-tuple-element.5), kind=kLoop, calls=%fused_computation.3 | loop fusion | flops 37748736 | bytes 83886080 | tf_op jit(solution)/shard_map/convert_element_type | solution.py:66
  132.2 9.1 %fusion.14 = bf16[1024,512]{1,0:T(8,128)(2,1)S(1)} fusion(bf16[1024,4096]{1,0:T(8,128)(2,1)} %fusion.1, bf16[4096,256]{1,0:T(8,128)(2,1)} %get-tuple-element.15, bf16[4096,256]{1,0:T(8,128)(2,1)} %get-tuple-element.14), kind=kOutput, calls=%fused_computation.28 | convolution fusion | flops 4303880192 | bytes 13631488 | tf_op jit(solution)/shard_map/dot_general | solution.py:69
  141.2 0.5 reshape.53
  141.7 1.2 copy.24
  142.9 0.0 all-gather.2.cloned.1.call-update
  142.9 111.5 %all-gather.2.cloned.1.call-done = bf16[256,1024,16,2]{0,2,3,1:T(8,128)(2,1)} async-done(((bf16[256,64,16,2]{0,2,3,1:T(8,128)(2,1)}), bf16[256,1024,16,2]{0,2,3,1:T(8,128)(2,1)}) %all-gather.2.cloned.1.call-update) | async-done | bytes 16777232 | tf_op jit(solution)/shard_map/all_gather | solution.py:73
  254.4 26.0 %copy.25 = bf16[256,1024,16,2]{1,2,3,0:T(8,128)(2,1)} copy(bf16[256,1024,16,2]{0,2,3,1:T(8,128)(2,1)} %all-gather.2.cloned.1.call-done) | data formatting | bytes 33554432 | tf_op jit(solution)/shard_map/all_gather | solution.py:73
  280.4 5.7 %all-to-all-start = ((bf16[256,1024,16,2]{1,2,3,0:T(8,128)(2,1)}), bf16[256,1024,16,2]{1,2,3,0:T(8,128)(2,1)}, u32[]{:S(2)}, u32[]{:S(2)}) async-start(bf16[256,1024,16,2]{1,2,3,0:T(8,128)(2,1)} %copy.25), calls=%async_computation | async-start | bytes 33554432 | tf_op jit(solution)/shard_map/all_to_all | solution.py:74
  286.1 183.5 %all-to-all-done = bf16[256,1024,16,2]{1,2,3,0:T(8,128)(2,1)} async-done(((bf16[256,1024,16,2]{1,2,3,0:T(8,128)(2,1)}), bf16[256,1024,16,2]{1,2,3,0:T(8,128)(2,1)}, u32[]{:S(2)}, u32[]{:S(2)}) %all-to-all-start) | async-done | bytes 16777248 | tf_op jit(solution)/shard_map/all_to_all | solution.py:74
  469.6 18.6 %copy.26 = bf16[32,1024,8,16,2]{1,0,4,3,2:T(8,128)(2,1)} copy(bf16[32,1024,8,16,2]{1,3,4,0,2:T(8,128)(2,1)} %bitcast.6) | data formatting | bytes 33554432 | tf_op jit(solution)/shard_map/all_to_all | solution.py:74
  488.3 23.2 %copy.27 = bf16[32,1024,256]{2,1,0:T(8,128)(2,1)} copy(bf16[32,1024,256]{1,0,2:T(8,128)(2,1)} %bitcast.41) | data formatting | bytes 33554432 | tf_op jit(solution)/shard_map/reshape | solution.py:76
  511.5 1.3 constant_dynamic-slice_fusion
  512.8 3.1 copy.29
  515.9 14.2 %convolution_bitcast_fusion = f32[32,1,64,1024]{3,2,0,1:T(8,128)} fusion(bf16[32,64,256]{2,1,0:T(8,128)(2,1)S(1)} %constant_dynamic-slice_fusion, bf16[32,1024,256]{2,1,0:T(8,128)(2,1)} %copy.27), kind=kOutput, calls=%fused_computation.24 | convolution fusion | flops 1073741824 | bytes 26214400 | tf_op jit(solution)/shard_map/fqk,fpk->fqp/dot_general | solution.py:51
  530.0 0.2 fusion.20
  530.2 0.4 pad_maximum_fusion.2
  530.6 11.2 %convolution_bitcast_fusion.1 = f32[32,1,64,1024]{3,2,0,1:T(8,128)} fusion(bf16[32,1024,256]{2,1,0:T(8,128)(2,1)} %copy.27, bf16[32,64,256]{1,0,2:T(8,128)(2,1)S(1)} %bitcast.46), kind=kOutput, calls=%fused_computation.25 | convolution fusion | flops 1073741824 | bytes 26214400 | tf_op jit(solution)/shard_map/fqk,fpk->fqp/dot_general | solution.py:52
  541.9 6.8 %maximum_multiply_fusion = f32[32,2,64,1024]{3,2,0,1:T(8,128)S(1)} fusion(f32[32,1,64,1024]{3,2,0,1:T(8,128)} %convolution_bitcast_fusion.1, f32[32,1,64,1024]{3,2,0,1:T(8,128)} %convolution_bitcast_fusion), kind=kLoop, calls=%fused_computation | loop fusion | flops 8388608 | bytes 33554432 | tf_op jit(solution)/shard_map/mul | solution.py:80
  548.7 6.2 %copy.32 = f32[32,2,64,1024]{3,2,1,0:T(8,128)} copy(f32[32,2,64,1024]{3,2,0,1:T(8,128)S(1)} %maximum_multiply_fusion) | data formatting | bytes 33554432 | tf_op jit(solution)/shard_map/mul | solution.py:80
  (4 shorter events, 0.0 us)
Async XLA Ops:
  6.5 7.8 %copy-start = (f32[16,16]{1,0:T(8,128)S(1)}, f32[16,16]{1,0:T(8,128)}, u32[]{:S(2)}) copy-start(f32[16,16]{1,0:T(8,128)} %param.5) | copy-start | bytes 3076
  6.5 7.8 %copy-start.1 = (s32[16,16]{1,0:T(8,128)S(1)}, s32[16,16]{1,0:T(8,128)}, u32[]{:S(2)}) copy-start(s32[16,16]{1,0:T(8,128)} %param.4) | copy-start | bytes 3076
  6.5 247.9 %all-gather.2.cloned.1.call-start = ((), (), s32[]{:S(2)}) async-start(), calls=%async_computation.1 | async-start | bytes 17825792 | tf_op jit(solution)/shard_map/all_gather | solution.py:73
  11.3 86.8 %collective-permute-start = (bf16[16,1,16,4096]{3,2,1,0:T(8,128)(2,1)}, bf16[16,1,16,4096]{3,2,1,0:T(8,128)(2,1)}, u32[]{:S(2)}, u32[]{:S(2)}) collective-permute-start(bf16[16,1,16,4096]{3,2,1,0:T(8,128)(2,1)} %get-tuple-element.7), channel_id=1, source_target_pairs={{0,8},{8,16},{16,24},{24,32},{32,40},{40,48},{48,56},{56,64},{64,7... | collective-permute-start | bytes 6291464 | tf_op jit(solution)/shard_map/ppermute | solution.py:17
  14.3 83.8 %collective-permute-start.1 = (bf16[16,1,16,4096]{3,2,1,0:T(8,128)(2,1)}, bf16[16,1,16,4096]{3,2,1,0:T(8,128)(2,1)}, u32[]{:S(2)}, u32[]{:S(2)}) collective-permute-start(bf16[16,1,16,4096]{3,2,1,0:T(8,128)(2,1)} %get-tuple-element.8), channel_id=1, source_target_pairs={{8,0},{16,8},{24,16},{32,24},{40,32},{48,40},{56,48},{64,56},{72,6... | collective-permute-start | bytes 6291464 | tf_op jit(solution)/shard_map/ppermute | solution.py:20
  59.4 38.7 %slice-start = ((s8[8388608]{0:T(1024)(128)(4,1)}), s8[4194304]{0:T(1024)(128)(4,1)S(1)}, s32[]{:S(2)}) async-start(s8[8388608]{0:T(1024)(128)(4,1)} %bitcast.42), calls=%async_computation.2 | async-start | bytes 8388608
  59.4 38.6 %slice-start.1 = ((s8[8388608]{0:T(1024)(128)(4,1)}), s8[4194304]{0:T(1024)(128)(4,1)S(1)}, s32[]{:S(2)}) async-start(s8[8388608]{0:T(1024)(128)(4,1)} %bitcast.42), calls=%async_computation.3 | async-start | bytes 8388608
  78.8 27.3 %slice-start.2 = ((s8[8388608]{0:T(1024)(128)(4,1)}), s8[4194304]{0:T(1024)(128)(4,1)S(1)}, s32[]{:S(2)}) async-start(s8[8388608]{0:T(1024)(128)(4,1)} %bitcast.44), calls=%async_computation.4 | async-start | bytes 8388608
  98.0 8.1 %slice-start.3 = ((s8[8388608]{0:T(1024)(128)(4,1)}), s8[4194304]{0:T(1024)(128)(4,1)S(1)}, s32[]{:S(2)}) async-start(s8[8388608]{0:T(1024)(128)(4,1)} %bitcast.44), calls=%async_computation.5 | async-start | bytes 8388608
  280.4 189.2 %all-to-all-start = ((bf16[256,1024,16,2]{1,2,3,0:T(8,128)(2,1)}), bf16[256,1024,16,2]{1,2,3,0:T(8,128)(2,1)}, u32[]{:S(2)}, u32[]{:S(2)}) async-start(bf16[256,1024,16,2]{1,2,3,0:T(8,128)(2,1)} %copy.25), calls=%async_computation | async-start | bytes 33554432 | tf_op jit(solution)/shard_map/all_to_all | solution.py:74
Sparse Core Ops, SparseCore 0:
  143.1 111.2 all-gather.1
where the time goes:
time: 566 us; the launch traced here: 562 us
  waiting for transfers between devices  295 us (52%)
  local copies, waits for them, and re-layouts  149 us (26%)
  other arithmetic  60.8 us (11%)
  matrix products  34.5 us (6%)
  between operations  13.8 us (2%)
  starting transfers between devices  8.76 us (2%)
    all_to_all x1, waiting for transfers between devices, shards(): lax.all_to_all(gathered, 'tm', split_axis=0, concat_axis=2, tiled=True)  183 us
    all_gather x1, waiting for transfers between devices, shards(): gathered = lax.all_gather(spectra, 'az', axis=1, tiled=True)  111 us
    unnamed x15, local copies, waits for them, and re-layouts  58 us
    convert_element_type x1, other arithmetic, shards(): total.astype(jnp.bfloat16).reshape(cycles * sector * blocks, length)  26 us
    all_gather x1, local copies, waits for them, and re-layouts, shards(): gathered = lax.all_gather(spectra, 'az', axis=1, tiled=True)  26 us
    reshape x1, local copies, waits for them, and re-layouts, shards(): columns = shared.reshape(shared.shape[0], shared.shape[1], width * 2)  23.2 us
    another operation x1, other arithmetic  19.2 us
    all_to_all x1, local copies, waits for them, and re-layouts, shards(): lax.all_to_all(gathered, 'tm', split_axis=0, concat_axis=2, tiled=True)  18.6 us
  transfers between devices with their start and end apart: 4, of which 2 were waited for; matrix products, arithmetic and copies ran while one was open for 15% of the time, Pallas kernels for 0%

commit v1 on v0

v1 whole, which is shorter than its diff:
```python
import math

import jax
import jax.numpy as jnp
from jax import lax
from jax.sharding import PartitionSpec as P

FREQS = 256


def dft_table(length, freqs):
    times = jnp.arange(length, dtype=jnp.int32)
    bins = jnp.arange(1, freqs + 1, dtype=jnp.int32)
    phase = (times[:, None] * bins[None, :] % length).astype(jnp.float32) * (2.0 * math.pi / length)
    hann = 0.5 - 0.5 * jnp.cos(times.astype(jnp.float32) * (2.0 * math.pi / length))
    factor = hann[:, None] / math.sqrt(3.0 * length / 8.0)
    return jnp.concatenate([factor * jnp.cos(phase), -factor * jnp.sin(phase)], axis=1).astype(
        jnp.bfloat16
    )


def interp_weights(offsets, frac):
    rows = []
    for shift in range(-1, 2):
        low = (offsets == shift).astype(frac.dtype)
        high = (offsets + 1 == shift).astype(frac.dtype)
        rows.append((1.0 - frac) * low + frac * high)
    return jnp.stack(rows, 0)


def shards(pressure, offsets, frac):
    cycles, sector, blocks, length = pressure.shape
    subs = offsets.shape[1]
    sub_len = length // subs
    n_az = lax.axis_size("az")
    n_tm = lax.axis_size("tm")
    forward = [(i, (i + 1) % n_az) for i in range(n_az)]
    backward = [((i + 1) % n_az, i) for i in range(n_az)]
    left = lax.ppermute(pressure[:, sector - 1 :], "az", forward)
    right = lax.ppermute(pressure[:, :1], "az", backward)
    weights = jnp.repeat(interp_weights(offsets, frac), sub_len, axis=2)[:, None, None]
    prev = jnp.concatenate([left, pressure[:, :-1]], axis=1).astype(jnp.float32)
    nxt = jnp.concatenate([pressure[:, 1:], right], axis=1).astype(jnp.float32)
    total = weights[0] * prev + weights[1] * pressure.astype(jnp.float32) + weights[2] * nxt
    virtual = total.astype(jnp.bfloat16).reshape(cycles * sector * blocks, length)
    table = dft_table(length, FREQS)
    freqs = FREQS
    spectra = jnp.dot(virtual, table, preferred_element_type=jnp.float32).astype(jnp.bfloat16)
    spectra = spectra.reshape(cycles, sector, blocks, 2, freqs).transpose(4, 1, 0, 3, 2)
    local_rows = sector * cycles
    spectra = spectra.reshape(n_tm, freqs // n_tm, local_rows, 2, blocks)
    shared = lax.all_to_all(spectra, "tm", 0, 0, tiled=True)
    shared = shared.reshape(n_tm, freqs // n_tm, local_rows, 2, blocks).transpose(1, 2, 3, 0, 4)
    fl = freqs // n_tm
    shared = shared.reshape(fl, local_rows, 2, n_tm * blocks)
    rows = shared.reshape(fl, local_rows, 2 * n_tm * blocks)
    turned = jnp.concatenate([shared[:, :, 1], -shared[:, :, 0]], axis=2)
    lhs = jnp.stack([rows, turned], 1)
    columns = lax.all_gather(rows, "az", axis=1, tiled=True)
    result = jnp.einsum("fcqk,fpk->fcqp", lhs, columns, preferred_element_type=jnp.float32)
    return result * (1.0 / (n_tm * blocks))


def solution(mesh):
    return jax.shard_map(
        shards,
        mesh=mesh,
        in_specs=(P(None, "az", "tm", None), P("tm", None), P("tm", None)),
        out_specs=P("tm", None, "az", None),
        check_vma=False,
    )
```

time: 566 us -> 219 us (0.39)
  waiting for transfers between devices: 295 us -> 110 us
  local copies, waits for them, and re-layouts: 149 us -> 30.7 us
  other arithmetic: 60.8 us -> 27 us
  matrix products: 34.5 us -> 19.2 us
  blocking collectives: 0 us -> 15.3 us
    all_to_all x1 -> x0, waiting for transfers between devices: 183 us -> none  [shards(): lax.all_to_all(gathered, 'tm', split_axis=0, concat_axis=2, tiled=True)]
    unnamed x15 -> x13, local copies, waits for them, and re-layouts: 58 us -> 10.5 us
    all_gather x1 -> x0, local copies, waits for them, and re-layouts: 26 us -> none  [shards(): gathered = lax.all_gather(spectra, 'az', axis=1, tiled=True)]
    all_to_all x1 -> x0, local copies, waits for them, and re-layouts: 18.6 us -> none  [shards(): lax.all_to_all(gathered, 'tm', split_axis=0, concat_axis=2, tiled=True)]
    convert_element_type x1, other arithmetic: 26 us -> 7.67 us  [shards(): total.astype(jnp.bfloat16).reshape(cycles * sector * blocks, length)]
    all_to_all x0 -> x1, blocking collectives: none -> 15.3 us  [shards(): shared = lax.all_to_all(spectra, 'tm', 0, 0, tiled=True)]
    reshape x3 -> x4, local copies, waits for them, and re-layouts: 24.9 us -> 10.7 us  [the longest x2 10.2 us: shards(): spectra = spectra.reshape(n_tm, freqs // n_tm, local_rows, 2, blocks)]
    dot_general x2 -> x1, matrix products: 25.4 us -> 12.5 us  [shards(): jnp.einsum('fcqk,fpk->fcqp', lhs, columns, preferred_element_type=jnp.flo...]
  transfers between devices with their start and end apart: 4 -> 3, of which waited for: 2 -> 2; matrix products, arithmetic and copies ran while one was open for 15% -> 13% of each run, Pallas kernels for 0% -> 0%
where the time goes in v1:
time: 219 us
  waiting for transfers between devices  110 us (50%)
  local copies, waits for them, and re-layouts  30.7 us (14%)
  other arithmetic  27 us (12%)
  matrix products  19.2 us (9%)
  blocking collectives  15.3 us (7%)
  between operations  13.6 us (6%)
  starting transfers between devices  3.17 us (1%)
    all_gather x1, waiting for transfers between devices, shards(): columns = lax.all_gather(rows, 'az', axis=1, tiled=True)  109 us
    another operation x1, other arithmetic  19.1 us
    all_to_all x1, blocking collectives, shards(): shared = lax.all_to_all(spectra, 'tm', 0, 0, tiled=True)  15.3 us
    dot_general x1, matrix products, shards(): jnp.einsum('fcqk,fpk->fcqp', lhs, columns, preferred_element_type=jnp.flo...  12.5 us
    unnamed x13, local copies, waits for them, and re-layouts  10.5 us
    reshape x2, local copies, waits for them, and re-layouts, shards(): spectra = spectra.reshape(n_tm, freqs // n_tm, local_rows, 2, blocks)  10.2 us
    convert_element_type x1, other arithmetic, shards(): total.astype(jnp.bfloat16).reshape(cycles * sector * blocks, length)  7.67 us
    dot_general x1, matrix products, shards(): jnp.dot(virtual, table, preferred_element_type=jnp.float32)  6.71 us
  transfers between devices with their start and end apart: 3, of which 2 were waited for; matrix products, arithmetic and copies ran while one was open for 13% of the time, Pallas kernels for 0%

profile of v1, /device:TPU:1, one launch (start us, length us, event | category | flops | bytes accessed | tf_op | source)
XLA Modules:
  0.0 218.6 jit_solution(10856519465996937360)
XLA Ops:
  6.5 0.0 copy-start.1
  6.5 0.0 copy-start.2
  6.5 0.0 all-gather.2.cloned.1.call-start
  6.5 0.0 copy-start
  6.5 2.6 %fusion.24 = (bf16[16,1,16,4096]{3,2,1,0:T(8,128)(2,1)S(1)}, bf16[16,1,16,4096]{3,2,1,0:T(8,128)(2,1)S(1)}) fusion(bf16[16,4,16,4096]{3,2,1,0:T(8,128)(2,1)} %param.3), kind=kLoop, calls=%fused_computation.35 | loop fusion | bytes 8388608 | tf_op jit(solution)/shard_map/slice | solution.py:40
  9.2 1.5 collective-permute-start.1
  10.6 1.7 collective-permute-start
  12.4 0.1 subtract_multiply_fusion
  12.4 0.0 copy-done.1
  12.5 0.0 copy-done.2
  12.5 0.1 broadcast_in_dim.16
  12.6 0.9 copy.25
  13.4 0.1 broadcast_in_dim.20
  13.6 0.9 copy.27
  14.4 0.1 broadcast_in_dim.18
  14.5 0.9 copy.26
  15.4 19.1 %multiply_convert_fusion.1 = (bf16[4096,256]{1,0:T(8,128)(2,1)}, bf16[4096,256]{1,0:T(8,128)(2,1)}) fusion(s32[256]{0:T(256)S(1)} %iota_add_fusion, f32[4096]{0:T(1024)S(1)} %get-tuple-element.16, f32[4096]{0:T(1024)S(1)} %get-tuple-element.17), kind=kLoop, calls=%fused_computation.15 | loop fusion | flops 18874368 | bytes 4228096 | tf_op jit(solution)/shard_map/convert
  34.4 0.0 copy-done
  34.4 1.5 fusion.23
  36.0 0.3 collective-permute-done.1
  36.3 0.0 collective-permute-done
  36.3 7.7 %add_convert_fusion = bf16[16,4,16,4096]{3,2,1,0:T(8,128)(2,1)S(1)} fusion(bf16[16,4,16,4096]{3,2,1,0:T(8,128)(2,1)S(1)} %copy-done, bf16[16,3,16,4096]{3,2,1,0:T(8,128)(2,1)S(1)} %get-tuple-element.6, bf16[16,1,16,4096]{3,2,1,0:T(8,128)(2,1)S(1)} %collective-permute-done, bf16[16,1,16,4096]{3,2,1,0:T(8,128)(2,1)S(1)} %collective-permute-done.1, ...), kind=kLoop, calls=%fused_computation.2 | loop fusion | flops 46137344 | bytes 34340864 | tf_op jit(solution)/shard_map/convert_element_type | solution.py:45
  44.0 6.7 %fusion.17 = bf16[1024,512]{1,0:T(8,128)(2,1)S(1)} fusion(bf16[1024,4096]{1,0:T(8,128)(2,1)S(1)} %bitcast.39, bf16[4096,256]{1,0:T(8,128)(2,1)} %get-tuple-element.15, bf16[4096,256]{1,0:T(8,128)(2,1)} %get-tuple-element.14), kind=kOutput, calls=%fused_computation.22 | convolution fusion | flops 4303880192 | bytes 13631488 | tf_op jit(solution)/shard_map/dot_general | solution.py:48
  50.7 0.3 reshape.44
  51.0 0.2 copy.29
  51.2 3.3 %reshape.45 = bf16[8,32,64,2,16]{1,0,4,3,2:T(8,128)(2,1)} reshape(bf16[256,4,16,2,16]{0,4,3,2,1:T(8,128)(2,1)S(1)} %bitcast.40) | data formatting | bytes 2097152 | tf_op jit(solution)/shard_map/reshape | solution.py:51
  54.5 7.0 %copy.14 = bf16[8,32,64,2,16]{2,4,3,1,0:T(8,128)(2,1)S(1)} copy(bf16[8,32,64,2,16]{1,0,4,3,2:T(8,128)(2,1)} %reshape.45) | data formatting | bytes 2097152 | tf_op jit(solution)/shard_map/reshape | solution.py:51
  61.5 1.7 reshape.48
  63.1 15.3 %all_to_all.5 = bf16[8,2,32768]{2,1,0:T(2,128)(2,1)} all-to-all(bf16[8,2,32768]{2,1,0:T(2,128)(2,1)S(1)} %reshape.48), channel_id=1, replica_groups=mesh['az'=16,'tm'=8] {'tm'}, dimensions={0} | all-to-all | bytes 2097152 | tf_op jit(solution)/shard_map/all_to_all | solution.py:52
  78.5 3.1 %reshape.49 = bf16[8,32,2,16,64]{4,3,2,1,0:T(8,128)(2,1)S(1)} reshape(bf16[8,2,32768]{2,1,0:T(2,128)(2,1)} %all_to_all.5) | data formatting | bytes 2097152
  81.6 0.4 bitcast_bitcast_fusion
  82.0 0.6 copy.15
  82.6 1.6 copy.21
  84.2 0.0 all-gather.2.cloned.1.call-update
  84.2 0.8 copy.19
  85.1 1.5 fusion.25
  86.5 1.6 copy.23
  88.1 1.6 copy.24
  89.7 0.1 negate_bitcast_fusion
  89.8 0.1 maximum_bitcast_fusion
  90.0 109.3 %all-gather.2.cloned.1.call-done = bf16[32,1024,256]{2,1,0:T(8,128)(2,1)} async-done(((bf16[32,64,256]{2,1,0:T(8,128)(2,1)}), bf16[32,1024,256]{2,1,0:T(8,128)(2,1)}) %all-gather.2.cloned.1.call-update) | async-done | bytes 16777232 | tf_op jit(solution)/shard_map/all_gather | solution.py:59
  199.3 12.5 %broadcast_multiply_fusion = f32[32,2,64,1024]{3,2,1,0:T(8,128)} fusion(bf16[32,1024,256]{2,1,0:T(8,128)(2,1)} %all-gather.2.cloned.1.call-done, bf16[32,1,64,256]{3,2,1,0:T(8,128)(2,1)S(1)} %maximum_bitcast_fusion, bf16[32,1,64,256]{3,2,1,0:T(8,128)(2,1)S(1)} %copy.19), kind=kOutput, calls=%fused_computation.3 | convolution fusion | flops 2152726528 | bytes 35651584 | tf_op jit(solution)/shard_map/fcqk,fpk->fcqp/dot_general | solution.py:60
  (2 shorter events, 0.0 us)
Async XLA Ops:
  6.5 5.9 %copy-start.1 = (f32[16,16]{1,0:T(8,128)S(1)}, f32[16,16]{1,0:T(8,128)}, u32[]{:S(2)}) copy-start(f32[16,16]{1,0:T(8,128)} %param.5) | copy-start | bytes 3076
  6.5 5.9 %copy-start.2 = (s32[16,16]{1,0:T(8,128)S(1)}, s32[16,16]{1,0:T(8,128)}, u32[]{:S(2)}) copy-start(s32[16,16]{1,0:T(8,128)} %param.4) | copy-start | bytes 3076
  6.5 192.7 %all-gather.2.cloned.1.call-start = ((), (), s32[]{:S(2)}) async-start(), calls=%async_computation.1 | async-start | bytes 17825792 | tf_op jit(solution)/shard_map/all_gather | solution.py:59
  6.5 27.9 %copy-start = (bf16[16,4,16,4096]{3,2,1,0:T(8,128)(2,1)S(1)}, bf16[16,4,16,4096]{3,2,1,0:T(8,128)(2,1)}, u32[]{:S(2)}) copy-start(bf16[16,4,16,4096]{3,2,1,0:T(8,128)(2,1)} %param.3) | copy-start | bytes 25165828
  9.2 27.1 %collective-permute-start.1 = (bf16[16,1,16,4096]{3,2,1,0:T(8,128)(2,1)S(1)}, bf16[16,1,16,4096]{3,2,1,0:T(8,128)(2,1)S(1)}, u32[]{:S(2)}, u32[]{:S(2)}) collective-permute-start(bf16[16,1,16,4096]{3,2,1,0:T(8,128)(2,1)S(1)} %get-tuple-element.7), channel_id=1, source_target_pairs={{8,0},{16,8},{24,16},{32,24},{40,32},{48,40},{56,48},{64,56},{72,6... | collective-permute-start | bytes 6291464 | tf_op jit(solution)/shard_map/ppermute | solution.py:40
  10.6 25.7 %collective-permute-start = (bf16[16,1,16,4096]{3,2,1,0:T(8,128)(2,1)S(1)}, bf16[16,1,16,4096]{3,2,1,0:T(8,128)(2,1)S(1)}, u32[]{:S(2)}, u32[]{:S(2)}) collective-permute-start(bf16[16,1,16,4096]{3,2,1,0:T(8,128)(2,1)S(1)} %get-tuple-element.8), channel_id=1, source_target_pairs={{0,8},{8,16},{16,24},{24,32},{32,40},{40,48},{48,56},{56,64},{64,7... | collective-permute-start | bytes 6291464 | tf_op jit(solution)/shard_map/ppermute | solution.py:39
Sparse Core Ops, SparseCore 0:
  84.3 114.8 all-gather.1

commit v2 on v1

v2 whole, which is shorter than its diff:
```python
import math

import jax
import jax.numpy as jnp
from jax import lax
from jax.sharding import Mesh
from jax.sharding import PartitionSpec as P

FREQS = 256
CHUNKS = 4
AZ = ("xh", "z", "core")
TM = ("xl", "y")
CHIPS = ("xh", "z")


def dft_table(length, freqs):
    step = 64
    bins = jnp.arange(1, freqs + 1, dtype=jnp.int32)
    high = jnp.arange(length // step, dtype=jnp.int32)
    low = jnp.arange(step, dtype=jnp.int32)
    scale = 2.0 * math.pi / length
    a = (high[:, None] * step * bins[None, :] % length).astype(jnp.float32) * scale
    b = (low[:, None] * bins[None, :] % length).astype(jnp.float32) * scale
    ca, sa = jnp.cos(a)[:, None], jnp.sin(a)[:, None]
    cb, sb = jnp.cos(b)[None], jnp.sin(b)[None]
    ca, sa, cb, sb = lax.optimization_barrier((ca, sa, cb, sb))
    cos = (ca * cb - sa * sb).reshape(length, freqs)
    sin = (sa * cb + ca * sb).reshape(length, freqs)
    times = jnp.arange(length, dtype=jnp.int32)
    hann = 0.5 - 0.5 * jnp.cos(times.astype(jnp.float32) * scale)
    factor = hann[:, None] / math.sqrt(3.0 * length / 8.0)
    return jnp.concatenate([factor * cos, -factor * sin], axis=1).astype(jnp.bfloat16)


def interp_weights(offsets, frac):
    rows = []
    for shift in range(-1, 2):
        low = (offsets == shift).astype(frac.dtype)
        high = (offsets + 1 == shift).astype(frac.dtype)
        rows.append((1.0 - frac) * low + frac * high)
    return jnp.stack(rows, 0)


def shards(pressure, offsets, frac):
    cycles, sector, blocks, length = pressure.shape
    subs = offsets.shape[1]
    sub_len = length // subs
    n_az = lax.axis_size(AZ)
    n_tm = lax.axis_size(TM)
    forward = [(i, (i + 1) % n_az) for i in range(n_az)]
    backward = [((i + 1) % n_az, i) for i in range(n_az)]
    left = lax.ppermute(pressure[:, sector - 1 :], AZ, forward)
    right = lax.ppermute(pressure[:, :1], AZ, backward)
    weights = jnp.repeat(interp_weights(offsets, frac), sub_len, axis=2)[:, None, None]
    prev = jnp.concatenate([left, pressure[:, :-1]], axis=1).astype(jnp.float32)
    nxt = jnp.concatenate([pressure[:, 1:], right], axis=1).astype(jnp.float32)
    total = weights[0] * prev + weights[1] * pressure.astype(jnp.float32) + weights[2] * nxt
    virtual = total.astype(jnp.bfloat16).reshape(cycles * sector * blocks, length)
    table = dft_table(length, FREQS)
    fl = FREQS // n_tm
    spectra = lax.dot_general(
        table, virtual, (((0,), (1,)), ((), ())), preferred_element_type=jnp.float32
    ).astype(jnp.bfloat16)
    spectra = spectra.reshape(2, n_tm, fl, cycles, sector, blocks).transpose(1, 2, 0, 3, 4, 5)
    shared = lax.all_to_all(spectra, TM, 0, 0, tiled=True)
    local_rows = sector * cycles
    width = n_tm * blocks
    x = shared.transpose(1, 4, 3, 2, 0, 5).reshape(fl, local_rows, 2, width)
    rows = x.reshape(fl, local_rows, 2 * width)
    turned = jnp.concatenate([x[:, :, 1], -x[:, :, 0]], axis=2)
    lhs = jnp.stack([rows, turned], 1).reshape(fl, 2, local_rows, 2, width)
    core = lax.axis_index("core")
    chip = lax.all_gather(x, "core", axis=1, tiled=True)
    mine = lax.dynamic_index_in_dim(chip, core, axis=2, keepdims=False)
    l_own = lax.dynamic_index_in_dim(lhs, core, axis=3, keepdims=False)
    l_other = lax.dynamic_index_in_dim(lhs, 1 - core, axis=3, keepdims=False)
    fc = fl // CHUNKS
    outs = []
    for j in range(CHUNKS):
        part = mine[j * fc : (j + 1) * fc]
        own_cols = lax.all_gather(part, CHIPS, axis=1, tiled=True)
        other_cols = lax.ppermute(own_cols, "core", [(0, 1), (1, 0)])
        res = jnp.einsum(
            "fcqk,fpk->fcqp", l_own[j * fc : (j + 1) * fc], own_cols,
            preferred_element_type=jnp.float32,
        ) + jnp.einsum(
            "fcqk,fpk->fcqp", l_other[j * fc : (j + 1) * fc], other_cols,
            preferred_element_type=jnp.float32,
        )
        outs.append(res * (1.0 / width))
    return jnp.concatenate(outs, 0)


def solution(mesh):
    az, tm = mesh.devices.shape
    fine = Mesh(mesh.devices.reshape(2, az // 4, 2, 2, tm // 2), ("xh", "z", "core", "xl", "y"))
    return jax.shard_map(
        shards,
        mesh=fine,
        in_specs=(P(None, AZ, TM, None), P(TM, None), P(TM, None)),
        out_specs=P(TM, None, AZ, None),
        check_vma=False,
    )
```

time: 219 us -> 373 us (1.70)
  waiting for transfers between devices: 110 us -> 227 us
  local copies, waits for them, and re-layouts: 30.7 us -> 61.4 us
  starting transfers between devices: 3.17 us -> 8.93 us
    all_gather x1 -> x5, waiting for transfers between devices: 109 us -> 211 us  [the longest x4 191 us: shards(): own_cols = lax.all_gather(part, CHIPS, axis=1, tiled=True)]
    transpose x2 -> x3, local copies, waits for them, and re-layouts: 1.01 us -> 18.2 us  [the longest x2 9.29 us: shards(): x = shared.transpose(1, 4, 3, 2, 0, 5).reshape(fl, local_rows, 2, width)]
    another operation x2, other arithmetic: 19.2 us -> 4.52 us
    ppermute x2 -> x6, waiting for transfers between devices: 0.34 us -> 14.4 us  [the longest x1 14.4 us: shards(): right = lax.ppermute(pressure[:, :1], AZ, backward)]
    concatenate x0 -> x2, other arithmetic: none -> 7.83 us  [the longest x1 6.45 us: shards(): return jnp.concatenate(outs, 0)]
    unnamed x13 -> x21, local copies, waits for them, and re-layouts: 10.5 us -> 16.3 us
    ppermute x2 -> x6, starting transfers between devices: 3.17 us -> 8.76 us  [the longest x4 5.6 us: shards(): other_cols = lax.ppermute(own_cols, 'core', [(0, 1), (1, 0)])]
    another operation x2 -> x3, local copies, waits for them, and re-layouts: 2.45 us -> 6.62 us  [shards(): lhs = jnp.stack([rows, turned], 1).reshape(fl, 2, local_rows, 2, width)]
  transfers between devices with their start and end apart: 3 -> 11, of which waited for: 2 -> 6; matrix products, arithmetic and copies ran while one was open for 13% -> 10% of each run, Pallas kernels for 0% -> 0%
where the time goes in v2:
time: 373 us; the launch traced here: 372 us
  waiting for transfers between devices  227 us (61%)
  local copies, waits for them, and re-layouts  61.4 us (16%)
  other arithmetic  25.7 us (7%)
  matrix products  20.6 us (6%)
  blocking collectives  15.2 us (4%)
  between operations  13.4 us (4%)
  starting transfers between devices  8.93 us (2%)
    all_gather x4, waiting for transfers between devices, shards(): own_cols = lax.all_gather(part, CHIPS, axis=1, tiled=True)  191 us
    all_gather x1, waiting for transfers between devices, shards(): chip = lax.all_gather(x, 'core', axis=1, tiled=True)  19.4 us
    unnamed x21, local copies, waits for them, and re-layouts  16.3 us
    all_to_all x1, blocking collectives, shards(): shared = lax.all_to_all(spectra, TM, 0, 0, tiled=True)  15.2 us
    ppermute x1, waiting for transfers between devices, shards(): right = lax.ppermute(pressure[:, :1], AZ, backward)  14.4 us
    dot_general x4, matrix products, shards(): jnp.einsum('fcqk,fpk->fcqp', l_other[j * fc:(j + 1) * fc], other_cols, pr...  9.37 us
    transpose x2, local copies, waits for them, and re-layouts, shards(): x = shared.transpose(1, 4, 3, 2, 0, 5).reshape(fl, local_rows, 2, width)  9.29 us
    transpose x1, local copies, waits for them, and re-layouts, shards(): spectra.reshape(2, n_tm, fl, cycles, sector, blocks)  8.93 us
  transfers between devices with their start and end apart: 11, of which 6 were waited for; matrix products, arithmetic and copies ran while one was open for 10% of the time, Pallas kernels for 0%

profile of v2, /device:TPU:1, one launch (start us, length us, event | category | flops | bytes accessed | tf_op | source)
XLA Modules:
  0.0 372.0 jit_solution(11300357520508606070)
XLA Ops:
  6.5 2.5 fusion.40
  9.1 1.5 collective-permute-start.1
  10.5 1.7 collective-permute-start
  12.2 0.1 fusion.37
  12.3 0.1 subtract_multiply_fusion
  12.4 0.3 fusion.33
  12.7 0.3 fusion.35
  13.1 0.1 broadcast_in_dim.22
  13.2 0.9 copy.38
  14.0 0.1 broadcast_in_dim.26
  14.1 0.9 copy.40
  15.0 0.1 broadcast_in_dim.24
  15.1 0.9 copy.39
  16.0 0.9 multiply_subtract_fusion
  16.8 3.4 fusion.4
  20.2 1.5 fusion.39
  21.8 14.4 %collective-permute-done.1 = bf16[16,1,16,4096]{3,2,1,0:T(8,128)(2,1)S(1)} collective-permute-done((bf16[16,1,16,4096]{3,2,1,0:T(8,128)(2,1)S(1)}, bf16[16,1,16,4096]{3,2,1,0:T(8,128)(2,1)S(1)}, u32[]{:S(2)}, u32[]{:S(2)}) %collective-permute-start.1) | collective-permute-done | bytes 2097184 | tf_op jit(solution)/shard_map/ppermute | solution.py:53
  36.2 7.7 %add_convert_fusion = bf16[16,4,16,4096]{3,2,1,0:T(8,128)(2,1)S(1)} fusion(bf16[16,4,16,4096]{3,2,1,0:T(8,128)(2,1)S(1)} %bitcast.105, bf16[16,3,16,4096]{3,2,1,0:T(8,128)(2,1)S(1)} %get-tuple-element.14, bf16[16,1,16,4096]{3,2,1,0:T(8,128)(2,1)S(1)} %collective-permute-done, bf16[16,1,16,4096]{3,2,1,0:T(8,128)(2,1)S(1)} %collective-permute-done.1, ...), kind=kLoop, calls=%fused_computation.1 | loop fusion | flops 46137344 | bytes 34340864 | tf_op jit(solution)/shard_map/convert_element_type | solution.py:58
  43.9 6.8 %fusion.19 = bf16[512,1024]{1,0:T(8,128)(2,1)S(1)} fusion(bf16[1024,4096]{1,0:T(8,128)(2,1)S(1)} %bitcast.111, bf16[4096,256]{1,0:T(8,128)(2,1)} %get-tuple-element.34, bf16[4096,256]{1,0:T(8,128)(2,1)} %get-tuple-element.35), kind=kOutput, calls=%fused_computation.35 | convolution fusion | flops 4303880192 | bytes 13631488 | tf_op jit(solution)/shard_map/dot_general | solution.py:61
  50.7 0.5 copy.21
  51.2 3.7 %reshape.298 = bf16[2,8,32,16,4,16]{2,1,0,5,4,3:T(8,128)(2,1)} reshape(bf16[512,1024]{0,1:T(8,128)(2,1)S(1)} %copy.21) | data formatting | bytes 2097152 | tf_op jit(solution)/shard_map/reshape | solution.py:64
  55.0 8.9 %copy.42 = bf16[8,32,2,16,4,16]{1,2,5,4,3,0:T(2,128)(2,1)} copy(bf16[8,32,2,16,4,16]{1,0,2,5,4,3:T(8,128)(2,1)} %bitcast.109) | data formatting | bytes 2097152 | tf_op jit(solution)/shard_map/transpose | solution.py:64
  63.9 7.0 %reshape.312 = bf16[8,2,32768]{2,1,0:T(2,128)(2,1)S(1)} reshape(bf16[8,16,4,16,2,32]{5,4,3,2,1,0:T(2,128)(2,1)} %bitcast.110) | data formatting | bytes 2097152
  70.9 15.2 %all_to_all.5 = bf16[8,2,32768]{2,1,0:T(2,128)(2,1)S(1)} all-to-all(bf16[8,2,32768]{2,1,0:T(2,128)(2,1)S(1)} %reshape.312), channel_id=1, replica_groups=mesh['xh'=2,'z'=4,'core'=2,'xl'=2,'y'=4] {'xl','y'}, dimensions={0} | all-to-all | bytes 2097152 | tf_op jit(solution)/shard_map/all_to_all | solution.py:65
  86.1 4.5 %reshape.313 = bf16[8,16,4,16,2,32]{5,4,3,2,1,0:T(2,128)(2,1)} reshape(bf16[8,2,32768]{2,1,0:T(2,128)(2,1)S(1)} %all_to_all.5) | data formatting | bytes 2097152
  90.5 6.1 %bitcast_bitcast_fusion = bf16[32,4,16,2,8,16]{0,3,5,1,2,4:T(2,128)(2,1)S(1)} fusion(bf16[8,16,4,16,2,32]{5,4,3,2,1,0:T(2,128)(2,1)} %reshape.313), kind=kLoop, calls=%fused_computation.82 | loop fusion | bytes 2097152 | tf_op jit(solution)/shard_map/transpose | solution.py:68
  96.7 3.2 copy.23
  99.8 4.9 %copy.29 = bf16[32,64,2,128]{3,1,0,2:T(8,128)(2,1)} copy(bf16[32,64,2,128]{0,3,2,1:T(8,128)(2,1)} %bitcast.106) | data formatting | bytes 2097152 | tf_op jit(solution)/shard_map/reshape | solution.py:68
  104.7 0.0 all-gather.18.cloned.1.call-start
  104.8 19.4 %all-gather.10.cloned.1.call-done = bf16[32,128,2,128]{3,1,0,2:T(8,128)(2,1)} async-done(((bf16[32,64,2,128]{3,1,0,2:T(8,128)(2,1)}), bf16[32,128,2,128]{3,1,0,2:T(8,128)(2,1)}) %all-gather.10.cloned.1.call-update) | async-done | bytes 2097168 | tf_op jit(solution)/shard_map/all_gather | solution.py:73
  124.2 2.2 constant_dynamic-slice_fusion.1
  126.4 0.0 all-gather.16.cloned.1.call-start
  126.5 0.7 all-gather.16.cloned.1.call-update
  127.2 0.5 all-gather.14.cloned.1.call-update
  127.7 0.0 all-gather.12.cloned.1.call-start
  127.8 0.5 all-gather.12.cloned.1.call-update
  128.3 4.0 %copy.27 = bf16[32,1,64,2,128]{4,2,1,0,3:T(8,128)(2,1)S(1)} copy(bf16[32,1,64,2,128]{0,4,3,2,1:T(8,128)(2,1)} %bitcast.107) | data formatting | bytes 2097152 | tf_op jit(solution)/shard_map/stack | solution.py:71
  132.4 48.1 %all-gather.18.cloned.1.call-done = bf16[8,1024,1,128]{3,1,0,2:T(8,128)(2,1)} async-done(((bf16[8,128,1,128]{3,1,0,2:T(8,128)(2,1)}), bf16[8,1024,1,128]{3,1,0,2:T(8,128)(2,1)}) %all-gather.18.cloned.1.call-update) | async-done | bytes 2097168 | tf_op jit(solution)/shard_map/all_gather | solution.py:81
  180.5 1.4 collective-permute-start.5
  181.9 4.0 %slice_bitcast_fusion = (bf16[32,64,128]{0,2,1:T(8,128)(2,1)}, bf16[32,64,128]{0,2,1:T(8,128)(2,1)S(1)}) fusion(bf16[32,64,2,128]{0,3,2,1:T(8,128)(2,1)} %bitcast.108), kind=kLoop, calls=%fused_computation.22 | loop fusion | flops 262144 | bytes 2097152 | tf_op jit(solution)/shard_map/squeeze | solution.py:70
  185.9 2.9 copy.25
  188.8 1.8 copy.26
  190.5 1.4 pad_maximum_fusion.1
  191.9 1.1 stack.13
  193.0 1.5 copy.28
  194.5 39.7 %all-gather.16.cloned.1.call-done = bf16[8,1024,1,128]{3,1,0,2:T(8,128)(2,1)} async-done(((bf16[8,128,1,128]{3,1,0,2:T(8,128)(2,1)}), bf16[8,1024,1,128]{3,1,0,2:T(8,128)(2,1)}) %all-gather.16.cloned.1.call-update) | async-done | bytes 2097168 | tf_op jit(solution)/shard_map/all_gather | solution.py:81
  234.2 1.4 collective-permute-start.4
  235.6 1.2 fusion.22
  236.8 51.1 %all-gather.14.cloned.1.call-done = bf16[8,1024,1,128]{3,1,0,2:T(8,128)(2,1)} async-done(((bf16[8,128,1,128]{3,1,0,2:T(8,128)(2,1)}), bf16[8,1024,1,128]{3,1,0,2:T(8,128)(2,1)}) %all-gather.14.cloned.1.call-update) | async-done | bytes 2097168 | tf_op jit(solution)/shard_map/all_gather | solution.py:81
  287.9 1.4 collective-permute-start.3
  289.3 52.2 %all-gather.12.cloned.1.call-done = bf16[8,1024,1,128]{3,1,0,2:T(8,128)(2,1)} async-done(((bf16[8,128,1,128]{3,1,0,2:T(8,128)(2,1)}), bf16[8,1024,1,128]{3,1,0,2:T(8,128)(2,1)}) %all-gather.12.cloned.1.call-update) | async-done | bytes 2097168 | tf_op jit(solution)/shard_map/all_gather | solution.py:81
  341.5 1.4 collective-permute-start.2
  342.9 2.3 fusion.8
  345.2 0.7 fusion.11
  345.9 0.9 copy-done.2
  346.8 0.7 fusion.14
  347.5 0.9 copy-done.3
  348.4 0.7 fusion.17
  349.1 0.5 copy-done
  349.6 2.3 add_multiply_fusion
  352.0 2.3 add_multiply_fusion.1
  354.3 2.3 add_multiply_fusion.2
  356.7 2.3 add_multiply_fusion.3
  359.1 6.4 %pad_maximum_fusion = f32[32,2,64,1024]{3,2,1,0:T(8,128)} fusion(f32[8,2,64,1024]{3,2,1,0:T(8,128)S(1)} %add_multiply_fusion, f32[8,2,64,1024]{3,2,1,0:T(8,128)S(1)} %add_multiply_fusion.1, f32[8,2,64,1024]{3,2,1,0:T(8,128)S(1)} %add_multiply_fusion.2, f32[8,2,64,1024]{3,2,1,0:T(8,128)S(1)} %add_multiply_fusion.3), kind=kLoop, calls=%fused_computation | loop fusion | flops 12582912 | bytes 33554432 | tf_op jit(solution)/shard_map/concatenate | solution.py:91
  (26 shorter events, 0.1 us)
Async XLA Ops:
  6.5 6.5 %copy-start.4 = (f32[16,16]{1,0:T(8,128)S(1)}, f32[16,16]{1,0:T(8,128)}, u32[]{:S(2)}) copy-start(f32[16,16]{1,0:T(8,128)} %param.5) | copy-start | bytes 3076
  6.5 6.5 %copy-start.5 = (s32[16,16]{1,0:T(8,128)S(1)}, s32[16,16]{1,0:T(8,128)}, u32[]{:S(2)}) copy-start(s32[16,16]{1,0:T(8,128)} %param.4) | copy-start | bytes 3076
  6.5 117.7 %all-gather.10.cloned.1.call-start = ((), (), s32[]{:S(2)}) async-start(), calls=%async_computation.1 | async-start | bytes 3145728 | tf_op jit(solution)/shard_map/all_gather | solution.py:73
  9.1 27.1 %collective-permute-start.1 = (bf16[16,1,16,4096]{3,2,1,0:T(8,128)(2,1)S(1)}, bf16[16,1,16,4096]{3,2,1,0:T(8,128)(2,1)S(1)}, u32[]{:S(2)}, u32[]{:S(2)}) collective-permute-start(bf16[16,1,16,4096]{3,2,1,0:T(8,128)(2,1)S(1)} %get-tuple-element.15), channel_id=1, source_target_pairs={{8,0},{16,8},{24,16},{32,24},{40,32},{48,40},{56,48},{64,56},{72,6... | collective-permute-start | bytes 6291464 | tf_op jit(solution)/shard_map/ppermute | solution.py:53
  10.5 25.7 %collective-permute-start = (bf16[16,1,16,4096]{3,2,1,0:T(8,128)(2,1)S(1)}, bf16[16,1,16,4096]{3,2,1,0:T(8,128)(2,1)S(1)}, u32[]{:S(2)}, u32[]{:S(2)}) collective-permute-start(bf16[16,1,16,4096]{3,2,1,0:T(8,128)(2,1)S(1)} %get-tuple-element.16), channel_id=1, source_target_pairs={{0,8},{8,16},{16,24},{24,32},{32,40},{40,48},{48,56},{56,64},{64,7... | collective-permute-start | bytes 6291464 | tf_op jit(solution)/shard_map/ppermute | solution.py:52
  16.0 4.3 %slice-start = ((s8[8388608]{0:T(1024)(128)(4,1)}), s8[4194304]{0:T(1024)(128)(4,1)S(1)}, s32[]{:S(2)}) async-start(s8[8388608]{0:T(1024)(128)(4,1)} %bitcast.104), calls=%async_computation.6 | async-start | bytes 8388608
  16.8 3.4 slice-start.1
  104.7 75.7 %all-gather.18.cloned.1.call-start = ((), (), s32[]{:S(2)}) async-start(), calls=%async_computation.5 | async-start | bytes 2359296 | tf_op jit(solution)/shard_map/all_gather | solution.py:81
  126.4 107.8 %all-gather.16.cloned.1.call-start = ((), (), s32[]{:S(2)}) async-start(), calls=%async_computation.4 | async-start | bytes 2359296 | tf_op jit(solution)/shard_map/all_gather | solution.py:81
  127.2 160.7 %all-gather.14.cloned.1.call-start = ((), (), s32[]{:S(2)}) async-start(), calls=%async_computation.3 | async-start | bytes 2359296 | tf_op jit(solution)/shard_map/all_gather | solution.py:81
  127.7 213.8 %all-gather.12.cloned.1.call-start = ((), (), s32[]{:S(2)}) async-start(), calls=%async_computation.2 | async-start | bytes 2359296 | tf_op jit(solution)/shard_map/all_gather | solution.py:81
  180.5 168.7 %collective-permute-start.5 = (bf16[8,1024,128]{2,1,0:T(8,128)(2,1)}, bf16[8,1024,128]{2,1,0:T(8,128)(2,1)}, u32[]{:S(2)}, u32[]{:S(2)}) collective-permute-start(bf16[8,1024,128]{2,1,0:T(8,128)(2,1)} %bitcast.112), channel_id=1, source_target_pairs={{0,8},{8,0},{1,9},{9,1},{2,10},{10,2},{3,11},{11,3},{4,12},{12,4},... | collective-permute-start | bytes 6291464 | tf_op jit(solution)/shard_map/ppermute | solution.py:82
  234.2 117.7 %collective-permute-start.4 = (bf16[8,1024,128]{2,1,0:T(8,128)(2,1)}, bf16[8,1024,128]{2,1,0:T(8,128)(2,1)}, u32[]{:S(2)}, u32[]{:S(2)}) collective-permute-start(bf16[8,1024,128]{2,1,0:T(8,128)(2,1)} %bitcast.113), channel_id=1, source_target_pairs={{0,8},{8,0},{1,9},{9,1},{2,10},{10,2},{3,11},{11,3},{4,12},{12,4},... | collective-permute-start | bytes 6291464 | tf_op jit(solution)/shard_map/ppermute | solution.py:82
  236.8 108.4 %copy-start.1 = (bf16[8,1024,1,128]{3,1,0,2:T(8,128)(2,1)S(1)}, bf16[8,1024,1,128]{3,1,0,2:T(8,128)(2,1)}, u32[]{:S(2)}) copy-start(bf16[8,1024,1,128]{3,1,0,2:T(8,128)(2,1)} %all-gather.16.cloned.1.call-done) | copy-start | bytes 6291460
  287.9 66.5 %collective-permute-start.3 = (bf16[8,1024,128]{2,1,0:T(8,128)(2,1)}, bf16[8,1024,128]{2,1,0:T(8,128)(2,1)}, u32[]{:S(2)}, u32[]{:S(2)}) collective-permute-start(bf16[8,1024,128]{2,1,0:T(8,128)(2,1)} %bitcast.114), channel_id=1, source_target_pairs={{0,8},{8,0},{1,9},{9,1},{2,10},{10,2},{3,11},{11,3},{4,12},{12,4},... | collective-permute-start | bytes 6291464 | tf_op jit(solution)/shard_map/ppermute | solution.py:82
  341.5 15.2 %collective-permute-start.2 = (bf16[8,1024,128]{2,1,0:T(8,128)(2,1)}, bf16[8,1024,128]{2,1,0:T(8,128)(2,1)}, u32[]{:S(2)}, u32[]{:S(2)}) collective-permute-start(bf16[8,1024,128]{2,1,0:T(8,128)(2,1)} %bitcast.115), channel_id=1, source_target_pairs={{0,8},{8,0},{1,9},{9,1},{2,10},{10,2},{3,11},{11,3},{4,12},{12,4},... | collective-permute-start | bytes 6291464 | tf_op jit(solution)/shard_map/ppermute | solution.py:82
  345.2 1.6 copy-start.2
  346.8 1.6 copy-start.3
  348.4 1.2 copy-start
Sparse Core Ops, SparseCore 0:
  104.8 19.3 all-gather.9
  126.6 53.8 all-gather.17
  182.8 51.4 all-gather.15
  236.4 51.4 all-gather.13
  290.0 51.4 all-gather.11

commit v3 on v1

v3 whole, which is shorter than its diff:
```python
import math

import jax
import jax.numpy as jnp
from jax import lax
from jax.sharding import PartitionSpec as P

FREQS = 256


def dft_table(length, freqs):
    step = 64
    bins = jnp.arange(1, freqs + 1, dtype=jnp.int32)
    high = jnp.arange(length // step, dtype=jnp.int32)
    low = jnp.arange(step, dtype=jnp.int32)
    scale = 2.0 * math.pi / length
    a = (high[:, None] * step * bins[None, :] % length).astype(jnp.float32) * scale
    b = (low[:, None] * bins[None, :] % length).astype(jnp.float32) * scale
    ca, sa = jnp.cos(a)[:, None], jnp.sin(a)[:, None]
    cb, sb = jnp.cos(b)[None], jnp.sin(b)[None]
    ca, sa, cb, sb = lax.optimization_barrier((ca, sa, cb, sb))
    cos = (ca * cb - sa * sb).reshape(length, freqs)
    sin = (sa * cb + ca * sb).reshape(length, freqs)
    times = jnp.arange(length, dtype=jnp.int32)
    hann = 0.5 - 0.5 * jnp.cos(times.astype(jnp.float32) * scale)
    factor = hann[:, None] / math.sqrt(3.0 * length / 8.0)
    return jnp.concatenate([factor * cos, -factor * sin], axis=1).astype(jnp.bfloat16)


def interp_weights(offsets, frac):
    rows = []
    for shift in range(-1, 2):
        low = (offsets == shift).astype(frac.dtype)
        high = (offsets + 1 == shift).astype(frac.dtype)
        rows.append((1.0 - frac) * low + frac * high)
    return jnp.stack(rows, 0)


def shards(pressure, offsets, frac):
    cycles, sector, blocks, length = pressure.shape
    subs = offsets.shape[1]
    sub_len = length // subs
    n_az = lax.axis_size("az")
    n_tm = lax.axis_size("tm")
    forward = [(i, (i + 1) % n_az) for i in range(n_az)]
    backward = [((i + 1) % n_az, i) for i in range(n_az)]
    left = lax.ppermute(pressure[:, sector - 1 :], "az", forward)
    right = lax.ppermute(pressure[:, :1], "az", backward)
    weights = jnp.repeat(interp_weights(offsets, frac), sub_len, axis=2)[:, None, None]
    prev = jnp.concatenate([left, pressure[:, :-1]], axis=1).astype(jnp.float32)
    nxt = jnp.concatenate([pressure[:, 1:], right], axis=1).astype(jnp.float32)
    total = weights[0] * prev + weights[1] * pressure.astype(jnp.float32) + weights[2] * nxt
    virtual = total.astype(jnp.bfloat16).transpose(2, 1, 0, 3).reshape(blocks * sector * cycles, length)
    table = dft_table(length, FREQS)
    fl = FREQS // n_tm
    local_rows = sector * cycles
    width = n_tm * blocks
    spectra = lax.dot_general(
        table, virtual, (((0,), (1,)), ((), ())), preferred_element_type=jnp.float32
    ).astype(jnp.bfloat16)
    spectra = spectra.reshape(2, n_tm, fl, blocks * local_rows).transpose(1, 0, 2, 3)
    shared = lax.all_to_all(spectra, "tm", 0, 0, tiled=True)
    shared = shared.reshape(n_tm, 2, fl, blocks, local_rows)
    x = shared.transpose(2, 4, 0, 1, 3)
    rows = x.reshape(fl, local_rows, 2 * width)
    turned = jnp.stack([x[:, :, :, 1], -x[:, :, :, 0]], 3).reshape(fl, local_rows, 2 * width)
    lhs = jnp.stack([rows, turned], 1)
    columns = lax.all_gather(rows, "az", axis=1, tiled=True)
    result = jnp.einsum("fcqk,fpk->fcqp", lhs, columns, preferred_element_type=jnp.float32)
    return result * (1.0 / width)


def solution(mesh):
    return jax.shard_map(
        shards,
        mesh=mesh,
        in_specs=(P(None, "az", "tm", None), P("tm", None), P("tm", None)),
        out_specs=P("tm", None, "az", None),
        check_vma=False,
    )
```

time: 219 us -> 234 us (1.068)
  local copies, waits for them, and re-layouts: 30.7 us -> 39.1 us
  matrix products: 19.2 us -> 22.1 us
  other arithmetic: 27 us -> 29.4 us
    another operation x2, other arithmetic: 19.2 us -> 3.73 us
    convert_element_type x1, other arithmetic: 7.67 us -> 21.5 us  [shards(): total.astype(jnp.bfloat16).transpose(2, 1, 0, 3)]
    unnamed x13 -> x21, local copies, waits for them, and re-layouts: 10.5 us -> 22.5 us
    reshape x4, local copies, waits for them, and re-layouts: 10.7 us -> 6.16 us  [the longest x2 4.46 us: shards(): shared = shared.reshape(n_tm, 2, fl, blocks, local_rows)]
    slice x1, local copies, waits for them, and re-layouts: 1.52 us -> 4.91 us  [shards(): nxt = jnp.concatenate([pressure[:, 1:], right], axis=1).astype(jnp.float32)]
    dot_general x1, matrix products: 6.71 us -> 9.19 us  [shards(): lax.dot_general(table, virtual, (((0,), (1,)), ((), ())), preferred_eleme...]
  transfers between devices with their start and end apart: 3 -> 3, of which waited for: 2 -> 1; matrix products, arithmetic and copies ran while one was open for 13% -> 15% of each run, Pallas kernels for 0% -> 0%
where the time goes in v3:
time: 234 us
  waiting for transfers between devices  111 us (47%)
  local copies, waits for them, and re-layouts  39.1 us (17%)
  other arithmetic  29.4 us (13%)
  matrix products  22.1 us (9%)
  blocking collectives  16 us (7%)
  between operations  13.6 us (6%)
  starting transfers between devices  3.02 us (1%)
    all_gather x1, waiting for transfers between devices, shards(): columns = lax.all_gather(rows, 'az', axis=1, tiled=True)  111 us
    unnamed x21, local copies, waits for them, and re-layouts  22.5 us
    convert_element_type x1, other arithmetic, shards(): total.astype(jnp.bfloat16).transpose(2, 1, 0, 3)  21.5 us
    all_to_all x1, blocking collectives, shards(): shared = lax.all_to_all(spectra, 'tm', 0, 0, tiled=True)  16 us
    dot_general x1, matrix products, shards(): jnp.einsum('fcqk,fpk->fcqp', lhs, columns, preferred_element_type=jnp.flo...  12.9 us
    dot_general x1, matrix products, shards(): lax.dot_general(table, virtual, (((0,), (1,)), ((), ())), preferred_eleme...  9.19 us
    slice x1, local copies, waits for them, and re-layouts, shards(): nxt = jnp.concatenate([pressure[:, 1:], right], axis=1).astype(jnp.float32)  4.91 us
  transfers between devices with their start and end apart: 3, of which 1 were waited for; matrix products, arithmetic and copies ran while one was open for 15% of the time, Pallas kernels for 0%

profile of v3, /device:TPU:1, one launch (start us, length us, event | category | flops | bytes accessed | tf_op | source)
XLA Modules:
  0.0 233.8 jit_solution(15698628586463301875)
XLA Ops:
  6.5 0.0 all-gather.2.cloned.1.call-start
  6.5 0.0 slice-start
  6.5 2.9 %fusion.33 = (bf16[16,1,16,4096]{3,2,1,0:T(8,128)(2,1)S(1)}, bf16[16,1,16,4096]{3,2,1,0:T(8,128)(2,1)S(1)}) fusion(bf16[16,4,16,4096]{3,2,1,0:T(8,128)(2,1)} %param.3), kind=kLoop, calls=%fused_computation.53 | loop fusion | bytes 8388608 | tf_op jit(solution)/shard_map/slice | solution.py:48
  9.4 0.0 slice-start.1
  9.4 2.5 %copy.32 = bf16[16,1,16,4096]{3,0,1,2:T(8,128)(2,1)} copy(bf16[16,1,16,4096]{3,2,1,0:T(8,128)(2,1)S(1)} %get-tuple-element.16) | data formatting | bytes 4194304
  11.9 3.0 %collective-permute-start = (bf16[16,1,16,4096]{3,0,1,2:T(8,128)(2,1)}, bf16[16,1,16,4096]{3,0,1,2:T(8,128)(2,1)S(1)}, u32[]{:S(2)}, u32[]{:S(2)}) collective-permute-start(bf16[16,1,16,4096]{3,0,1,2:T(8,128)(2,1)} %copy.32), channel_id=1, source_target_pairs={{0,8},{8,16},{16,24},{24,32},{32,40},{40,48},{48,56},{56,64},{64,7... | collective-permute-start | bytes 6291464 | tf_op jit(solution)/shard_map/ppermute | solution.py:47
  15.0 2.5 %copy.33 = bf16[16,1,16,4096]{3,0,1,2:T(8,128)(2,1)} copy(bf16[16,1,16,4096]{3,2,1,0:T(8,128)(2,1)S(1)} %get-tuple-element.15) | data formatting | bytes 4194304
  17.5 0.0 collective-permute-start.1
  17.5 0.0 slice-done
  17.5 0.0 slice-done.1
  17.5 0.0 copy-start.1
  17.6 0.0 copy-start.2
  17.6 4.9 %fusion.32 = (bf16[16,3,16,4096]{3,2,1,0:T(8,128)(2,1)}, bf16[16,3,16,4096]{3,2,1,0:T(8,128)(2,1)}) fusion(bf16[16,4,16,4096]{3,2,1,0:T(8,128)(2,1)S(1)} %bitcast.44), kind=kLoop, calls=%fused_computation.52 | loop fusion | bytes 25165824 | tf_op jit(solution)/shard_map/slice | solution.py:51
  22.5 0.9 fusion.25
  23.4 1.0 fusion.27
  24.4 0.0 copy-done.1
  24.4 0.0 copy-done.2
  24.4 0.1 broadcast_in_dim.22
  24.5 0.2 copy.25
  24.7 0.1 broadcast_in_dim.26
  24.8 0.2 copy.27
  24.9 0.1 broadcast_in_dim.24
  25.0 0.9 copy.26
  25.9 6.2 %copy.34 = bf16[16,3,16,4096]{3,0,1,2:T(8,128)(2,1)S(1)} copy(bf16[16,3,16,4096]{3,2,1,0:T(8,128)(2,1)} %get-tuple-element.13) | data formatting | bytes 12582912
  32.1 8.9 %copy.31 = bf16[16,3,16,4096]{3,0,1,2:T(8,128)(2,1)} copy(bf16[16,3,16,4096]{3,2,1,0:T(8,128)(2,1)} %get-tuple-element.14) | data formatting | bytes 12582912
  41.1 0.1 fusion.29
  41.1 0.1 subtract_multiply_fusion
  41.2 1.8 multiply_subtract_fusion
  43.0 0.0 slice-start.2
  43.0 0.0 slice-start.3
  43.1 0.0 copy-start
  43.1 3.3 %fusion.8 = (bf16[4096,256]{1,0:T(8,128)(2,1)}, bf16[4096,256]{1,0:T(8,128)(2,1)}) fusion(f32[64,64,256]{2,1,0:T(8,128)S(1)} %get-tuple-element.22, f32[4096]{0:T(1024)S(1)} %fusion.29, f32[64,64,256]{2,1,0:T(8,128)S(1)} %get-tuple-element.21, f32[4096]{0:T(1024)S(1)} %subtract_multiply_fusion), kind=kLoop, calls=%fused_computation.9 | loop fusion | flops 4194304 | bytes 12615680 | tf_op jit(solution)/shard_map/convert.1
  46.4 0.0 collective-permute-done
  46.4 0.0 collective-permute-done.1
  46.4 0.0 slice-done.2
  46.4 1.0 slice-done.3
  47.4 0.0 copy-done
  47.4 21.5 %add_convert_fusion = bf16[16,4,16,4096]{3,0,1,2:T(8,128)(2,1)} fusion(bf16[16,3,16,4096]{3,0,1,2:T(8,128)(2,1)S(1)} %bitcast.49, bf16[16,1,16,4096]{3,0,1,2:T(8,128)(2,1)S(1)} %collective-permute-done, bf16[16,1,16,4096]{3,0,1,2:T(8,128)(2,1)S(1)} %collective-permute-done.1, bf16[16,3,16,4096]{3,0,1,2:T(8,128)(2,1)S(1)} %copy.34, ...), kind=kLoop, calls=%fused_computation.2 | loop fusion | flops 46137344 | bytes 34340864 | tf_op jit(solution)/shard_map/convert_element_type | solution.py:53
  69.0 9.2 %fusion.13 = bf16[512,1024]{1,0:T(8,128)(2,1)S(1)} fusion(bf16[1024,4096]{1,0:T(8,128)(2,1)} %bitcast.51, bf16[4096,256]{1,0:T(8,128)(2,1)} %get-tuple-element.30, bf16[4096,256]{1,0:T(8,128)(2,1)} %get-tuple-element.31), kind=kOutput, calls=%fused_computation.18 | convolution fusion | flops 4303880192 | bytes 13631488 | tf_op jit(solution)/shard_map/dot_general | solution.py:58
  78.2 0.1 copy.36
  78.3 16.0 %all_to_all.5 = bf16[8,2,32,1024]{3,2,1,0:T(8,128)(2,1)S(1)} all-to-all(bf16[8,2,32,1024]{3,2,1,0:T(8,128)(2,1)S(1)} %bitcast.52), channel_id=1, replica_groups=mesh['az'=16,'tm'=8] {'tm'}, dimensions={0} | all-to-all | bytes 2097152 | tf_op jit(solution)/shard_map/all_to_all | solution.py:62
  94.2 2.3 reshape.284
  96.5 2.2 copy.37
  98.7 1.6 copy.23
  100.3 0.0 all-gather.2.cloned.1.call-update
  100.3 0.8 copy.21
  101.2 0.2 fusion.34
  101.4 0.4 pad_maximum_fusion
  101.8 1.6 copy.22
  103.4 110.7 %all-gather.2.cloned.1.call-done = bf16[32,1024,256]{2,1,0:T(8,128)(2,1)} async-done(((bf16[32,64,256]{2,1,0:T(8,128)(2,1)}), bf16[32,1024,256]{2,1,0:T(8,128)(2,1)}) %all-gather.2.cloned.1.call-update) | async-done | bytes 16777232 | tf_op jit(solution)/shard_map/all_gather | solution.py:68
  214.1 12.9 %broadcast_multiply_fusion = f32[32,2,64,1024]{3,2,1,0:T(8,128)} fusion(bf16[32,1024,256]{2,1,0:T(8,128)(2,1)} %all-gather.2.cloned.1.call-done, bf16[32,1,64,256]{3,2,1,0:T(8,128)(2,1)} %copy.22, bf16[32,1,64,256]{3,2,1,0:T(8,128)(2,1)S(1)} %copy.21), kind=kOutput, calls=%fused_computation.3 | convolution fusion | flops 2152726528 | bytes 35651584 | tf_op jit(solution)/shard_map/fcqk,fpk->fcqp/dot_general | solution.py:69
  (5 shorter events, 0.0 us)
Async XLA Ops:
  6.5 207.6 %all-gather.2.cloned.1.call-start = ((), (), s32[]{:S(2)}) async-start(), calls=%async_computation.1 | async-start | bytes 17825792 | tf_op jit(solution)/shard_map/all_gather | solution.py:68
  6.5 11.0 %slice-start = ((s8[8388608]{0:T(1024)(128)(4,1)}), s8[4194304]{0:T(1024)(128)(4,1)S(1)}, s32[]{:S(2)}) async-start(s8[8388608]{0:T(1024)(128)(4,1)} %bitcast.43), calls=%async_computation.2 | async-start | bytes 8388608
  9.4 8.1 %slice-start.1 = ((s8[8388608]{0:T(1024)(128)(4,1)}), s8[4194304]{0:T(1024)(128)(4,1)S(1)}, s32[]{:S(2)}) async-start(s8[8388608]{0:T(1024)(128)(4,1)} %bitcast.43), calls=%async_computation.3 | async-start | bytes 8388608
  11.9 34.4 %collective-permute-start = (bf16[16,1,16,4096]{3,0,1,2:T(8,128)(2,1)}, bf16[16,1,16,4096]{3,0,1,2:T(8,128)(2,1)S(1)}, u32[]{:S(2)}, u32[]{:S(2)}) collective-permute-start(bf16[16,1,16,4096]{3,0,1,2:T(8,128)(2,1)} %copy.32), channel_id=1, source_target_pairs={{0,8},{8,16},{16,24},{24,32},{32,40},{40,48},{48,56},{56,64},{64,7... | collective-permute-start | bytes 6291464 | tf_op jit(solution)/shard_map/ppermute | solution.py:47
  17.5 28.9 %collective-permute-start.1 = (bf16[16,1,16,4096]{3,0,1,2:T(8,128)(2,1)}, bf16[16,1,16,4096]{3,0,1,2:T(8,128)(2,1)S(1)}, u32[]{:S(2)}, u32[]{:S(2)}) collective-permute-start(bf16[16,1,16,4096]{3,0,1,2:T(8,128)(2,1)} %copy.33), channel_id=1, source_target_pairs={{8,0},{16,8},{24,16},{32,24},{40,32},{48,40},{56,48},{64,56},{72,6... | collective-permute-start | bytes 6291464 | tf_op jit(solution)/shard_map/ppermute | solution.py:48
  17.5 6.8 %copy-start.1 = (f32[16,16]{1,0:T(8,128)S(1)}, f32[16,16]{1,0:T(8,128)}, u32[]{:S(2)}) copy-start(f32[16,16]{1,0:T(8,128)} %param.5) | copy-start | bytes 3076
  17.6 6.8 %copy-start.2 = (s32[16,16]{1,0:T(8,128)S(1)}, s32[16,16]{1,0:T(8,128)}, u32[]{:S(2)}) copy-start(s32[16,16]{1,0:T(8,128)} %param.4) | copy-start | bytes 3076
  43.0 3.4 %slice-start.2 = ((s8[6291456]{0:T(1024)(128)(4,1)}), s8[4194304]{0:T(1024)(128)(4,1)S(1)}, s32[]{:S(2)}) async-start(s8[6291456]{0:T(1024)(128)(4,1)} %bitcast.48), calls=%async_computation.4 | async-start | bytes 8388608
  43.0 4.4 %slice-start.3 = ((s8[6291456]{0:T(1024)(128)(4,1)}), s8[2097152]{0:T(1024)(128)(4,1)S(1)}, s32[]{:S(2)}) async-start(s8[6291456]{0:T(1024)(128)(4,1)} %bitcast.48), calls=%async_computation.5 | async-start | bytes 4194304
  43.1 4.4 %copy-start = (f32[2,8,16,256]{3,1,2,0:T(8,128)S(1)}, f32[2,8,16,256]{3,1,2,0:T(8,128)}, u32[]{:S(2)}) copy-start(f32[2,8,16,256]{3,1,2,0:T(8,128)} %copy.26) | copy-start | bytes 786436
Sparse Core Ops, SparseCore 0:
  100.4 113.6 all-gather.1

commit v4 on v3

--- a/solution.py
+++ b/solution.py
@@ -6,6 +6,7 @@
 from jax.sharding import PartitionSpec as P
 
 FREQS = 256
+BLOCK_CHUNKS = 2
 
 
 def dft_table(length, freqs):
@@ -44,30 +45,35 @@
     n_tm = lax.axis_size("tm")
     forward = [(i, (i + 1) % n_az) for i in range(n_az)]
     backward = [((i + 1) % n_az, i) for i in range(n_az)]
-    left = lax.ppermute(pressure[:, sector - 1 :], "az", forward)
-    right = lax.ppermute(pressure[:, :1], "az", backward)
-    weights = jnp.repeat(interp_weights(offsets, frac), sub_len, axis=2)[:, None, None]
-    prev = jnp.concatenate([left, pressure[:, :-1]], axis=1).astype(jnp.float32)
-    nxt = jnp.concatenate([pressure[:, 1:], right], axis=1).astype(jnp.float32)
-    total = weights[0] * prev + weights[1] * pressure.astype(jnp.float32) + weights[2] * nxt
-    virtual = total.astype(jnp.bfloat16).transpose(2, 1, 0, 3).reshape(blocks * sector * cycles, length)
     table = dft_table(length, FREQS)
+    all_weights = jnp.repeat(interp_weights(offsets, frac), sub_len, axis=2)[:, None, None]
     fl = FREQS // n_tm
     local_rows = sector * cycles
-    width = n_tm * blocks
-    spectra = lax.dot_general(
-        table, virtual, (((0,), (1,)), ((), ())), preferred_element_type=jnp.float32
-    ).astype(jnp.bfloat16)
-    spectra = spectra.reshape(2, n_tm, fl, blocks * local_rows).transpose(1, 0, 2, 3)
-    shared = lax.all_to_all(spectra, "tm", 0, 0, tiled=True)
-    shared = shared.reshape(n_tm, 2, fl, blocks, local_rows)
-    x = shared.transpose(2, 4, 0, 1, 3)
-    rows = x.reshape(fl, local_rows, 2 * width)
-    turned = jnp.stack([x[:, :, :, 1], -x[:, :, :, 0]], 3).reshape(fl, local_rows, 2 * width)
-    lhs = jnp.stack([rows, turned], 1)
-    columns = lax.all_gather(rows, "az", axis=1, tiled=True)
-    result = jnp.einsum("fcqk,fpk->fcqp", lhs, columns, preferred_element_type=jnp.float32)
-    return result * (1.0 / width)
+    nb = blocks // BLOCK_CHUNKS
+    result = None
+    for j in range(BLOCK_CHUNKS):
+        block = pressure[:, :, j * nb : (j + 1) * nb]
+        left = lax.ppermute(block[:, sector - 1 :], "az", forward)
+        right = lax.ppermute(block[:, :1], "az", backward)
+        weights = all_weights[:, :, :, j * nb : (j + 1) * nb]
+        prev = jnp.concatenate([left, block[:, :-1]], axis=1).astype(jnp.float32)
+        nxt = jnp.concatenate([block[:, 1:], right], axis=1).astype(jnp.float32)
+        total = weights[0] * prev + weights[1] * block.astype(jnp.float32) + weights[2] * nxt
+        virtual = total.astype(jnp.bfloat16).reshape(cycles * sector * nb, length)
+        spectra = lax.dot_general(
+            table, virtual, (((0,), (1,)), ((), ())), preferred_element_type=jnp.float32
+        ).astype(jnp.bfloat16)
+        spectra = spectra.reshape(2, n_tm, fl, cycles * sector * nb).transpose(1, 0, 2, 3)
+        shared = lax.all_to_all(spectra, "tm", 0, 0, tiled=True)
+        x = shared.reshape(n_tm, 2, fl, cycles, sector, nb).transpose(2, 4, 3, 0, 1, 5)
+        x = x.reshape(fl, local_rows, n_tm, 2, nb)
+        rows = x.reshape(fl, local_rows, n_tm * 2 * nb)
+        turned = jnp.stack([x[:, :, :, 1], -x[:, :, :, 0]], 3).reshape(rows.shape)
+        lhs = jnp.stack([rows, turned], 1)
+        columns = lax.all_gather(rows, "az", axis=1, tiled=True)
+        part = jnp.einsum("fcqk,fpk->fcqp", lhs, columns, preferred_element_type=jnp.float32)
+        result = part if result is None else result + part
+    return result * (1.0 / (n_tm * blocks))
 
 
 def solution(mesh):

time: 234 us -> 249 us (1.064)
  matrix products: 22.1 us -> 37.1 us
  blocking collectives: 16 us -> 24.7 us
  other arithmetic: 29.4 us -> 23.1 us
  starting transfers between devices: 3.02 us -> 7.66 us
  local copies, waits for them, and re-layouts: 39.1 us -> 34.7 us
  waiting for transfers between devices: 111 us -> 108 us
    unnamed x21 -> x12, local copies, waits for them, and re-layouts: 22.5 us -> 0.03 us
    dot_general x1 -> x2, matrix products: 12.9 us -> 28.9 us  [shards(): jnp.einsum('fcqk,fpk->fcqp', lhs, columns, preferred_element_type=jnp.flo...]
    all_gather x1 -> x2, waiting for transfers between devices: 111 us -> 99.7 us  [shards(): columns = lax.all_gather(rows, 'az', axis=1, tiled=True)]
    convert_element_type x1, other arithmetic: 21.5 us -> 12.3 us  [shards(): virtual = total.astype(jnp.bfloat16).reshape(cycles * sector * nb, length)]
    all_to_all x1 -> x2, blocking collectives: 16 us -> 24.7 us  [shards(): shared = lax.all_to_all(spectra, 'tm', 0, 0, tiled=True)]
    ppermute x2 -> x4, waiting for transfers between devices: 0.01 us -> 8.07 us  [the longest x2 8.06 us: shards(): right = lax.ppermute(block[:, :1], 'az', backward)]
    another operation x0 -> x3, local copies, waits for them, and re-layouts: none -> 6.82 us  [the longest x2 4.63 us: shards(): rows = x.reshape(fl, local_rows, n_tm * 2 * nb)]
    reshape x4 -> x2, local copies, waits for them, and re-layouts: 6.16 us -> 0.07 us  [shards(): spectra.reshape(2, n_tm, fl, cycles * sector * nb).transpose(1, 0, 2, 3)]
  transfers between devices with their start and end apart: 3 -> 6, of which waited for: 1 -> 3; matrix products, arithmetic and copies ran while one was open for 15% -> 21% of each run, Pallas kernels for 0% -> 0%
where the time goes in v4:
time: 249 us
  waiting for transfers between devices  108 us (43%)
  matrix products  37.1 us (15%)
  local copies, waits for them, and re-layouts  34.7 us (14%)
  blocking collectives  24.7 us (10%)
  other arithmetic  23.1 us (9%)
  between operations  13.6 us (5%)
  starting transfers between devices  7.66 us (3%)
    all_gather x2, waiting for transfers between devices, shards(): columns = lax.all_gather(rows, 'az', axis=1, tiled=True)  99.7 us
    dot_general x2, matrix products, shards(): jnp.einsum('fcqk,fpk->fcqp', lhs, columns, preferred_element_type=jnp.flo...  28.9 us
    all_to_all x2, blocking collectives, shards(): shared = lax.all_to_all(spectra, 'tm', 0, 0, tiled=True)  24.7 us
    convert_element_type x1, other arithmetic, shards(): virtual = total.astype(jnp.bfloat16).reshape(cycles * sector * nb, length)  12.3 us
    dot_general x2, matrix products, shards(): lax.dot_general(table, virtual, (((0,), (1,)), ((), ())), preferred_eleme...  8.21 us
    ppermute x2, waiting for transfers between devices, shards(): right = lax.ppermute(block[:, :1], 'az', backward)  8.06 us
    another operation x4, local copies, waits for them, and re-layouts, shards(): lhs = jnp.stack([rows, turned], 1)  7.97 us
    transpose x2, local copies, waits for them, and re-layouts, shards(): shared.reshape(n_tm, 2, fl, cycles, sector, nb).transpose(2, 4, 3, 0, 1, 5)  5.71 us
  transfers between devices with their start and end apart: 6, of which 3 were waited for; matrix products, arithmetic and copies ran while one was open for 21% of the time, Pallas kernels for 0%

profile of v4, /device:TPU:1, one launch (start us, length us, event | category | flops | bytes accessed | tf_op | source)
XLA Modules:
  0.0 248.6 jit_solution(11958431329202797710)
XLA Ops:
  6.5 0.0 all-gather.3.cloned.1.call-start
  6.5 0.0 copy-start
  6.5 4.6 %fusion.34 = (bf16[16,1,8,4096]{3,2,1,0:T(8,128)(2,1)}, bf16[16,1,8,4096]{3,2,1,0:T(8,128)(2,1)}, bf16[16,1,8,4096]{3,2,1,0:T(8,128)(2,1)}, bf16[16,1,8,4096]{3,2,1,0:T(8,128)(2,1)}) fusion(bf16[16,4,16,4096]{3,2,1,0:T(8,128)(2,1)} %param.3), kind=kLoop, calls=%fused_computation.69 | loop fusion | bytes 8388608 | tf_op jit(solution)/shard_map/slice | solution.py:57
  11.1 3.0 %collective-permute-start.2 = (bf16[16,1,8,4096]{3,2,1,0:T(8,128)(2,1)}, bf16[16,1,8,4096]{3,2,1,0:T(8,128)(2,1)}, u32[]{:S(2)}, u32[]{:S(2)}) collective-permute-start(bf16[16,1,8,4096]{3,2,1,0:T(8,128)(2,1)} %get-tuple-element.20), channel_id=1, source_target_pairs={{0,8},{8,16},{16,24},{24,32},{32,40},{40,48},{48,56},{56,64},{64,7... | collective-permute-start | bytes 3145736 | tf_op jit(solution)/shard_map/ppermute | solution.py:56
  14.1 0.0 collective-permute-start.3
  14.1 4.4 %collective-permute-start.1 = (bf16[16,1,8,4096]{3,2,1,0:T(8,128)(2,1)}, bf16[16,1,8,4096]{3,2,1,0:T(8,128)(2,1)}, u32[]{:S(2)}, u32[]{:S(2)}) collective-permute-start(bf16[16,1,8,4096]{3,2,1,0:T(8,128)(2,1)} %get-tuple-element.21), channel_id=1, source_target_pairs={{8,0},{16,8},{24,16},{32,24},{40,32},{48,40},{56,48},{64,56},{72,6... | collective-permute-start | bytes 3145736 | tf_op jit(solution)/shard_map/ppermute | solution.py:57
  18.5 0.0 collective-permute-start
  18.5 0.0 copy-done
  18.5 3.8 %fusion.33 = (bf16[16,3,8,4096]{3,2,1,0:T(8,128)(2,1)S(1)}, bf16[16,3,8,4096]{3,2,1,0:T(8,128)(2,1)}, bf16[16,3,8,4096]{3,2,1,0:T(8,128)(2,1)}, bf16[16,3,8,4096]{3,2,1,0:T(8,128)(2,1)}) fusion(bf16[16,4,16,4096]{3,2,1,0:T(8,128)(2,1)S(1)} %copy-done), kind=kLoop, calls=%fused_computation.68 | loop fusion | bytes 25165824 | tf_op jit(solution)/shard_map/slice | solution.py:60
  22.3 0.1 fusion.28
  22.4 0.1 subtract_multiply_fusion
  22.5 0.3 fusion.24
  22.8 0.3 fusion.26
  23.1 1.2 multiply_subtract_fusion
  24.3 0.0 copy-start.4
  24.3 0.0 copy-start.5
  24.3 3.2 %fusion.3 = (bf16[4096,256]{1,0:T(8,128)(2,1)}, bf16[4096,256]{1,0:T(8,128)(2,1)}) fusion(f32[64,64,256]{2,1,0:T(8,128)S(1)} %get-tuple-element.34, f32[4096]{0:T(1024)S(1)} %fusion.28, f32[64,64,256]{2,1,0:T(8,128)S(1)} %get-tuple-element.33, f32[4096]{0:T(1024)S(1)} %subtract_multiply_fusion), kind=kLoop, calls=%fused_computation.8 | loop fusion | flops 4194304 | bytes 12615680 | tf_op jit(solution)/shard_map/convert.1
  27.6 0.0 copy-done.4
  27.6 0.0 copy-done.5
  27.6 1.0 broadcast_in_dim.2
  28.7 2.2 broadcast_in_dim_reshape.3
  30.8 1.3 slice_bitcast_fusion.2
  32.1 0.0 collective-permute-done.2
  32.1 0.0 collective-permute-done.3
  32.1 8.1 %collective-permute-done.1 = bf16[16,1,8,4096]{3,2,1,0:T(8,128)(2,1)} collective-permute-done((bf16[16,1,8,4096]{3,2,1,0:T(8,128)(2,1)}, bf16[16,1,8,4096]{3,2,1,0:T(8,128)(2,1)}, u32[]{:S(2)}, u32[]{:S(2)}) %collective-permute-start.1) | collective-permute-done | bytes 1048608 | tf_op jit(solution)/shard_map/ppermute | solution.py:57
  40.2 0.0 collective-permute-done
  40.2 0.0 copy-start.2
  40.2 0.0 copy-start.3
  40.2 12.3 %add_convert_fusion = (bf16[16,4,8,4096]{3,2,1,0:T(8,128)(2,1)}, bf16[16,4,8,4096]{3,2,1,0:T(8,128)(2,1)S(1)}) fusion(bf16[16,3,8,4096]{3,2,1,0:T(8,128)(2,1)} %get-tuple-element.16, bf16[16,1,8,4096]{3,2,1,0:T(8,128)(2,1)} %collective-permute-done.2, bf16[16,1,8,4096]{3,2,1,0:T(8,128)(2,1)} %collective-permute-done.3, ...), kind=kLoop, calls=%fused_computation.4 | loop fusion | flops 46137344 | bytes 34340864 | tf_op jit(solution)/shard_map/convert_element_type | solution.py:62
  52.5 0.0 copy-done.2
  52.5 0.0 copy-done.3
  52.5 2.4 fusion.7
  54.9 12.5 %all_to_all.10 = bf16[8,2,32,512]{3,2,1,0:T(8,128)(2,1)S(1)} all-to-all(bf16[8,2,32,512]{3,2,1,0:T(8,128)(2,1)S(1)} %bitcast.80), channel_id=1, replica_groups=mesh['az'=16,'tm'=8] {'tm'}, dimensions={0} | all-to-all | bytes 1048576 | tf_op jit(solution)/shard_map/all_to_all | solution.py:67
  67.4 1.7 copy.35
  69.1 2.2 copy.36
  71.3 1.8 copy.42
  73.1 0.0 all-gather.3.cloned.1.call-update
  73.1 0.2 all-gather.5.cloned.1.call-start
  73.3 5.8 %fusion.8 = bf16[512,512]{1,0:T(8,128)(2,1)S(1)} fusion(bf16[512,4096]{1,0:T(8,128)(2,1)} %bitcast.78, bf16[4096,256]{1,0:T(8,128)(2,1)} %get-tuple-element.42, bf16[4096,256]{1,0:T(8,128)(2,1)} %get-tuple-element.43), kind=kOutput, calls=%fused_computation.18 | convolution fusion | flops 2156134400 | bytes 8912896 | tf_op jit(solution)/shard_map/dot_general | solution.py:63
  79.2 12.2 %all_to_all.11 = bf16[8,2,32,512]{3,2,1,0:T(8,128)(2,1)S(1)} all-to-all(bf16[8,2,32,512]{3,2,1,0:T(8,128)(2,1)S(1)} %bitcast.81), channel_id=1, replica_groups=mesh['az'=16,'tm'=8] {'tm'}, dimensions={0} | all-to-all | bytes 1048576 | tf_op jit(solution)/shard_map/all_to_all | solution.py:67
  91.4 1.7 copy.44
  93.1 3.5 %copy.45 = bf16[32,4,16,8,2,8]{0,5,4,3,2,1:T(8,128)(2,1)} copy(bf16[32,4,16,8,2,8]{0,5,1,2,4,3:T(8,128)(2,1)} %bitcast.77) | data formatting | bytes 1048576 | tf_op jit(solution)/shard_map/transpose | solution.py:68
  96.7 2.9 %copy.51 = bf16[32,64,128]{2,1,0:T(8,128)(2,1)} copy(bf16[32,64,128]{0,2,1:T(8,128)(2,1)} %bitcast.71) | data formatting | bytes 1048576 | tf_op jit(solution)/shard_map/reshape;reshape | solution.py:70
  99.5 0.0 all-gather.5.cloned.1.call-update
  99.6 0.3 fusion.36
  99.8 1.8 pad_maximum_fusion.3
  101.6 2.9 %copy.40 = bf16[32,1,64,128]{3,2,1,0:T(8,128)(2,1)} copy(bf16[32,1,64,128]{0,3,2,1:T(8,128)(2,1)} %bitcast.74) | data formatting | bytes 1048576 | tf_op jit(solution)/shard_map/stack;reshape | solution.py:72
  104.5 1.8 copy.39
  106.3 1.7 fusion.35
  108.0 0.0 copy-start.1
  108.0 1.8 pad_maximum_fusion.4
  109.8 2.2 copy.49
  112.0 0.0 copy-done.1
  112.0 1.1 copy.48
  113.2 38.8 %all-gather.3.cloned.1.call-done = bf16[32,1024,128]{2,1,0:T(8,128)(2,1)} async-done(((bf16[32,64,128]{2,1,0:T(8,128)(2,1)}), bf16[32,1024,128]{2,1,0:T(8,128)(2,1)}) %all-gather.3.cloned.1.call-update) | async-done | bytes 8388624 | tf_op jit(solution)/shard_map/all_gather | solution.py:73
  152.0 12.2 %fusion.1 = f32[32,2,64,1024]{3,2,1,0:T(8,128)} fusion(bf16[32,1024,128]{2,1,0:T(8,128)(2,1)} %all-gather.3.cloned.1.call-done, bf16[32,1,64,128]{3,2,1,0:T(8,128)(2,1)} %copy.40, bf16[32,1,64,128]{3,2,1,0:T(8,128)(2,1)} %copy.39), kind=kOutput, calls=%fused_computation.2 | convolution fusion | flops 1074266112 | bytes 26214400 | tf_op jit(solution)/shard_map/fcqk,fpk->fcqp/dot_general | solution.py:74
  164.2 60.8 %all-gather.5.cloned.1.call-done = bf16[32,1024,128]{2,1,0:T(8,128)(2,1)} async-done(((bf16[32,64,128]{2,1,0:T(8,128)(2,1)}), bf16[32,1024,128]{2,1,0:T(8,128)(2,1)}) %all-gather.5.cloned.1.call-update) | async-done | bytes 8388624 | tf_op jit(solution)/shard_map/all_gather | solution.py:73
  225.1 16.7 %add_multiply_fusion = f32[32,2,64,1024]{3,2,1,0:T(8,128)} fusion(f32[32,2,64,1024]{3,2,1,0:T(8,128)} %fusion.1, bf16[32,1024,128]{2,1,0:T(8,128)(2,1)} %all-gather.5.cloned.1.call-done, bf16[32,1,64,128]{3,2,1,0:T(8,128)(2,1)S(1)} %copy.49, bf16[32,1,64,128]{3,2,1,0:T(8,128)(2,1)S(1)} %copy.48), kind=kOutput, calls=%fused_computation | convolution fusion | flops 1082654720 | bytes 42991616 | tf_op jit(solution)/shard_map/fcqk,fpk->fcqp/dot_general | solution.py:74
  (6 shorter events, 0.1 us)
Async XLA Ops:
  6.5 145.5 %all-gather.3.cloned.1.call-start = ((), (), s32[]{:S(2)}) async-start(), calls=%async_computation.2 | async-start | bytes 8912896 | tf_op jit(solution)/shard_map/all_gather | solution.py:73
  6.5 12.0 %copy-start = (bf16[16,4,16,4096]{3,2,1,0:T(8,128)(2,1)S(1)}, bf16[16,4,16,4096]{3,2,1,0:T(8,128)(2,1)}, u32[]{:S(2)}) copy-start(bf16[16,4,16,4096]{3,2,1,0:T(8,128)(2,1)} %param.3) | copy-start | bytes 25165828
  11.1 21.0 %collective-permute-start.2 = (bf16[16,1,8,4096]{3,2,1,0:T(8,128)(2,1)}, bf16[16,1,8,4096]{3,2,1,0:T(8,128)(2,1)}, u32[]{:S(2)}, u32[]{:S(2)}) collective-permute-start(bf16[16,1,8,4096]{3,2,1,0:T(8,128)(2,1)} %get-tuple-element.20), channel_id=1, source_target_pairs={{0,8},{8,16},{16,24},{24,32},{32,40},{40,48},{48,56},{56,64},{64,7... | collective-permute-start | bytes 3145736 | tf_op jit(solution)/shard_map/ppermute | solution.py:56
  14.1 18.0 %collective-permute-start.3 = (bf16[16,1,8,4096]{3,2,1,0:T(8,128)(2,1)}, bf16[16,1,8,4096]{3,2,1,0:T(8,128)(2,1)}, u32[]{:S(2)}, u32[]{:S(2)}) collective-permute-start(bf16[16,1,8,4096]{3,2,1,0:T(8,128)(2,1)} %get-tuple-element.19), channel_id=1, source_target_pairs={{8,0},{16,8},{24,16},{32,24},{40,32},{48,40},{56,48},{64,56},{72,6... | collective-permute-start | bytes 3145736 | tf_op jit(solution)/shard_map/ppermute | solution.py:57
  14.1 26.1 %collective-permute-start.1 = (bf16[16,1,8,4096]{3,2,1,0:T(8,128)(2,1)}, bf16[16,1,8,4096]{3,2,1,0:T(8,128)(2,1)}, u32[]{:S(2)}, u32[]{:S(2)}) collective-permute-start(bf16[16,1,8,4096]{3,2,1,0:T(8,128)(2,1)} %get-tuple-element.21), channel_id=1, source_target_pairs={{8,0},{16,8},{24,16},{32,24},{40,32},{48,40},{56,48},{64,56},{72,6... | collective-permute-start | bytes 3145736 | tf_op jit(solution)/shard_map/ppermute | solution.py:57
  18.5 21.7 %collective-permute-start = (bf16[16,1,8,4096]{3,2,1,0:T(8,128)(2,1)}, bf16[16,1,8,4096]{3,2,1,0:T(8,128)(2,1)}, u32[]{:S(2)}, u32[]{:S(2)}) collective-permute-start(bf16[16,1,8,4096]{3,2,1,0:T(8,128)(2,1)} %get-tuple-element.22), channel_id=1, source_target_pairs={{0,8},{8,16},{16,24},{24,32},{32,40},{40,48},{48,56},{56,64},{64,7... | collective-permute-start | bytes 3145736 | tf_op jit(solution)/shard_map/ppermute | solution.py:56
  24.3 3.3 %copy-start.4 = (f32[16,16]{1,0:T(8,128)S(1)}, f32[16,16]{1,0:T(8,128)}, u32[]{:S(2)}) copy-start(f32[16,16]{1,0:T(8,128)} %param.5) | copy-start | bytes 3076
  24.3 3.3 %copy-start.5 = (s32[16,16]{1,0:T(8,128)S(1)}, s32[16,16]{1,0:T(8,128)}, u32[]{:S(2)}) copy-start(s32[16,16]{1,0:T(8,128)} %param.4) | copy-start | bytes 3076
  40.2 12.3 %copy-start.2 = (bf16[4096,256]{1,0:T(8,128)(2,1)S(1)}, bf16[4096,256]{1,0:T(8,128)(2,1)}, u32[]{:S(2)}) copy-start(bf16[4096,256]{1,0:T(8,128)(2,1)} %get-tuple-element.42) | copy-start | bytes 6291460
  40.2 12.3 %copy-start.3 = (bf16[4096,256]{1,0:T(8,128)(2,1)S(1)}, bf16[4096,256]{1,0:T(8,128)(2,1)}, u32[]{:S(2)}) copy-start(bf16[4096,256]{1,0:T(8,128)(2,1)} %get-tuple-element.43) | copy-start | bytes 6291460
  73.1 152.0 %all-gather.5.cloned.1.call-start = ((), (), s32[]{:S(2)}) async-start(), calls=%async_computation.3 | async-start | bytes 8912896 | tf_op jit(solution)/shard_map/all_gather | solution.py:73
  108.0 4.0 %copy-start.1 = (bf16[32,4,16,8,2,8]{0,5,4,3,2,1:T(8,128)(2,1)S(1)}, bf16[32,4,16,8,2,8]{0,5,4,3,2,1:T(8,128)(2,1)}, u32[]{:S(2)}) copy-start(bf16[32,4,16,8,2,8]{0,5,4,3,2,1:T(8,128)(2,1)} %copy.45) | copy-start | bytes 1572868
Sparse Core Ops, SparseCore 0:
  73.2 78.7 all-gather.2
  154.5 70.5 all-gather.4

commit v5 on v4

--- a/solution.py
+++ b/solution.py
@@ -6,7 +6,7 @@
 from jax.sharding import PartitionSpec as P
 
 FREQS = 256
-BLOCK_CHUNKS = 2
+BLOCK_CHUNKS = 1
 
 
 def dft_table(length, freqs):

time: 249 us -> 214 us (0.86)
  matrix products: 37.1 us -> 19.3 us
  blocking collectives: 24.7 us -> 15.2 us
  waiting for transfers between devices: 108 us -> 116 us
  local copies, waits for them, and re-layouts: 34.7 us -> 28.6 us
  other arithmetic: 23.1 us -> 18 us
  starting transfers between devices: 7.66 us -> 3.17 us
    dot_general x2 -> x1, matrix products: 28.9 us -> 12.5 us  [shards(): jnp.einsum('fcqk,fpk->fcqp', lhs, columns, preferred_element_type=jnp.flo...]
    all_to_all x2 -> x1, blocking collectives: 24.7 us -> 15.2 us  [shards(): shared = lax.all_to_all(spectra, 'tm', 0, 0, tiled=True)]
    ppermute x2 -> x1, waiting for transfers between devices: 8.06 us -> 14.1 us  [shards(): right = lax.ppermute(block[:, :1], 'az', backward)]
    convert_element_type x1, other arithmetic: 12.3 us -> 7.67 us  [shards(): virtual = total.astype(jnp.bfloat16).reshape(cycles * sector * nb, length)]
    unnamed x12 -> x11, local copies, waits for them, and re-layouts: 0.03 us -> 3.16 us
    ppermute x2 -> x1, starting transfers between devices: 4.42 us -> 1.45 us  [shards(): right = lax.ppermute(block[:, :1], 'az', backward)]
    all_gather x2 -> x1, waiting for transfers between devices: 99.7 us -> 102 us  [shards(): columns = lax.all_gather(rows, 'az', axis=1, tiled=True)]
    dot_general x2 -> x1, matrix products: 8.21 us -> 6.81 us  [shards(): lax.dot_general(table, virtual, (((0,), (1,)), ((), ())), preferred_eleme...]
  transfers between devices with their start and end apart: 6 -> 3, of which waited for: 3 -> 2; matrix products, arithmetic and copies ran while one was open for 21% -> 11% of each run, Pallas kernels for 0% -> 0%
where the time goes in v5:
time: 214 us
  waiting for transfers between devices  116 us (54%)
  local copies, waits for them, and re-layouts  28.6 us (13%)
  matrix products  19.3 us (9%)
  other arithmetic  18 us (8%)
  blocking collectives  15.2 us (7%)
  between operations  13.5 us (6%)
  starting transfers between devices  3.17 us (1%)
    all_gather x1, waiting for transfers between devices, shards(): columns = lax.all_gather(rows, 'az', axis=1, tiled=True)  102 us
    all_to_all x1, blocking collectives, shards(): shared = lax.all_to_all(spectra, 'tm', 0, 0, tiled=True)  15.2 us
    ppermute x1, waiting for transfers between devices, shards(): right = lax.ppermute(block[:, :1], 'az', backward)  14.1 us
    dot_general x1, matrix products, shards(): jnp.einsum('fcqk,fpk->fcqp', lhs, columns, preferred_element_type=jnp.flo...  12.5 us
    another operation x2, local copies, waits for them, and re-layouts, shards(): lhs = jnp.stack([rows, turned], 1)  7.81 us
    convert_element_type x1, other arithmetic, shards(): virtual = total.astype(jnp.bfloat16).reshape(cycles * sector * nb, length)  7.67 us
    dot_general x1, matrix products, shards(): lax.dot_general(table, virtual, (((0,), (1,)), ((), ())), preferred_eleme...  6.81 us
    transpose x1, local copies, waits for them, and re-layouts, shards(): shared.reshape(n_tm, 2, fl, cycles, sector, nb).transpose(2, 4, 3, 0, 1, 5)  5.36 us
  transfers between devices with their start and end apart: 3, of which 2 were waited for; matrix products, arithmetic and copies ran while one was open for 11% of the time, Pallas kernels for 0%

profile of v5, /device:TPU:1, one launch (start us, length us, event | category | flops | bytes accessed | tf_op | source)
XLA Modules:
  0.0 213.6 jit_solution(7524426625062007662)
XLA Ops:
  6.5 0.0 copy-start
  6.5 0.0 copy-start.1
  6.5 0.0 all-gather.2.cloned.1.call-start
  6.5 2.5 %fusion.33 = (bf16[16,1,16,4096]{3,2,1,0:T(8,128)(2,1)S(1)}, bf16[16,1,16,4096]{3,2,1,0:T(8,128)(2,1)S(1)}) fusion(bf16[16,4,16,4096]{3,2,1,0:T(8,128)(2,1)} %param.3), kind=kLoop, calls=%fused_computation.52 | loop fusion | bytes 8388608 | tf_op jit(solution)/shard_map/slice | solution.py:57
  9.1 1.5 collective-permute-start.1
  10.5 1.7 collective-permute-start
  12.2 0.1 fusion.29
  12.3 0.1 subtract_multiply_fusion
  12.4 0.3 fusion.25
  12.7 0.3 fusion.27
  13.0 0.0 copy-done
  13.0 0.0 copy-done.1
  13.1 0.1 broadcast_in_dim.22
  13.2 0.9 copy.31
  14.0 0.1 broadcast_in_dim.26
  14.1 0.9 copy.33
  15.0 0.1 broadcast_in_dim.24
  15.1 0.9 copy.32
  16.0 0.0 slice-start
  16.0 0.9 multiply_subtract_fusion
  16.8 0.0 slice-start.1
  16.9 3.2 %fusion.8 = (bf16[4096,256]{1,0:T(8,128)(2,1)}, bf16[4096,256]{1,0:T(8,128)(2,1)}) fusion(f32[64,64,256]{2,1,0:T(8,128)S(1)} %get-tuple-element.20, f32[4096]{0:T(1024)S(1)} %fusion.29, f32[64,64,256]{2,1,0:T(8,128)S(1)} %get-tuple-element.19, f32[4096]{0:T(1024)S(1)} %subtract_multiply_fusion), kind=kLoop, calls=%fused_computation.10 | loop fusion | flops 4194304 | bytes 12615680 | tf_op jit(solution)/shard_map/convert.1
  20.0 0.0 slice-done
  20.0 0.5 slice-done.1
  20.6 1.5 fusion.32
  22.1 14.1 %collective-permute-done.1 = bf16[16,1,16,4096]{3,2,1,0:T(8,128)(2,1)S(1)} collective-permute-done((bf16[16,1,16,4096]{3,2,1,0:T(8,128)(2,1)S(1)}, bf16[16,1,16,4096]{3,2,1,0:T(8,128)(2,1)S(1)}, u32[]{:S(2)}, u32[]{:S(2)}) %collective-permute-start.1) | collective-permute-done | bytes 2097184 | tf_op jit(solution)/shard_map/ppermute | solution.py:57
  36.2 0.0 collective-permute-done
  36.2 7.7 %add_convert_fusion = bf16[16,4,16,4096]{3,2,1,0:T(8,128)(2,1)S(1)} fusion(bf16[16,4,16,4096]{3,2,1,0:T(8,128)(2,1)S(1)} %bitcast.39, bf16[16,3,16,4096]{3,2,1,0:T(8,128)(2,1)S(1)} %get-tuple-element.14, bf16[16,1,16,4096]{3,2,1,0:T(8,128)(2,1)S(1)} %collective-permute-done, bf16[16,1,16,4096]{3,2,1,0:T(8,128)(2,1)S(1)} %collective-permute-done.1, ...), kind=kLoop, calls=%fused_computation.2 | loop fusion | flops 46137344 | bytes 34340864 | tf_op jit(solution)/shard_map/convert_element_type | solution.py:62
  43.9 6.8 %fusion.13 = bf16[512,1024]{1,0:T(8,128)(2,1)S(1)} fusion(bf16[1024,4096]{1,0:T(8,128)(2,1)S(1)} %bitcast.45, bf16[4096,256]{1,0:T(8,128)(2,1)} %get-tuple-element.28, bf16[4096,256]{1,0:T(8,128)(2,1)} %get-tuple-element.29), kind=kOutput, calls=%fused_computation.19 | convolution fusion | flops 4303880192 | bytes 13631488 | tf_op jit(solution)/shard_map/dot_general | solution.py:63
  50.7 0.1 copy.35
  50.8 15.2 %all_to_all.5 = bf16[8,2,32,1024]{3,2,1,0:T(8,128)(2,1)S(1)} all-to-all(bf16[8,2,32,1024]{3,2,1,0:T(8,128)(2,1)S(1)} %bitcast.46), channel_id=1, replica_groups=mesh['az'=16,'tm'=8] {'tm'}, dimensions={0} | all-to-all | bytes 2097152 | tf_op jit(solution)/shard_map/all_to_all | solution.py:67
  66.0 3.1 %copy.20 = bf16[8,2,32,1024]{2,3,1,0:T(8,128)(2,1)} copy(bf16[8,2,32,1024]{3,2,1,0:T(8,128)(2,1)S(1)} %all_to_all.5) | data formatting | bytes 2097152 | tf_op jit(solution)/shard_map/all_to_all | solution.py:67
  69.0 5.4 %copy.21 = bf16[32,4,16,8,2,16]{0,5,4,3,2,1:T(8,128)(2,1)} copy(bf16[32,4,16,8,2,16]{0,5,1,2,4,3:T(8,128)(2,1)} %bitcast.44) | data formatting | bytes 2097152 | tf_op jit(solution)/shard_map/transpose | solution.py:68
  74.4 4.8 %copy.27 = bf16[32,64,256]{2,1,0:T(8,128)(2,1)} copy(bf16[32,64,256]{0,2,1:T(8,128)(2,1)} %bitcast.40) | data formatting | bytes 2097152 | tf_op jit(solution)/shard_map/reshape;reshape | solution.py:70
  79.2 0.0 all-gather.2.cloned.1.call-update
  79.3 3.9 %copy.24 = bf16[32,1,64,256]{3,2,1,0:T(8,128)(2,1)S(1)} copy(bf16[32,1,64,256]{0,3,2,1:T(8,128)(2,1)} %bitcast.41) | data formatting | bytes 2097152 | tf_op jit(solution)/shard_map/stack;reshape;reshape | solution.py:72
  83.2 2.6 %fusion.34 = (bf16[32,64,8,1,16]{0,4,3,2,1:T(8,128)(2,1)S(1)}, bf16[32,64,8,1,16]{0,4,3,2,1:T(8,128)(2,1)S(1)}) fusion(bf16[32,64,8,2,16]{0,4,3,2,1:T(8,128)(2,1)} %bitcast.42), kind=kLoop, calls=%fused_computation.53 | loop fusion | flops 262144 | bytes 2097152 | tf_op jit(solution)/shard_map/slice | solution.py:71
  85.8 2.8 %pad_maximum_fusion = bf16[32,64,8,2,16]{0,4,3,2,1:T(8,128)(2,1)} fusion(bf16[32,64,8,1,16]{0,4,3,2,1:T(8,128)(2,1)S(1)} %get-tuple-element.18, bf16[32,64,8,1,16]{0,4,3,2,1:T(8,128)(2,1)S(1)} %get-tuple-element.17), kind=kLoop, calls=%fused_computation.8 | loop fusion | flops 524288 | bytes 2097152 | tf_op jit(solution)/shard_map/stack | solution.py:71
  88.6 3.9 %copy.25 = bf16[32,1,64,256]{3,2,1,0:T(8,128)(2,1)S(1)} copy(bf16[32,1,64,256]{0,3,2,1:T(8,128)(2,1)} %bitcast.43) | data formatting | bytes 2097152 | tf_op jit(solution)/shard_map/stack;reshape | solution.py:72
  92.5 101.8 %all-gather.2.cloned.1.call-done = bf16[32,1024,256]{2,1,0:T(8,128)(2,1)} async-done(((bf16[32,64,256]{2,1,0:T(8,128)(2,1)}), bf16[32,1024,256]{2,1,0:T(8,128)(2,1)}) %all-gather.2.cloned.1.call-update) | async-done | bytes 16777232 | tf_op jit(solution)/shard_map/all_gather | solution.py:73
  194.3 12.5 %broadcast_multiply_fusion = f32[32,2,64,1024]{3,2,1,0:T(8,128)} fusion(bf16[32,1024,256]{2,1,0:T(8,128)(2,1)} %all-gather.2.cloned.1.call-done, bf16[32,1,64,256]{3,2,1,0:T(8,128)(2,1)S(1)} %copy.25, bf16[32,1,64,256]{3,2,1,0:T(8,128)(2,1)S(1)} %copy.24), kind=kOutput, calls=%fused_computation.3 | convolution fusion | flops 2152726528 | bytes 35651584 | tf_op jit(solution)/shard_map/fcqk,fpk->fcqp/dot_general | solution.py:74
  (4 shorter events, 0.0 us)
Async XLA Ops:
  6.5 6.5 %copy-start = (f32[16,16]{1,0:T(8,128)S(1)}, f32[16,16]{1,0:T(8,128)}, u32[]{:S(2)}) copy-start(f32[16,16]{1,0:T(8,128)} %param.5) | copy-start | bytes 3076
  6.5 6.5 %copy-start.1 = (s32[16,16]{1,0:T(8,128)S(1)}, s32[16,16]{1,0:T(8,128)}, u32[]{:S(2)}) copy-start(s32[16,16]{1,0:T(8,128)} %param.4) | copy-start | bytes 3076
  6.5 187.8 %all-gather.2.cloned.1.call-start = ((), (), s32[]{:S(2)}) async-start(), calls=%async_computation.1 | async-start | bytes 17825792 | tf_op jit(solution)/shard_map/all_gather | solution.py:73
  9.1 27.1 %collective-permute-start.1 = (bf16[16,1,16,4096]{3,2,1,0:T(8,128)(2,1)S(1)}, bf16[16,1,16,4096]{3,2,1,0:T(8,128)(2,1)S(1)}, u32[]{:S(2)}, u32[]{:S(2)}) collective-permute-start(bf16[16,1,16,4096]{3,2,1,0:T(8,128)(2,1)S(1)} %get-tuple-element.15), channel_id=1, source_target_pairs={{8,0},{16,8},{24,16},{32,24},{40,32},{48,40},{56,48},{64,56},{72,6... | collective-permute-start | bytes 6291464 | tf_op jit(solution)/shard_map/ppermute | solution.py:57
  10.5 25.7 %collective-permute-start = (bf16[16,1,16,4096]{3,2,1,0:T(8,128)(2,1)S(1)}, bf16[16,1,16,4096]{3,2,1,0:T(8,128)(2,1)S(1)}, u32[]{:S(2)}, u32[]{:S(2)}) collective-permute-start(bf16[16,1,16,4096]{3,2,1,0:T(8,128)(2,1)S(1)} %get-tuple-element.16), channel_id=1, source_target_pairs={{0,8},{8,16},{16,24},{24,32},{32,40},{40,48},{48,56},{56,64},{64,7... | collective-permute-start | bytes 6291464 | tf_op jit(solution)/shard_map/ppermute | solution.py:56
  16.0 4.1 %slice-start = ((s8[8388608]{0:T(1024)(128)(4,1)}), s8[4194304]{0:T(1024)(128)(4,1)S(1)}, s32[]{:S(2)}) async-start(s8[8388608]{0:T(1024)(128)(4,1)} %bitcast.38), calls=%async_computation.2 | async-start | bytes 8388608
  16.8 3.7 %slice-start.1 = ((s8[8388608]{0:T(1024)(128)(4,1)}), s8[4194304]{0:T(1024)(128)(4,1)S(1)}, s32[]{:S(2)}) async-start(s8[8388608]{0:T(1024)(128)(4,1)} %bitcast.38), calls=%async_computation.3 | async-start | bytes 8388608
Sparse Core Ops, SparseCore 0:
  79.4 114.8 all-gather.1

commit v6 on v5

--- a/solution.py
+++ b/solution.py
@@ -53,16 +53,27 @@
     result = None
     for j in range(BLOCK_CHUNKS):
         block = pressure[:, :, j * nb : (j + 1) * nb]
-        left = lax.ppermute(block[:, sector - 1 :], "az", forward)
-        right = lax.ppermute(block[:, :1], "az", backward)
         weights = all_weights[:, :, :, j * nb : (j + 1) * nb]
-        prev = jnp.concatenate([left, block[:, :-1]], axis=1).astype(jnp.float32)
-        nxt = jnp.concatenate([block[:, 1:], right], axis=1).astype(jnp.float32)
+
+        def transform(v):
+            rows = v.astype(jnp.bfloat16).reshape(-1, length)
+            return lax.dot_general(
+                table, rows, (((0,), (1,)), ((), ())), preferred_element_type=jnp.float32
+            )
+
+        to_next = transform(weights[0] * block[:, sector - 1 :].astype(jnp.float32))
+        to_prev = transform(weights[2] * block[:, :1].astype(jnp.float32))
+        from_prev = lax.ppermute(to_next, "az", forward).reshape(2 * FREQS, cycles, 1, nb)
+        from_next = lax.ppermute(to_prev, "az", backward).reshape(2 * FREQS, cycles, 1, nb)
+        zero = jnp.zeros_like(block[:, :1])
+        prev = jnp.concatenate([zero, block[:, :-1]], axis=1).astype(jnp.float32)
+        nxt = jnp.concatenate([block[:, 1:], zero], axis=1).astype(jnp.float32)
         total = weights[0] * prev + weights[1] * block.astype(jnp.float32) + weights[2] * nxt
-        virtual = total.astype(jnp.bfloat16).reshape(cycles * sector * nb, length)
-        spectra = lax.dot_general(
-            table, virtual, (((0,), (1,)), ((), ())), preferred_element_type=jnp.float32
-        ).astype(jnp.bfloat16)
+        inner = transform(total).reshape(2 * FREQS, cycles, sector, nb)
+        edges = jnp.concatenate(
+            [from_prev, jnp.zeros((2 * FREQS, cycles, sector - 2, nb), jnp.float32), from_next], axis=2
+        )
+        spectra = (inner + edges).astype(jnp.bfloat16)
         spectra = spectra.reshape(2, n_tm, fl, cycles * sector * nb).transpose(1, 0, 2, 3)
         shared = lax.all_to_all(spectra, "tm", 0, 0, tiled=True)
         x = shared.reshape(n_tm, 2, fl, cycles, sector, nb).transpose(2, 4, 3, 0, 1, 5)

time: 214 us -> 213 us (level)
  waiting for transfers between devices: 116 us -> 102 us
  local copies, waits for them, and re-layouts: 28.6 us -> 39.1 us
  matrix products: 19.3 us -> 26.3 us
  other arithmetic: 18 us -> 13.6 us
    ppermute x2, waiting for transfers between devices: 14.1 us -> 0.01 us  [the longest x1 0.01 us: shards(): lax.ppermute(to_next, 'az', forward).reshape(2 * FREQS, cycles, 1, nb)]
    dot_general x1 -> x3, matrix products: 6.81 us -> 13.8 us  [transform(): lax.dot_general(table, rows, (((0,), (1,)), ((), ())), preferred_element_...]
    convert_element_type x1, other arithmetic: 7.67 us -> 3.23 us  [transform(): rows = v.astype(jnp.bfloat16).reshape(-1, length)]
    transpose x0 -> x1, local copies, waits for them, and re-layouts: none -> 4.42 us  [shards(): spectra.reshape(2, n_tm, fl, cycles * sector * nb).transpose(1, 0, 2, 3)]
    reshape x1, local copies, waits for them, and re-layouts: 0.09 us -> 3.73 us  [shards(): spectra.reshape(2, n_tm, fl, cycles * sector * nb).transpose(1, 0, 2, 3)]
    ppermute x0 -> x2, local copies, waits for them, and re-layouts: none -> 3.09 us  [the longest x1 2.05 us: shards(): lax.ppermute(to_next, 'az', forward).reshape(2 * FREQS, cycles, 1, nb)]
    slice x2 -> x1, local copies, waits for them, and re-layouts: 4.02 us -> 5.18 us  [shards(): prev = jnp.concatenate([zero, block[:, :-1]], axis=1).astype(jnp.float32)]
  transfers between devices with their start and end apart: 3 -> 3, of which waited for: 2 -> 1; matrix products, arithmetic and copies ran while one was open for 11% -> 11% of each run, Pallas kernels for 0% -> 0%
where the time goes in v6:
time: 213 us
  waiting for transfers between devices  102 us (48%)
  local copies, waits for them, and re-layouts  39.1 us (18%)
  matrix products  26.3 us (12%)
  blocking collectives  15.2 us (7%)
  other arithmetic  13.6 us (6%)
  between operations  13.5 us (6%)
  starting transfers between devices  3.12 us (1%)
    all_gather x1, waiting for transfers between devices, shards(): columns = lax.all_gather(rows, 'az', axis=1, tiled=True)  102 us
    all_to_all x1, blocking collectives, shards(): shared = lax.all_to_all(spectra, 'tm', 0, 0, tiled=True)  15.2 us
    dot_general x3, matrix products, transform(): lax.dot_general(table, rows, (((0,), (1,)), ((), ())), preferred_element_...  13.8 us
    dot_general x1, matrix products, shards(): jnp.einsum('fcqk,fpk->fcqp', lhs, columns, preferred_element_type=jnp.flo...  12.5 us
    another operation x2, local copies, waits for them, and re-layouts, shards(): lhs = jnp.stack([rows, turned], 1)  7.81 us
    transpose x1, local copies, waits for them, and re-layouts, shards(): shared.reshape(n_tm, 2, fl, cycles, sector, nb).transpose(2, 4, 3, 0, 1, 5)  5.36 us
    slice x1, local copies, waits for them, and re-layouts, shards(): prev = jnp.concatenate([zero, block[:, :-1]], axis=1).astype(jnp.float32)  5.18 us
    another operation x1, local copies, waits for them, and re-layouts, shards(): rows = x.reshape(fl, local_rows, n_tm * 2 * nb)  4.85 us
  transfers between devices with their start and end apart: 3, of which 1 were waited for; matrix products, arithmetic and copies ran while one was open for 11% of the time, Pallas kernels for 0%

profile of v6, /device:TPU:1, one launch (start us, length us, event | category | flops | bytes accessed | tf_op | source)
XLA Modules:
  0.0 212.6 jit_solution(15911288217753831179)
XLA Ops:
  6.5 0.0 all-gather.2.cloned.1.call-start
  6.5 0.1 fusion.29
  6.6 0.1 subtract_multiply_fusion
  6.7 0.3 fusion.25
  7.0 0.3 fusion.27
  7.3 0.7 select_add_fusion.1
  8.0 0.1 broadcast_in_dim.26
  8.1 0.2 copy.48
  8.3 0.1 broadcast_in_dim.30
  8.4 0.2 copy.50
  8.6 0.0 copy-start.1
  8.6 3.2 %multiply_convert_fusion.1 = (bf16[16,1,16,4096]{3,2,1,0:T(8,128)(2,1)S(1)}, bf16[16,1,16,4096]{3,2,1,0:T(8,128)(2,1)S(1)}) fusion(bf16[16,4,16,4096]{3,2,1,0:T(8,128)(2,1)} %param.3, f32[16,4096]{1,0:T(8,128)S(1)} %bitcast.60, f32[16,4096]{1,0:T(8,128)S(1)} %bitcast.62), kind=kLoop, calls=%fused_computation.13 | loop fusion | flops 6291456 | bytes 8912896 | tf_op jit(solution)/shard_map/convert_element_type | solution.py:59
  11.8 0.0 copy-done.1
  11.8 1.2 multiply_subtract_fusion
  13.1 2.2 %fusion.6 = (bf16[4096,256]{1,0:T(8,128)(2,1)S(1)}, bf16[4096,256]{1,0:T(8,128)(2,1)S(1)}) fusion(f32[64,64,256]{2,1,0:T(8,128)S(1)} %get-tuple-element.20, f32[4096]{0:T(1024)S(1)} %fusion.29, f32[64,64,256]{2,1,0:T(8,128)S(1)} %get-tuple-element.19, f32[4096]{0:T(1024)S(1)} %subtract_multiply_fusion), kind=kLoop, calls=%fused_computation.9 | loop fusion | flops 4194304 | bytes 12615680 | tf_op jit(solution)/shard_map/convert.1
  15.2 0.0 copy-start
  15.2 0.0 slice-start
  15.2 1.3 fusion.12
  16.6 1.5 collective-permute-start.1
  18.0 0.0 slice-start.1
  18.0 0.0 copy-done
  18.0 2.1 fusion.13
  20.1 1.7 collective-permute-start
  21.8 0.0 slice-done
  21.8 0.0 slice-done.1
  21.8 5.2 %fusion.35 = (bf16[16,3,16,4096]{3,2,1,0:T(8,128)(2,1)}, bf16[16,3,16,4096]{3,2,1,0:T(8,128)(2,1)}) fusion(bf16[16,4,16,4096]{3,2,1,0:T(8,128)(2,1)S(1)} %bitcast.54), kind=kLoop, calls=%fused_computation.57 | loop fusion | bytes 25165824 | tf_op jit(solution)/shard_map/slice | solution.py:69
  27.0 0.1 broadcast_in_dim.28
  27.1 0.9 copy.49
  28.0 0.1 pad.7.clone
  28.0 0.0 collective-permute-done.1
  28.0 1.0 copy.34
  29.1 0.0 collective-permute-done
  29.1 2.1 copy.33
  31.1 10.4 %fusion.8 = bf16[512,16,4,16]{0,3,2,1:T(8,128)(2,1)S(1)} fusion(f32[512,16,1,16]{0,3,2,1:T(8,128)} %bitcast.67, f32[512,16,1,16]{0,3,2,1:T(8,128)} %bitcast.68, bf16[16,4,16,4096]{3,2,1,0:T(8,128)(2,1)} %param.3, bf16[16,3,16,4096]{3,2,1,0:T(8,128)(2,1)} %get-tuple-element.14, f32[16,4096]{1,0:T(8,128)} %bitcast.63, f32[16,4096]{1,0:T(8,128)} %bitcast.73, ...), kind=kOutput, calls=%fused_computation.18 | convolution fusion | flops 4343201792 | bytes 28049424 | tf_op jit(solution)/shard_map/dot_general | solution.py:60
  41.5 3.7 %reshape.305 = bf16[2,8,32,1024]{2,1,0,3:T(8,128)(2,1)} reshape(bf16[512,16,4,16]{0,3,2,1:T(8,128)(2,1)S(1)} %fusion.8) | data formatting | bytes 2097152 | tf_op jit(solution)/shard_map/reshape | solution.py:77
  45.2 4.4 %copy.35 = bf16[8,2,32,1024]{3,2,1,0:T(8,128)(2,1)S(1)} copy(bf16[8,2,32,1024]{2,0,1,3:T(8,128)(2,1)} %bitcast.55) | data formatting | bytes 2097152 | tf_op jit(solution)/shard_map/transpose | solution.py:77
  49.7 15.2 %all_to_all.5 = bf16[8,2,32,1024]{3,2,1,0:T(8,128)(2,1)S(1)} all-to-all(bf16[8,2,32,1024]{3,2,1,0:T(8,128)(2,1)S(1)} %copy.35), channel_id=1, replica_groups=mesh['az'=16,'tm'=8] {'tm'}, dimensions={0} | all-to-all | bytes 2097152 | tf_op jit(solution)/shard_map/all_to_all | solution.py:78
  64.9 3.1 %copy.36 = bf16[8,2,32,1024]{2,3,1,0:T(8,128)(2,1)} copy(bf16[8,2,32,1024]{3,2,1,0:T(8,128)(2,1)S(1)} %all_to_all.5) | data formatting | bytes 2097152 | tf_op jit(solution)/shard_map/all_to_all | solution.py:78
  67.9 5.4 %copy.37 = bf16[32,4,16,8,2,16]{0,5,4,3,2,1:T(8,128)(2,1)} copy(bf16[32,4,16,8,2,16]{0,5,1,2,4,3:T(8,128)(2,1)} %bitcast.57) | data formatting | bytes 2097152 | tf_op jit(solution)/shard_map/transpose | solution.py:79
  73.3 4.8 %copy.43 = bf16[32,64,256]{2,1,0:T(8,128)(2,1)} copy(bf16[32,64,256]{0,2,1:T(8,128)(2,1)} %bitcast.50) | data formatting | bytes 2097152 | tf_op jit(solution)/shard_map/reshape;reshape | solution.py:81
  78.1 0.0 all-gather.2.cloned.1.call-update
  78.1 3.9 %copy.40 = bf16[32,1,64,256]{3,2,1,0:T(8,128)(2,1)S(1)} copy(bf16[32,1,64,256]{0,3,2,1:T(8,128)(2,1)} %bitcast.51) | data formatting | bytes 2097152 | tf_op jit(solution)/shard_map/stack;reshape;reshape | solution.py:83
  82.1 2.6 %fusion.36 = (bf16[32,64,8,1,16]{0,4,3,2,1:T(8,128)(2,1)S(1)}, bf16[32,64,8,1,16]{0,4,3,2,1:T(8,128)(2,1)S(1)}) fusion(bf16[32,64,8,2,16]{0,4,3,2,1:T(8,128)(2,1)} %bitcast.52), kind=kLoop, calls=%fused_computation.58 | loop fusion | flops 262144 | bytes 2097152 | tf_op jit(solution)/shard_map/slice | solution.py:82
  84.7 2.8 %pad_maximum_fusion.1 = bf16[32,64,8,2,16]{0,4,3,2,1:T(8,128)(2,1)} fusion(bf16[32,64,8,1,16]{0,4,3,2,1:T(8,128)(2,1)S(1)} %get-tuple-element.18, bf16[32,64,8,1,16]{0,4,3,2,1:T(8,128)(2,1)S(1)} %get-tuple-element.17), kind=kLoop, calls=%fused_computation.6 | loop fusion | flops 524288 | bytes 2097152 | tf_op jit(solution)/shard_map/stack | solution.py:82
  87.5 3.9 %copy.41 = bf16[32,1,64,256]{3,2,1,0:T(8,128)(2,1)S(1)} copy(bf16[32,1,64,256]{0,3,2,1:T(8,128)(2,1)} %bitcast.56) | data formatting | bytes 2097152 | tf_op jit(solution)/shard_map/stack;reshape | solution.py:83
  91.4 101.9 %all-gather.2.cloned.1.call-done = bf16[32,1024,256]{2,1,0:T(8,128)(2,1)} async-done(((bf16[32,64,256]{2,1,0:T(8,128)(2,1)}), bf16[32,1024,256]{2,1,0:T(8,128)(2,1)}) %all-gather.2.cloned.1.call-update) | async-done | bytes 16777232 | tf_op jit(solution)/shard_map/all_gather | solution.py:84
  193.3 12.5 %broadcast_multiply_fusion = f32[32,2,64,1024]{3,2,1,0:T(8,128)} fusion(bf16[32,1024,256]{2,1,0:T(8,128)(2,1)} %all-gather.2.cloned.1.call-done, bf16[32,1,64,256]{3,2,1,0:T(8,128)(2,1)S(1)} %copy.41, bf16[32,1,64,256]{3,2,1,0:T(8,128)(2,1)S(1)} %copy.40), kind=kOutput, calls=%fused_computation.3 | convolution fusion | flops 2152726528 | bytes 35651584 | tf_op jit(solution)/shard_map/fcqk,fpk->fcqp/dot_general | solution.py:85
  (4 shorter events, 0.0 us)
Async XLA Ops:
  6.5 186.8 %all-gather.2.cloned.1.call-start = ((), (), s32[]{:S(2)}) async-start(), calls=%async_computation.1 | async-start | bytes 17825792 | tf_op jit(solution)/shard_map/all_gather | solution.py:84
  8.6 3.3 %copy-start.1 = (f32[2,8,16,256]{3,1,2,0:T(8,128)}, f32[2,8,16,256]{3,1,2,0:T(8,128)S(1)}, u32[]{:S(2)}) copy-start(f32[2,8,16,256]{3,1,2,0:T(8,128)S(1)} %copy.50) | copy-start | bytes 786436
  15.2 2.8 %copy-start = (bf16[4096,256]{1,0:T(8,128)(2,1)}, bf16[4096,256]{1,0:T(8,128)(2,1)S(1)}, u32[]{:S(2)}) copy-start(bf16[4096,256]{1,0:T(8,128)(2,1)S(1)} %get-tuple-element.29) | copy-start | bytes 6291460
  15.2 6.6 %slice-start = ((s8[8388608]{0:T(1024)(128)(4,1)}), s8[4194304]{0:T(1024)(128)(4,1)S(1)}, s32[]{:S(2)}) async-start(s8[8388608]{0:T(1024)(128)(4,1)} %bitcast.53), calls=%async_computation.2 | async-start | bytes 8388608
  16.6 11.5 %collective-permute-start.1 = (f32[512,256]{1,0:T(8,128)S(1)}, f32[512,256]{1,0:T(8,128)S(1)}, u32[]{:S(2)}, u32[]{:S(2)}) collective-permute-start(f32[512,256]{1,0:T(8,128)S(1)} %fusion.12), channel_id=1, source_target_pairs={{8,0},{16,8},{24,16},{32,24},{40,32},{48,40},{56,48},{64,56},{72,6... | collective-permute-start | bytes 1572872 | tf_op jit(solution)/shard_map/ppermute | solution.py:67
  18.0 3.8 %slice-start.1 = ((s8[8388608]{0:T(1024)(128)(4,1)}), s8[4194304]{0:T(1024)(128)(4,1)S(1)}, s32[]{:S(2)}) async-start(s8[8388608]{0:T(1024)(128)(4,1)} %bitcast.53), calls=%async_computation.3 | async-start | bytes 8388608
  20.1 9.0 %collective-permute-start = (f32[512,256]{1,0:T(8,128)}, f32[512,256]{1,0:T(8,128)}, u32[]{:S(2)}, u32[]{:S(2)}) collective-permute-start(f32[512,256]{1,0:T(8,128)} %fusion.13), channel_id=1, source_target_pairs={{0,8},{8,16},{16,24},{24,32},{32,40},{40,48},{48,56},{56,64},{64,7... | collective-permute-start | bytes 1572872 | tf_op jit(solution)/shard_map/ppermute | solution.py:66
Sparse Core Ops, SparseCore 0:
  78.3 114.9 all-gather.1

commit v7 on v6

--- a/solution.py
+++ b/solution.py
@@ -75,7 +75,12 @@
         )
         spectra = (inner + edges).astype(jnp.bfloat16)
         spectra = spectra.reshape(2, n_tm, fl, cycles * sector * nb).transpose(1, 0, 2, 3)
-        shared = lax.all_to_all(spectra, "tm", 0, 0, tiled=True)
+        me = lax.axis_index("tm")
+        pieces = [lax.dynamic_index_in_dim(spectra, me, 0, keepdims=False)]
+        for s in range(1, n_tm):
+            piece = lax.dynamic_index_in_dim(spectra, (me + s) % n_tm, 0, keepdims=False)
+            pieces.append(lax.ppermute(piece, "tm", [(i, (i + s) % n_tm) for i in range(n_tm)]))
+        shared = jnp.stack(pieces, 0)
         x = shared.reshape(n_tm, 2, fl, cycles, sector, nb).transpose(2, 4, 3, 0, 1, 5)
         x = x.reshape(fl, local_rows, n_tm, 2, nb)
         rows = x.reshape(fl, local_rows, n_tm * 2 * nb)

time: 213 us -> 251 us (1.18)
  local copies, waits for them, and re-layouts: 39.1 us -> 79.3 us
  blocking collectives: 15.2 us -> 0 us
  starting transfers between devices: 3.12 us -> 13.2 us
    another operation x0 -> x10, local copies, waits for them, and re-layouts: none -> 39.2 us
    all_to_all x1 -> x0, blocking collectives: 15.2 us -> none  [shards(): shared = lax.all_to_all(spectra, 'tm', 0, 0, tiled=True)]
    ppermute x0 -> x7, starting transfers between devices: none -> 10.2 us  [shards(): lax.ppermute(piece, 'tm', [(i, (i + s) % n_tm) for i in range(n_tm)])]
    unnamed x11 -> x18, local copies, waits for them, and re-layouts: 1.21 us -> 7.04 us
    transpose x1 -> x0, local copies, waits for them, and re-layouts: 4.42 us -> none  [shards(): spectra.reshape(2, n_tm, fl, cycles * sector * nb).transpose(1, 0, 2, 3)]
    all_to_all x1 -> x0, local copies, waits for them, and re-layouts: 3.05 us -> none  [shards(): shared = lax.all_to_all(spectra, 'tm', 0, 0, tiled=True)]
    ppermute x0 -> x7, local copies, waits for them, and re-layouts: none -> 2.81 us  [shards(): lax.ppermute(piece, 'tm', [(i, (i + s) % n_tm) for i in range(n_tm)])]
  transfers between devices with their start and end apart: 3 -> 10, of which waited for: 1 -> 1; matrix products, arithmetic and copies ran while one was open for 11% -> 18% of each run, Pallas kernels for 0% -> 0%
where the time goes in v7:
time: 251 us; the launch traced here: 250 us
  waiting for transfers between devices  103 us (41%)
  local copies, waits for them, and re-layouts  79.3 us (32%)
  matrix products  27.1 us (11%)
  other arithmetic  13.6 us (5%)
  between operations  13.6 us (5%)
  starting transfers between devices  13.2 us (5%)
    all_gather x1, waiting for transfers between devices, shards(): columns = lax.all_gather(rows, 'az', axis=1, tiled=True)  103 us
    another operation x9, local copies, waits for them, and re-layouts  38.4 us
    dot_general x3, matrix products, transform(): lax.dot_general(table, rows, (((0,), (1,)), ((), ())), preferred_element_...  14.6 us
    dot_general x1, matrix products, shards(): jnp.einsum('fcqk,fpk->fcqp', lhs, columns, preferred_element_type=jnp.flo...  12.5 us
    ppermute x7, starting transfers between devices, shards(): lax.ppermute(piece, 'tm', [(i, (i + s) % n_tm) for i in range(n_tm)])  10.2 us
    another operation x2, local copies, waits for them, and re-layouts, shards(): lhs = jnp.stack([rows, turned], 1)  7.81 us
    unnamed x18, local copies, waits for them, and re-layouts  7.04 us
    transpose x1, local copies, waits for them, and re-layouts, shards(): shared.reshape(n_tm, 2, fl, cycles, sector, nb).transpose(2, 4, 3, 0, 1, 5)  5.34 us
  transfers between devices with their start and end apart: 10, of which 1 were waited for; matrix products, arithmetic and copies ran while one was open for 18% of the time, Pallas kernels for 0%

profile of v7, /device:TPU:1, one launch (start us, length us, event | category | flops | bytes accessed | tf_op | source)
XLA Modules:
  0.0 250.1 jit_solution(13492398511088268047)
XLA Ops:
  6.5 0.1 fusion.29
  6.6 0.1 subtract_multiply_fusion
  6.7 0.3 fusion.25
  7.0 0.3 fusion.27
  7.3 0.7 select_add_fusion.1
  8.0 0.1 broadcast_in_dim.26
  8.1 0.2 copy.56
  8.3 0.1 broadcast_in_dim.30
  8.4 0.2 copy.58
  8.6 3.2 %multiply_convert_fusion.1 = (bf16[16,1,16,4096]{3,2,1,0:T(8,128)(2,1)S(1)}, bf16[16,1,16,4096]{3,2,1,0:T(8,128)(2,1)S(1)}) fusion(bf16[16,4,16,4096]{3,2,1,0:T(8,128)(2,1)} %param.3, f32[16,4096]{1,0:T(8,128)S(1)} %bitcast.79, f32[16,4096]{1,0:T(8,128)S(1)} %bitcast.81), kind=kLoop, calls=%fused_computation.13 | loop fusion | flops 6291456 | bytes 8912896 | tf_op jit(solution)/shard_map/convert_element_type | solution.py:59
  11.8 1.2 multiply_subtract_fusion
  13.1 2.2 fusion.6
  15.2 2.2 fusion.12
  17.4 1.4 collective-permute-start.1
  18.8 2.1 fusion.13
  20.9 1.6 collective-permute-start
  22.5 5.1 %fusion.35 = (bf16[16,3,16,4096]{3,2,1,0:T(8,128)(2,1)}, bf16[16,3,16,4096]{3,2,1,0:T(8,128)(2,1)}) fusion(bf16[16,4,16,4096]{3,2,1,0:T(8,128)(2,1)S(1)} %bitcast.66), kind=kLoop, calls=%fused_computation.73 | loop fusion | bytes 25165824 | tf_op jit(solution)/shard_map/slice | solution.py:69
  27.6 0.1 broadcast_in_dim.28
  27.7 0.9 copy.57
  28.6 0.1 pad.7.clone
  28.7 1.1 copy.29
  29.7 2.0 copy.28
  31.8 10.3 %fusion.8 = bf16[512,16,4,16]{0,3,2,1:T(8,128)(2,1)S(1)} fusion(f32[512,16,1,16]{0,3,2,1:T(8,128)} %bitcast.86, f32[512,16,1,16]{0,3,2,1:T(8,128)} %bitcast.87, bf16[16,4,16,4096]{3,2,1,0:T(8,128)(2,1)} %param.3, bf16[16,3,16,4096]{3,2,1,0:T(8,128)(2,1)} %get-tuple-element.14, f32[16,4096]{1,0:T(8,128)} %bitcast.82, f32[16,4096]{1,0:T(8,128)} %bitcast.92, ...), kind=kOutput, calls=%fused_computation.18 | convolution fusion | flops 4343201792 | bytes 28049424 | tf_op jit(solution)/shard_map/dot_general | solution.py:60
  42.1 3.7 %reshape.334 = bf16[2,8,32,1024]{2,1,0,3:T(8,128)(2,1)} reshape(bf16[512,16,4,16]{0,3,2,1:T(8,128)(2,1)S(1)} %fusion.8) | data formatting | bytes 2097152 | tf_op jit(solution)/shard_map/reshape | solution.py:77
  45.9 21.6 %constant_dynamic-slice_fusion = (bf16[2,1,32,1024]{2,1,0,3:T(2,128)(2,1)}, bf16[2,1,32,1024]{2,1,0,3:T(2,128)(2,1)}, bf16[2,1,32,1024]{2,1,0,3:T(2,128)(2,1)}, ...) fusion(bf16[2,8,32,1024]{2,1,0,3:T(8,128)(2,1)} %reshape.334, ...), kind=kLoop, calls=%fused_computation.58 | loop fusion | bytes 2097184 | tf_op jit(solution)/shard_map/dynamic-slice.7
  67.4 3.4 %copy.31 = bf16[2,1,32,1024]{3,2,0,1:T(8,128)(2,1)} copy(bf16[2,1,32,1024]{2,1,0,3:T(2,128)(2,1)} %get-tuple-element.25) | data formatting | bytes 262144 | tf_op jit(solution)/shard_map/dynamic-slice.1
  70.8 1.3 collective-permute-start.2
  72.1 2.2 copy.43
  74.3 2.2 copy.41
  76.6 2.2 copy.39
  78.8 3.4 %copy.37 = bf16[2,1,32,1024]{3,2,0,1:T(8,128)(2,1)} copy(bf16[2,1,32,1024]{2,1,0,3:T(2,128)(2,1)} %get-tuple-element.22) | data formatting | bytes 262144 | tf_op jit(solution)/shard_map/dynamic-slice.4
  82.2 2.1 copy.35
  84.3 1.2 copy.33
  85.5 2.7 %collective-permute-start.3 = (bf16[2,32,1024]{2,1,0:T(8,128)(2,1)S(1)}, bf16[2,32,1024]{2,1,0:T(8,128)(2,1)S(1)}, u32[]{:S(2)}, u32[]{:S(2)}) collective-permute-start(bf16[2,32,1024]{2,1,0:T(8,128)(2,1)S(1)} %bitcast.98), channel_id=1, source_target_pairs={{0,2},{1,3},{2,4},{3,5},{4,6},{5,7},{6,0},{7,1},{8,10},{9,11},{10,... | collective-permute-start | bytes 393224 | tf_op jit(solution)/shard_map/ppermute | solution.py:82
  88.2 2.0 collective-permute-start.4
  90.2 0.3 collective-permute-start.5
  90.4 1.3 collective-permute-start.6
  91.7 0.1 copy.30
  91.8 0.8 constant_dynamic-update-slice_fusion.7
  92.7 1.3 collective-permute-start.7
  93.9 1.2 copy.32
  95.1 0.8 constant_dynamic-update-slice_fusion.6
  96.0 1.4 collective-permute-start.8
  97.3 0.3 copy.34
  97.6 0.8 constant_dynamic-update-slice_fusion.5
  98.4 0.3 copy.36
  98.7 0.8 constant_dynamic-update-slice_fusion.4
  99.6 0.3 copy.38
  99.8 0.8 constant_dynamic-update-slice_fusion.3
  100.7 0.3 copy.40
  101.0 0.8 constant_dynamic-update-slice_fusion.2
  101.8 0.3 copy.42
  102.1 0.8 constant_dynamic-update-slice_fusion.1
  102.9 0.3 copy.44
  103.2 0.8 constant_dynamic-update-slice_fusion
  104.0 5.3 %copy.45 = bf16[32,4,16,8,2,16]{0,5,4,3,2,1:T(8,128)(2,1)} copy(bf16[32,4,16,8,2,16]{0,5,1,2,4,3:T(8,128)(2,1)} %bitcast.68) | data formatting | bytes 2097152 | tf_op jit(solution)/shard_map/transpose | solution.py:84
  109.4 4.8 %copy.51 = bf16[32,64,256]{2,1,0:T(8,128)(2,1)} copy(bf16[32,64,256]{0,2,1:T(8,128)(2,1)} %bitcast.62) | data formatting | bytes 2097152 | tf_op jit(solution)/shard_map/reshape;reshape | solution.py:86
  114.2 0.0 all-gather.2.cloned.1.call-update
  114.2 3.9 %copy.48 = bf16[32,1,64,256]{3,2,1,0:T(8,128)(2,1)S(1)} copy(bf16[32,1,64,256]{0,3,2,1:T(8,128)(2,1)} %bitcast.63) | data formatting | bytes 2097152 | tf_op jit(solution)/shard_map/stack;reshape;reshape | solution.py:88
  118.1 2.6 %fusion.36 = (bf16[32,64,8,1,16]{0,4,3,2,1:T(8,128)(2,1)S(1)}, bf16[32,64,8,1,16]{0,4,3,2,1:T(8,128)(2,1)S(1)}) fusion(bf16[32,64,8,2,16]{0,4,3,2,1:T(8,128)(2,1)} %bitcast.64), kind=kLoop, calls=%fused_computation.74 | loop fusion | flops 262144 | bytes 2097152 | tf_op jit(solution)/shard_map/slice | solution.py:87
  120.8 2.8 %pad_maximum_fusion.1 = bf16[32,64,8,2,16]{0,4,3,2,1:T(8,128)(2,1)} fusion(bf16[32,64,8,1,16]{0,4,3,2,1:T(8,128)(2,1)S(1)} %get-tuple-element.18, bf16[32,64,8,1,16]{0,4,3,2,1:T(8,128)(2,1)S(1)} %get-tuple-element.17), kind=kLoop, calls=%fused_computation.6 | loop fusion | flops 524288 | bytes 2097152 | tf_op jit(solution)/shard_map/stack | solution.py:87
  123.6 3.9 %copy.49 = bf16[32,1,64,256]{3,2,1,0:T(8,128)(2,1)S(1)} copy(bf16[32,1,64,256]{0,3,2,1:T(8,128)(2,1)} %bitcast.67) | data formatting | bytes 2097152 | tf_op jit(solution)/shard_map/stack;reshape | solution.py:88
  127.5 103.2 %all-gather.2.cloned.1.call-done = bf16[32,1024,256]{2,1,0:T(8,128)(2,1)} async-done(((bf16[32,64,256]{2,1,0:T(8,128)(2,1)}), bf16[32,1024,256]{2,1,0:T(8,128)(2,1)}) %all-gather.2.cloned.1.call-update) | async-done | bytes 16777232 | tf_op jit(solution)/shard_map/all_gather | solution.py:89
  230.8 12.5 %broadcast_multiply_fusion = f32[32,2,64,1024]{3,2,1,0:T(8,128)} fusion(bf16[32,1024,256]{2,1,0:T(8,128)(2,1)} %all-gather.2.cloned.1.call-done, bf16[32,1,64,256]{3,2,1,0:T(8,128)(2,1)S(1)} %copy.49, bf16[32,1,64,256]{3,2,1,0:T(8,128)(2,1)S(1)} %copy.48), kind=kOutput, calls=%fused_computation.3 | convolution fusion | flops 2152726528 | bytes 35651584 | tf_op jit(solution)/shard_map/fcqk,fpk->fcqp/dot_general | solution.py:90
  (22 shorter events, 0.1 us)
Async XLA Ops:
  6.5 224.2 %all-gather.2.cloned.1.call-start = ((), (), s32[]{:S(2)}) async-start(), calls=%async_computation | async-start | bytes 17825792 | tf_op jit(solution)/shard_map/all_gather | solution.py:89
  8.6 3.3 %copy-start.1 = (f32[2,8,16,256]{3,1,2,0:T(8,128)}, f32[2,8,16,256]{3,1,2,0:T(8,128)S(1)}, u32[]{:S(2)}) copy-start(f32[2,8,16,256]{3,1,2,0:T(8,128)S(1)} %copy.58) | copy-start | bytes 786436
  15.2 3.6 %copy-start = (bf16[4096,256]{1,0:T(8,128)(2,1)}, bf16[4096,256]{1,0:T(8,128)(2,1)S(1)}, u32[]{:S(2)}) copy-start(bf16[4096,256]{1,0:T(8,128)(2,1)S(1)} %get-tuple-element.37) | copy-start | bytes 6291460
  15.2 7.3 %slice-start = ((s8[8388608]{0:T(1024)(128)(4,1)}), s8[4194304]{0:T(1024)(128)(4,1)S(1)}, s32[]{:S(2)}) async-start(s8[8388608]{0:T(1024)(128)(4,1)} %bitcast.65), calls=%async_computation.1 | async-start | bytes 8388608
  17.4 11.3 %collective-permute-start.1 = (f32[512,256]{1,0:T(8,128)}, f32[512,256]{1,0:T(8,128)S(1)}, u32[]{:S(2)}, u32[]{:S(2)}) collective-permute-start(f32[512,256]{1,0:T(8,128)} %fusion.12), channel_id=1, source_target_pairs={{8,0},{16,8},{24,16},{32,24},{40,32},{48,40},{56,48},{64,56},{72,6... | collective-permute-start | bytes 1572872 | tf_op jit(solution)/shard_map/ppermute | solution.py:67
  18.8 3.8 %slice-start.1 = ((s8[8388608]{0:T(1024)(128)(4,1)}), s8[4194304]{0:T(1024)(128)(4,1)S(1)}, s32[]{:S(2)}) async-start(s8[8388608]{0:T(1024)(128)(4,1)} %bitcast.65), calls=%async_computation.2 | async-start | bytes 8388608
  20.9 8.8 %collective-permute-start = (f32[512,256]{1,0:T(8,128)}, f32[512,256]{1,0:T(8,128)}, u32[]{:S(2)}, u32[]{:S(2)}) collective-permute-start(f32[512,256]{1,0:T(8,128)} %fusion.13), channel_id=1, source_target_pairs={{0,8},{8,16},{16,24},{24,32},{32,40},{40,48},{48,56},{56,64},{64,7... | collective-permute-start | bytes 1572872 | tf_op jit(solution)/shard_map/ppermute | solution.py:66
  70.8 21.9 %collective-permute-start.2 = (bf16[2,32,1024]{2,1,0:T(8,128)(2,1)}, bf16[2,32,1024]{2,1,0:T(8,128)(2,1)}, u32[]{:S(2)}, u32[]{:S(2)}) collective-permute-start(bf16[2,32,1024]{2,1,0:T(8,128)(2,1)} %bitcast.13), channel_id=1, source_target_pairs={{0,1},{1,2},{2,3},{3,4},{4,5},{5,6},{6,7},{7,0},{8,9},{9,10},{10,1... | collective-permute-start | bytes 393224 | tf_op jit(solution)/shard_map/ppermute | solution.py:82
  85.5 10.5 %collective-permute-start.3 = (bf16[2,32,1024]{2,1,0:T(8,128)(2,1)S(1)}, bf16[2,32,1024]{2,1,0:T(8,128)(2,1)S(1)}, u32[]{:S(2)}, u32[]{:S(2)}) collective-permute-start(bf16[2,32,1024]{2,1,0:T(8,128)(2,1)S(1)} %bitcast.98), channel_id=1, source_target_pairs={{0,2},{1,3},{2,4},{3,5},{4,6},{5,7},{6,0},{7,1},{8,10},{9,11},{10,... | collective-permute-start | bytes 393224 | tf_op jit(solution)/shard_map/ppermute | solution.py:82
  88.2 10.3 %collective-permute-start.4 = (bf16[2,32,1024]{2,1,0:T(8,128)(2,1)}, bf16[2,32,1024]{2,1,0:T(8,128)(2,1)S(1)}, u32[]{:S(2)}, u32[]{:S(2)}) collective-permute-start(bf16[2,32,1024]{2,1,0:T(8,128)(2,1)} %bitcast.97), channel_id=1, source_target_pairs={{0,3},{1,4},{2,5},{3,6},{4,7},{5,0},{6,1},{7,2},{8,11},{9,12},{10,... | collective-permute-start | bytes 393224 | tf_op jit(solution)/shard_map/ppermute | solution.py:82
  90.2 9.4 %collective-permute-start.5 = (bf16[2,32,1024]{2,1,0:T(8,128)(2,1)}, bf16[2,32,1024]{2,1,0:T(8,128)(2,1)S(1)}, u32[]{:S(2)}, u32[]{:S(2)}) collective-permute-start(bf16[2,32,1024]{2,1,0:T(8,128)(2,1)} %bitcast.96), channel_id=1, source_target_pairs={{0,4},{1,5},{2,6},{3,7},{4,0},{5,1},{6,2},{7,3},{8,12},{9,13},{10,... | collective-permute-start | bytes 393224 | tf_op jit(solution)/shard_map/ppermute | solution.py:82
  90.4 10.2 %collective-permute-start.6 = (bf16[2,32,1024]{2,1,0:T(8,128)(2,1)S(1)}, bf16[2,32,1024]{2,1,0:T(8,128)(2,1)S(1)}, u32[]{:S(2)}, u32[]{:S(2)}) collective-permute-start(bf16[2,32,1024]{2,1,0:T(8,128)(2,1)S(1)} %bitcast.95), channel_id=1, source_target_pairs={{0,5},{1,6},{2,7},{3,0},{4,1},{5,2},{6,3},{7,4},{8,13},{9,14},{10,... | collective-permute-start | bytes 393224 | tf_op jit(solution)/shard_map/ppermute | solution.py:82
  92.7 9.1 %collective-permute-start.7 = (bf16[2,32,1024]{2,1,0:T(8,128)(2,1)S(1)}, bf16[2,32,1024]{2,1,0:T(8,128)(2,1)S(1)}, u32[]{:S(2)}, u32[]{:S(2)}) collective-permute-start(bf16[2,32,1024]{2,1,0:T(8,128)(2,1)S(1)} %bitcast.94), channel_id=1, source_target_pairs={{0,6},{1,7},{2,0},{3,1},{4,2},{5,3},{6,4},{7,5},{8,14},{9,15},{10,... | collective-permute-start | bytes 393224 | tf_op jit(solution)/shard_map/ppermute | solution.py:82
  96.0 7.0 %collective-permute-start.8 = (bf16[2,32,1024]{2,1,0:T(8,128)(2,1)S(1)}, bf16[2,32,1024]{2,1,0:T(8,128)(2,1)S(1)}, u32[]{:S(2)}, u32[]{:S(2)}) collective-permute-start(bf16[2,32,1024]{2,1,0:T(8,128)(2,1)S(1)} %bitcast.93), channel_id=1, source_target_pairs={{0,7},{1,0},{2,1},{3,2},{4,3},{5,4},{6,5},{7,6},{8,15},{9,8},{10,9... | collective-permute-start | bytes 393224 | tf_op jit(solution)/shard_map/ppermute | solution.py:82
Sparse Core Ops, SparseCore 0:
  114.4 116.3 all-gather.1

commit v8 on v6

--- a/solution.py
+++ b/solution.py
@@ -69,11 +69,11 @@
         prev = jnp.concatenate([zero, block[:, :-1]], axis=1).astype(jnp.float32)
         nxt = jnp.concatenate([block[:, 1:], zero], axis=1).astype(jnp.float32)
         total = weights[0] * prev + weights[1] * block.astype(jnp.float32) + weights[2] * nxt
-        inner = transform(total).reshape(2 * FREQS, cycles, sector, nb)
+        inner = lax.optimization_barrier(transform(total))
         edges = jnp.concatenate(
             [from_prev, jnp.zeros((2 * FREQS, cycles, sector - 2, nb), jnp.float32), from_next], axis=2
         )
-        spectra = (inner + edges).astype(jnp.bfloat16)
+        spectra = (inner + edges.reshape(inner.shape)).astype(jnp.bfloat16)
         spectra = spectra.reshape(2, n_tm, fl, cycles * sector * nb).transpose(1, 0, 2, 3)
         shared = lax.all_to_all(spectra, "tm", 0, 0, tiled=True)
         x = shared.reshape(n_tm, 2, fl, cycles, sector, nb).transpose(2, 4, 3, 0, 1, 5)

time: 213 us -> 205 us (0.962)
  local copies, waits for them, and re-layouts: 39.1 us -> 26.8 us
  other arithmetic: 13.6 us -> 21.9 us
  matrix products: 26.3 us -> 22.5 us
    convert_element_type x1 -> x2, other arithmetic: 3.23 us -> 8.68 us  [transform(): rows = v.astype(jnp.bfloat16).reshape(-1, length)]
    transpose x1 -> x0, local copies, waits for them, and re-layouts: 4.42 us -> none  [shards(): spectra.reshape(2, n_tm, fl, cycles * sector * nb).transpose(1, 0, 2, 3)]
    dot_general x3, matrix products: 13.8 us -> 10.1 us  [transform(): lax.dot_general(table, rows, (((0,), (1,)), ((), ())), preferred_element_...]
    slice x1, local copies, waits for them, and re-layouts: 5.18 us -> 1.5 us  [shards(): prev = jnp.concatenate([zero, block[:, :-1]], axis=1).astype(jnp.float32)]
    reshape x1, local copies, waits for them, and re-layouts: 3.73 us -> 0.07 us  [shards(): spectra.reshape(2, n_tm, fl, cycles * sector * nb).transpose(1, 0, 2, 3)]
    convert_element_type x0 -> x1, other arithmetic: none -> 2.54 us  [shards(): spectra = (inner + edges.reshape(inner.shape)).astype(jnp.bfloat16)]
  transfers between devices with their start and end apart: 3 -> 3, of which waited for: 1 -> 1; matrix products, arithmetic and copies ran while one was open for 11% -> 14% of each run, Pallas kernels for 0% -> 0%
where the time goes in v8:
time: 205 us; the launch traced here: 204 us
  waiting for transfers between devices  100 us (49%)
  local copies, waits for them, and re-layouts  26.8 us (13%)
  matrix products  22.5 us (11%)
  other arithmetic  21.9 us (11%)
  blocking collectives  16.2 us (8%)
  between operations  13.6 us (7%)
  starting transfers between devices  3.02 us (1%)
    all_gather x1, waiting for transfers between devices, shards(): columns = lax.all_gather(rows, 'az', axis=1, tiled=True)  100 us
    all_to_all x1, blocking collectives, shards(): shared = lax.all_to_all(spectra, 'tm', 0, 0, tiled=True)  16.2 us
    dot_general x1, matrix products, shards(): jnp.einsum('fcqk,fpk->fcqp', lhs, columns, preferred_element_type=jnp.flo...  12.5 us
    dot_general x3, matrix products, transform(): lax.dot_general(table, rows, (((0,), (1,)), ((), ())), preferred_element_...  10.1 us
    convert_element_type x2, other arithmetic, transform(): rows = v.astype(jnp.bfloat16).reshape(-1, length)  8.68 us
    another operation x2, local copies, waits for them, and re-layouts, shards(): lhs = jnp.stack([rows, turned], 1)  7.81 us
    transpose x1, local copies, waits for them, and re-layouts, shards(): shared.reshape(n_tm, 2, fl, cycles, sector, nb).transpose(2, 4, 3, 0, 1, 5)  5.37 us
    another operation x1, local copies, waits for them, and re-layouts, shards(): rows = x.reshape(fl, local_rows, n_tm * 2 * nb)  4.86 us
  transfers between devices with their start and end apart: 3, of which 1 were waited for; matrix products, arithmetic and copies ran while one was open for 14% of the time, Pallas kernels for 0%

profile of v8, /device:TPU:1, one launch (start us, length us, event | category | flops | bytes accessed | tf_op | source)
XLA Modules:
  0.0 204.2 jit_solution(967209556386822124)
XLA Ops:
  6.5 0.0 all-gather.2.cloned.1.call-start
  6.5 0.1 fusion.25
  6.6 0.1 subtract_multiply_fusion
  6.7 0.3 fusion.21
  7.0 0.3 fusion.23
  7.3 0.7 select_add_fusion.2
  8.0 0.1 broadcast_in_dim.26
  8.1 0.2 copy.48
  8.3 0.1 broadcast_in_dim.30
  8.4 0.2 copy.50
  8.6 3.1 %multiply_convert_fusion.1 = (bf16[16,1,16,4096]{3,2,1,0:T(8,128)(2,1)S(1)}, bf16[16,1,16,4096]{3,2,1,0:T(8,128)(2,1)S(1)}) fusion(bf16[16,4,16,4096]{3,2,1,0:T(8,128)(2,1)} %param.3, f32[16,4096]{1,0:T(8,128)S(1)} %bitcast.60, f32[16,4096]{1,0:T(8,128)S(1)} %bitcast.62), kind=kLoop, calls=%fused_computation.11 | loop fusion | flops 6291456 | bytes 8912896 | tf_op jit(solution)/shard_map/convert_element_type | solution.py:59
  11.7 1.2 multiply_subtract_fusion
  12.9 2.2 %fusion.4 = (bf16[4096,256]{1,0:T(8,128)(2,1)S(1)}, bf16[4096,256]{1,0:T(8,128)(2,1)S(1)}) fusion(f32[64,64,256]{2,1,0:T(8,128)S(1)} %get-tuple-element.20, f32[4096]{0:T(1024)S(1)} %fusion.25, f32[64,64,256]{2,1,0:T(8,128)S(1)} %get-tuple-element.19, f32[4096]{0:T(1024)S(1)} %subtract_multiply_fusion), kind=kLoop, calls=%fused_computation.7 | loop fusion | flops 4194304 | bytes 12615680 | tf_op jit(solution)/shard_map/convert.1
  15.1 0.0 slice-start
  15.1 2.1 %fusion.9 = f32[512,256]{1,0:T(8,128)} fusion(bf16[256,4096]{1,0:T(8,128)(2,1)S(1)} %bitcast.65, bf16[4096,256]{1,0:T(8,128)(2,1)S(1)} %get-tuple-element.28, bf16[4096,256]{1,0:T(8,128)(2,1)S(1)} %get-tuple-element.29), kind=kOutput, calls=%fused_computation.20 | convolution fusion | flops 1082130432 | bytes 6815744 | tf_op jit(solution)/shard_map/dot_general | solution.py:60
  17.2 1.4 collective-permute-start.1
  18.6 0.0 slice-start.1
  18.6 2.1 %fusion.10 = f32[512,256]{1,0:T(8,128)} fusion(bf16[256,4096]{1,0:T(8,128)(2,1)S(1)} %bitcast.64, bf16[4096,256]{1,0:T(8,128)(2,1)S(1)} %get-tuple-element.28, bf16[4096,256]{1,0:T(8,128)(2,1)S(1)} %get-tuple-element.29), kind=kOutput, calls=%fused_computation.21 | convolution fusion | flops 1082130432 | bytes 6815744 | tf_op jit(solution)/shard_map/dot_general | solution.py:60
  20.7 1.6 collective-permute-start
  22.4 0.0 slice-done
  22.4 0.0 slice-done.1
  22.4 1.5 fusion.30
  23.9 0.1 broadcast_in_dim.28
  24.0 0.2 copy.49
  24.1 5.5 %add_convert_fusion = bf16[16,4,16,4096]{3,2,1,0:T(8,128)(2,1)S(1)} fusion(bf16[16,4,16,4096]{3,2,1,0:T(8,128)(2,1)S(1)} %bitcast.50, bf16[16,3,16,4096]{3,2,1,0:T(8,128)(2,1)S(1)} %get-tuple-element.16, f32[16,4096]{1,0:T(8,128)S(1)} %bitcast.63, f32[16,4096]{1,0:T(8,128)S(1)} %bitcast.68, bf16[16,3,16,4096]{3,2,1,0:T(8,128)(2,1)S(1)} %get-tuple-element.15, ...), kind=kLoop, calls=%fused_computation.2 | loop fusion | flops 37748736 | bytes 30146560 | tf_op jit(solution)/shard_map/convert_element_type | solution.py:59
  29.7 5.9 %fusion.11 = f32[512,1024]{1,0:T(8,128)} fusion(bf16[1024,4096]{1,0:T(8,128)(2,1)S(1)} %bitcast.56, bf16[4096,256]{1,0:T(8,128)(2,1)S(1)} %get-tuple-element.28, bf16[4096,256]{1,0:T(8,128)(2,1)S(1)} %get-tuple-element.29), kind=kOutput, calls=%fused_computation.22 | convolution fusion | flops 4303355904 | bytes 14680064 | tf_op jit(solution)/shard_map/dot_general | solution.py:60
  35.6 0.1 pad.7.clone
  35.6 0.0 collective-permute-done.1
  35.6 0.2 copy.32
  35.8 0.0 collective-permute-done
  35.9 1.2 copy.31
  37.1 0.3 pad_maximum_fusion.2
  37.4 1.8 copy.35
  39.3 2.5 %add_convert_fusion.1 = bf16[512,1024]{1,0:T(8,128)(2,1)S(1)} fusion(f32[512,1024]{1,0:T(8,128)} %fusion.11, f32[512,1024]{1,0:T(8,128)} %copy.35), kind=kLoop, calls=%fused_computation.19 | loop fusion | flops 1048576 | bytes 5242880 | tf_op jit(solution)/shard_map/convert_element_type | solution.py:76
  41.8 0.1 copy.52
  41.9 16.2 %all_to_all.5 = bf16[8,2,32,1024]{3,2,1,0:T(8,128)(2,1)S(1)} all-to-all(bf16[8,2,32,1024]{3,2,1,0:T(8,128)(2,1)S(1)} %bitcast.59), channel_id=1, replica_groups=mesh['az'=16,'tm'=8] {'tm'}, dimensions={0} | all-to-all | bytes 2097152 | tf_op jit(solution)/shard_map/all_to_all | solution.py:78
  58.1 3.1 %copy.37 = bf16[8,2,32,1024]{2,3,1,0:T(8,128)(2,1)} copy(bf16[8,2,32,1024]{3,2,1,0:T(8,128)(2,1)S(1)} %all_to_all.5) | data formatting | bytes 2097152 | tf_op jit(solution)/shard_map/all_to_all | solution.py:78
  61.2 5.4 %copy.38 = bf16[32,4,16,8,2,16]{0,5,4,3,2,1:T(8,128)(2,1)} copy(bf16[32,4,16,8,2,16]{0,5,1,2,4,3:T(8,128)(2,1)} %bitcast.55) | data formatting | bytes 2097152 | tf_op jit(solution)/shard_map/transpose | solution.py:79
  66.5 4.9 %copy.44 = bf16[32,64,256]{2,1,0:T(8,128)(2,1)} copy(bf16[32,64,256]{0,2,1:T(8,128)(2,1)} %bitcast.51) | data formatting | bytes 2097152 | tf_op jit(solution)/shard_map/reshape;reshape | solution.py:81
  71.4 0.0 all-gather.2.cloned.1.call-update
  71.4 3.9 %copy.41 = bf16[32,1,64,256]{3,2,1,0:T(8,128)(2,1)S(1)} copy(bf16[32,1,64,256]{0,3,2,1:T(8,128)(2,1)} %bitcast.52) | data formatting | bytes 2097152 | tf_op jit(solution)/shard_map/stack;reshape;reshape | solution.py:83
  75.3 2.6 %fusion.31 = (bf16[32,64,8,1,16]{0,4,3,2,1:T(8,128)(2,1)S(1)}, bf16[32,64,8,1,16]{0,4,3,2,1:T(8,128)(2,1)S(1)}) fusion(bf16[32,64,8,2,16]{0,4,3,2,1:T(8,128)(2,1)} %bitcast.53), kind=kLoop, calls=%fused_computation.57 | loop fusion | flops 262144 | bytes 2097152 | tf_op jit(solution)/shard_map/slice | solution.py:82
  78.0 2.8 %pad_maximum_fusion.1 = bf16[32,64,8,2,16]{0,4,3,2,1:T(8,128)(2,1)} fusion(bf16[32,64,8,1,16]{0,4,3,2,1:T(8,128)(2,1)S(1)} %get-tuple-element.18, bf16[32,64,8,1,16]{0,4,3,2,1:T(8,128)(2,1)S(1)} %get-tuple-element.17), kind=kLoop, calls=%fused_computation.5 | loop fusion | flops 524288 | bytes 2097152 | tf_op jit(solution)/shard_map/stack | solution.py:82
  80.8 3.9 %copy.42 = bf16[32,1,64,256]{3,2,1,0:T(8,128)(2,1)S(1)} copy(bf16[32,1,64,256]{0,3,2,1:T(8,128)(2,1)} %bitcast.54) | data formatting | bytes 2097152 | tf_op jit(solution)/shard_map/stack;reshape | solution.py:83
  84.7 100.2 %all-gather.2.cloned.1.call-done = bf16[32,1024,256]{2,1,0:T(8,128)(2,1)} async-done(((bf16[32,64,256]{2,1,0:T(8,128)(2,1)}), bf16[32,1024,256]{2,1,0:T(8,128)(2,1)}) %all-gather.2.cloned.1.call-update) | async-done | bytes 16777232 | tf_op jit(solution)/shard_map/all_gather | solution.py:84
  184.9 12.5 %broadcast_multiply_fusion = f32[32,2,64,1024]{3,2,1,0:T(8,128)} fusion(bf16[32,1024,256]{2,1,0:T(8,128)(2,1)} %all-gather.2.cloned.1.call-done, bf16[32,1,64,256]{3,2,1,0:T(8,128)(2,1)S(1)} %copy.42, bf16[32,1,64,256]{3,2,1,0:T(8,128)(2,1)S(1)} %copy.41), kind=kOutput, calls=%fused_computation.3 | convolution fusion | flops 2152726528 | bytes 35651584 | tf_op jit(solution)/shard_map/fcqk,fpk->fcqp/dot_general | solution.py:85
  (4 shorter events, 0.0 us)
Async XLA Ops:
  6.5 178.4 %all-gather.2.cloned.1.call-start = ((), (), s32[]{:S(2)}) async-start(), calls=%async_computation.1 | async-start | bytes 17825792 | tf_op jit(solution)/shard_map/all_gather | solution.py:84
  15.1 7.2 %slice-start = ((s8[8388608]{0:T(1024)(128)(4,1)}), s8[4194304]{0:T(1024)(128)(4,1)S(1)}, s32[]{:S(2)}) async-start(s8[8388608]{0:T(1024)(128)(4,1)} %bitcast.49), calls=%async_computation.2 | async-start | bytes 8388608
  17.2 18.4 %collective-permute-start.1 = (f32[512,256]{1,0:T(8,128)}, f32[512,256]{1,0:T(8,128)S(1)}, u32[]{:S(2)}, u32[]{:S(2)}) collective-permute-start(f32[512,256]{1,0:T(8,128)} %fusion.9), channel_id=1, source_target_pairs={{8,0},{16,8},{24,16},{32,24},{40,32},{48,40},{56,48},{64,56},{72,6... | collective-permute-start | bytes 1572872 | tf_op jit(solution)/shard_map/ppermute | solution.py:67
  18.6 3.7 %slice-start.1 = ((s8[8388608]{0:T(1024)(128)(4,1)}), s8[4194304]{0:T(1024)(128)(4,1)S(1)}, s32[]{:S(2)}) async-start(s8[8388608]{0:T(1024)(128)(4,1)} %bitcast.49), calls=%async_computation.3 | async-start | bytes 8388608
  20.7 15.1 %collective-permute-start = (f32[512,256]{1,0:T(8,128)}, f32[512,256]{1,0:T(8,128)}, u32[]{:S(2)}, u32[]{:S(2)}) collective-permute-start(f32[512,256]{1,0:T(8,128)} %fusion.10), channel_id=1, source_target_pairs={{0,8},{8,16},{16,24},{24,32},{32,40},{40,48},{48,56},{56,64},{64,7... | collective-permute-start | bytes 1572872 | tf_op jit(solution)/shard_map/ppermute | solution.py:66
Sparse Core Ops, SparseCore 0:
  71.6 113.3 all-gather.1

commit v9 on v8

--- a/solution.py
+++ b/solution.py
@@ -63,20 +63,20 @@
 
         to_next = transform(weights[0] * block[:, sector - 1 :].astype(jnp.float32))
         to_prev = transform(weights[2] * block[:, :1].astype(jnp.float32))
-        from_prev = lax.ppermute(to_next, "az", forward).reshape(2 * FREQS, cycles, 1, nb)
-        from_next = lax.ppermute(to_prev, "az", backward).reshape(2 * FREQS, cycles, 1, nb)
+        from_prev = lax.ppermute(to_next, "az", forward).reshape(2 * FREQS, 1, cycles, nb)
+        from_next = lax.ppermute(to_prev, "az", backward).reshape(2 * FREQS, 1, cycles, nb)
         zero = jnp.zeros_like(block[:, :1])
         prev = jnp.concatenate([zero, block[:, :-1]], axis=1).astype(jnp.float32)
         nxt = jnp.concatenate([block[:, 1:], zero], axis=1).astype(jnp.float32)
         total = weights[0] * prev + weights[1] * block.astype(jnp.float32) + weights[2] * nxt
-        inner = lax.optimization_barrier(transform(total))
+        inner = lax.optimization_barrier(transform(total.transpose(1, 0, 2, 3)))
         edges = jnp.concatenate(
-            [from_prev, jnp.zeros((2 * FREQS, cycles, sector - 2, nb), jnp.float32), from_next], axis=2
+            [from_prev, jnp.zeros((2 * FREQS, sector - 2, cycles, nb), jnp.float32), from_next], axis=1
         )
         spectra = (inner + edges.reshape(inner.shape)).astype(jnp.bfloat16)
         spectra = spectra.reshape(2, n_tm, fl, cycles * sector * nb).transpose(1, 0, 2, 3)
         shared = lax.all_to_all(spectra, "tm", 0, 0, tiled=True)
-        x = shared.reshape(n_tm, 2, fl, cycles, sector, nb).transpose(2, 4, 3, 0, 1, 5)
+        x = shared.reshape(n_tm, 2, fl, local_rows, nb).transpose(2, 3, 0, 1, 4)
         x = x.reshape(fl, local_rows, n_tm, 2, nb)
         rows = x.reshape(fl, local_rows, n_tm * 2 * nb)
         turned = jnp.stack([x[:, :, :, 1], -x[:, :, :, 0]], 3).reshape(rows.shape)

time: 205 us -> 203 us (level)
  waiting for transfers between devices: 100 us -> 96.8 us
    another operation x2, local copies, waits for them, and re-layouts: 7.81 us -> 3.73 us  [shards(): lhs = jnp.stack([rows, turned], 1)]
    all_gather x1, waiting for transfers between devices: 100 us -> 96.8 us  [shards(): columns = lax.all_gather(rows, 'az', axis=1, tiled=True)]
    another operation x1, local copies, waits for them, and re-layouts: 4.86 us -> 7.37 us  [shards(): turned = jnp.stack([x[:, :, :, 1], -x[:, :, :, 0]], 3).reshape(rows.shape)]
  transfers between devices with their start and end apart: 3 -> 3, of which waited for: 1 -> 1; matrix products, arithmetic and copies ran while one was open for 14% -> 16% of each run, Pallas kernels for 0% -> 0%
where the time goes in v9:
time: 203 us
  waiting for transfers between devices  96.8 us (48%)
  local copies, waits for them, and re-layouts  28.1 us (14%)
  matrix products  23 us (11%)
  other arithmetic  21.9 us (11%)
  blocking collectives  16.2 us (8%)
  between operations  13.6 us (7%)
  starting transfers between devices  3.02 us (1%)
    all_gather x1, waiting for transfers between devices, shards(): columns = lax.all_gather(rows, 'az', axis=1, tiled=True)  96.8 us
    all_to_all x1, blocking collectives, shards(): shared = lax.all_to_all(spectra, 'tm', 0, 0, tiled=True)  16.2 us
    dot_general x1, matrix products, shards(): jnp.einsum('fcqk,fpk->fcqp', lhs, columns, preferred_element_type=jnp.flo...  12.9 us
    dot_general x3, matrix products, transform(): lax.dot_general(table, rows, (((0,), (1,)), ((), ())), preferred_element_...  10.1 us
    convert_element_type x2, other arithmetic, transform(): rows = v.astype(jnp.bfloat16).reshape(-1, length)  8.66 us
    another operation x1, local copies, waits for them, and re-layouts, shards(): turned = jnp.stack([x[:, :, :, 1], -x[:, :, :, 0]], 3).reshape(rows.shape)  7.37 us
    transpose x1, local copies, waits for them, and re-layouts, shards(): x = shared.reshape(n_tm, 2, fl, local_rows, nb).transpose(2, 3, 0, 1, 4)  6.64 us
  transfers between devices with their start and end apart: 3, of which 1 were waited for; matrix products, arithmetic and copies ran while one was open for 16% of the time, Pallas kernels for 0%

profile of v9, /device:TPU:1, one launch (start us, length us, event | category | flops | bytes accessed | tf_op | source)
XLA Modules:
  0.0 202.7 jit_solution(3962775587895311738)
XLA Ops:
  6.5 0.0 all-gather.2.cloned.1.call-start
  6.5 0.1 fusion.25
  6.6 0.1 subtract_multiply_fusion
  6.7 0.3 fusion.21
  7.0 0.3 fusion.23
  7.3 0.7 select_add_fusion.2
  8.0 0.1 broadcast_in_dim.26
  8.1 0.2 copy.35
  8.3 0.1 broadcast_in_dim.30
  8.4 0.2 copy.37
  8.6 3.1 %multiply_convert_fusion.1 = (bf16[16,1,16,4096]{3,2,1,0:T(8,128)(2,1)S(1)}, bf16[16,1,16,4096]{3,2,1,0:T(8,128)(2,1)S(1)}) fusion(bf16[16,4,16,4096]{3,2,1,0:T(8,128)(2,1)} %param.3, f32[16,4096]{1,0:T(8,128)S(1)} %bitcast.57, f32[16,4096]{1,0:T(8,128)S(1)} %bitcast.59), kind=kLoop, calls=%fused_computation.11 | loop fusion | flops 6291456 | bytes 8912896 | tf_op jit(solution)/shard_map/convert_element_type | solution.py:59
  11.7 1.2 multiply_subtract_fusion
  12.9 2.2 %fusion.4 = (bf16[4096,256]{1,0:T(8,128)(2,1)S(1)}, bf16[4096,256]{1,0:T(8,128)(2,1)S(1)}) fusion(f32[64,64,256]{2,1,0:T(8,128)S(1)} %get-tuple-element.20, f32[4096]{0:T(1024)S(1)} %fusion.25, f32[64,64,256]{2,1,0:T(8,128)S(1)} %get-tuple-element.19, f32[4096]{0:T(1024)S(1)} %subtract_multiply_fusion), kind=kLoop, calls=%fused_computation.7 | loop fusion | flops 4194304 | bytes 12615680 | tf_op jit(solution)/shard_map/convert.1
  15.1 0.0 slice-start
  15.1 2.1 %fusion.9 = f32[512,256]{1,0:T(8,128)} fusion(bf16[256,4096]{1,0:T(8,128)(2,1)S(1)} %bitcast.62, bf16[4096,256]{1,0:T(8,128)(2,1)S(1)} %get-tuple-element.28, bf16[4096,256]{1,0:T(8,128)(2,1)S(1)} %get-tuple-element.29), kind=kOutput, calls=%fused_computation.20 | convolution fusion | flops 1082130432 | bytes 6815744 | tf_op jit(solution)/shard_map/dot_general | solution.py:60
  17.2 1.4 collective-permute-start.1
  18.6 0.0 slice-start.1
  18.6 2.1 %fusion.10 = f32[512,256]{1,0:T(8,128)} fusion(bf16[256,4096]{1,0:T(8,128)(2,1)S(1)} %bitcast.61, bf16[4096,256]{1,0:T(8,128)(2,1)S(1)} %get-tuple-element.28, bf16[4096,256]{1,0:T(8,128)(2,1)S(1)} %get-tuple-element.29), kind=kOutput, calls=%fused_computation.21 | convolution fusion | flops 1082130432 | bytes 6815744 | tf_op jit(solution)/shard_map/dot_general | solution.py:60
  20.7 1.6 collective-permute-start
  22.4 0.0 slice-done
  22.4 0.0 slice-done.1
  22.4 1.5 fusion.30
  23.9 0.1 broadcast_in_dim.28
  24.0 0.2 copy.36
  24.1 5.5 %add_convert_fusion = bf16[16,4,16,4096]{3,2,0,1:T(8,128)(2,1)S(1)} fusion(f32[16,4096]{1,0:T(8,128)S(1)} %bitcast.60, f32[16,4096]{1,0:T(8,128)S(1)} %bitcast.65, f32[16,4096]{1,0:T(8,128)S(1)} %bitcast.58, bf16[16,4,16,4096]{3,2,1,0:T(8,128)(2,1)S(1)} %bitcast.47, bf16[16,3,16,4096]{3,2,1,0:T(8,128)(2,1)S(1)} %get-tuple-element.15, ...), kind=kLoop, calls=%fused_computation.2 | loop fusion | flops 37748736 | bytes 30146560 | tf_op jit(solution)/shard_map/convert_element_type | solution.py:59
  29.7 5.9 %fusion.11 = f32[512,1024]{1,0:T(8,128)} fusion(bf16[1024,4096]{1,0:T(8,128)(2,1)S(1)} %bitcast.52, bf16[4096,256]{1,0:T(8,128)(2,1)S(1)} %get-tuple-element.28, bf16[4096,256]{1,0:T(8,128)(2,1)S(1)} %get-tuple-element.29), kind=kOutput, calls=%fused_computation.22 | convolution fusion | flops 4303355904 | bytes 14680064 | tf_op jit(solution)/shard_map/dot_general | solution.py:60
  35.5 0.1 pad.7.clone
  35.6 0.0 collective-permute-done.1
  35.6 0.2 copy.24
  35.8 0.0 collective-permute-done
  35.8 1.2 copy.23
  37.1 0.3 pad_maximum_fusion.2
  37.4 1.8 copy.25
  39.2 2.5 %add_convert_fusion.1 = bf16[512,1024]{1,0:T(8,128)(2,1)S(1)} fusion(f32[512,1024]{1,0:T(8,128)} %fusion.11, f32[512,1024]{1,0:T(8,128)} %copy.25), kind=kLoop, calls=%fused_computation.19 | loop fusion | flops 1048576 | bytes 5242880 | tf_op jit(solution)/shard_map/convert_element_type | solution.py:76
  41.8 0.1 copy.46
  41.9 16.2 %all_to_all.5 = bf16[8,2,32,1024]{3,2,1,0:T(8,128)(2,1)S(1)} all-to-all(bf16[8,2,32,1024]{3,2,1,0:T(8,128)(2,1)S(1)} %bitcast.56), channel_id=1, replica_groups=mesh['az'=16,'tm'=8] {'tm'}, dimensions={0} | all-to-all | bytes 2097152 | tf_op jit(solution)/shard_map/all_to_all | solution.py:78
  58.1 3.1 %copy.27 = bf16[8,2,32,1024]{2,3,1,0:T(8,128)(2,1)} copy(bf16[8,2,32,1024]{3,2,1,0:T(8,128)(2,1)S(1)} %all_to_all.5) | data formatting | bytes 2097152 | tf_op jit(solution)/shard_map/all_to_all | solution.py:78
  61.1 6.6 %copy.28 = bf16[32,64,8,2,16]{1,4,3,2,0:T(8,128)(2,1)S(1)} copy(bf16[32,64,8,2,16]{0,4,1,3,2:T(8,128)(2,1)} %bitcast.48) | data formatting | bytes 2097152 | tf_op jit(solution)/shard_map/transpose | solution.py:79
  67.8 1.6 copy.33
  69.4 0.0 all-gather.2.cloned.1.call-update
  69.4 2.6 %fusion.31 = (bf16[32,64,8,1,16]{0,4,1,3,2:T(8,128)(2,1)S(1)}, bf16[32,64,8,1,16]{0,4,1,3,2:T(8,128)(2,1)S(1)}) fusion(bf16[32,64,8,2,16]{0,4,1,3,2:T(8,128)(2,1)} %bitcast.49), kind=kLoop, calls=%fused_computation.57 | loop fusion | flops 262144 | bytes 2097152 | tf_op jit(solution)/shard_map/slice | solution.py:82
  72.1 2.9 %pad_maximum_fusion.1 = bf16[32,64,8,2,16]{0,4,1,3,2:T(8,128)(2,1)} fusion(bf16[32,64,8,1,16]{0,4,1,3,2:T(8,128)(2,1)S(1)} %get-tuple-element.18, bf16[32,64,8,1,16]{0,4,1,3,2:T(8,128)(2,1)S(1)} %get-tuple-element.17), kind=kLoop, calls=%fused_computation.5 | loop fusion | flops 524288 | bytes 2097152 | tf_op jit(solution)/shard_map/stack | solution.py:82
  75.0 7.4 %copy.29 = bf16[32,64,8,2,16]{1,4,3,2,0:T(8,128)(2,1)} copy(bf16[32,64,8,2,16]{0,4,1,3,2:T(8,128)(2,1)} %pad_maximum_fusion.1) | data formatting | bytes 2097152 | tf_op jit(solution)/shard_map/stack | solution.py:82
  82.4 2.1 %copy.31 = bf16[32,1,64,256]{3,2,1,0:T(8,128)(2,1)S(1)} copy(bf16[32,1,64,256]{2,3,0,1:T(8,128)(2,1)} %bitcast.53) | data formatting | bytes 2097152 | tf_op jit(solution)/shard_map/stack;reshape | solution.py:83
  84.5 1.6 copy.30
  86.1 96.8 %all-gather.2.cloned.1.call-done = bf16[32,1024,256]{2,1,0:T(8,128)(2,1)} async-done(((bf16[32,64,256]{2,1,0:T(8,128)(2,1)}), bf16[32,1024,256]{2,1,0:T(8,128)(2,1)}) %all-gather.2.cloned.1.call-update) | async-done | bytes 16777232 | tf_op jit(solution)/shard_map/all_gather | solution.py:84
  182.9 12.9 %broadcast_multiply_fusion = f32[32,2,64,1024]{3,2,1,0:T(8,128)} fusion(bf16[32,1024,256]{2,1,0:T(8,128)(2,1)} %all-gather.2.cloned.1.call-done, bf16[32,1,64,256]{3,2,1,0:T(8,128)(2,1)S(1)} %copy.31, bf16[32,1,64,256]{3,2,1,0:T(8,128)(2,1)} %copy.30), kind=kOutput, calls=%fused_computation.3 | convolution fusion | flops 2152726528 | bytes 35651584 | tf_op jit(solution)/shard_map/fcqk,fpk->fcqp/dot_general | solution.py:85
  (4 shorter events, 0.0 us)
Async XLA Ops:
  6.5 176.4 %all-gather.2.cloned.1.call-start = ((), (), s32[]{:S(2)}) async-start(), calls=%async_computation.1 | async-start | bytes 17825792 | tf_op jit(solution)/shard_map/all_gather | solution.py:84
  15.1 7.2 %slice-start = ((s8[8388608]{0:T(1024)(128)(4,1)}), s8[4194304]{0:T(1024)(128)(4,1)S(1)}, s32[]{:S(2)}) async-start(s8[8388608]{0:T(1024)(128)(4,1)} %bitcast.46), calls=%async_computation.2 | async-start | bytes 8388608
  17.2 18.4 %collective-permute-start.1 = (f32[512,256]{1,0:T(8,128)}, f32[512,256]{1,0:T(8,128)S(1)}, u32[]{:S(2)}, u32[]{:S(2)}) collective-permute-start(f32[512,256]{1,0:T(8,128)} %fusion.9), channel_id=1, source_target_pairs={{8,0},{16,8},{24,16},{32,24},{40,32},{48,40},{56,48},{64,56},{72,6... | collective-permute-start | bytes 1572872 | tf_op jit(solution)/shard_map/ppermute | solution.py:67
  18.6 3.7 %slice-start.1 = ((s8[8388608]{0:T(1024)(128)(4,1)}), s8[4194304]{0:T(1024)(128)(4,1)S(1)}, s32[]{:S(2)}) async-start(s8[8388608]{0:T(1024)(128)(4,1)} %bitcast.46), calls=%async_computation.3 | async-start | bytes 8388608
  20.7 15.1 %collective-permute-start = (f32[512,256]{1,0:T(8,128)}, f32[512,256]{1,0:T(8,128)}, u32[]{:S(2)}, u32[]{:S(2)}) collective-permute-start(f32[512,256]{1,0:T(8,128)} %fusion.10), channel_id=1, source_target_pairs={{0,8},{8,16},{16,24},{24,32},{32,40},{40,48},{48,56},{56,64},{64,7... | collective-permute-start | bytes 1572872 | tf_op jit(solution)/shard_map/ppermute | solution.py:66
Sparse Core Ops, SparseCore 0:
  69.6 113.3 all-gather.1

commit v10 on v9

--- a/solution.py
+++ b/solution.py
@@ -63,17 +63,17 @@
 
         to_next = transform(weights[0] * block[:, sector - 1 :].astype(jnp.float32))
         to_prev = transform(weights[2] * block[:, :1].astype(jnp.float32))
-        from_prev = lax.ppermute(to_next, "az", forward).reshape(2 * FREQS, 1, cycles, nb)
-        from_next = lax.ppermute(to_prev, "az", backward).reshape(2 * FREQS, 1, cycles, nb)
+        from_prev = lax.ppermute(to_next, "az", forward)
+        from_next = lax.ppermute(to_prev, "az", backward)
         zero = jnp.zeros_like(block[:, :1])
         prev = jnp.concatenate([zero, block[:, :-1]], axis=1).astype(jnp.float32)
         nxt = jnp.concatenate([block[:, 1:], zero], axis=1).astype(jnp.float32)
         total = weights[0] * prev + weights[1] * block.astype(jnp.float32) + weights[2] * nxt
         inner = lax.optimization_barrier(transform(total.transpose(1, 0, 2, 3)))
-        edges = jnp.concatenate(
-            [from_prev, jnp.zeros((2 * FREQS, sector - 2, cycles, nb), jnp.float32), from_next], axis=1
-        )
-        spectra = (inner + edges.reshape(inner.shape)).astype(jnp.bfloat16)
+        run = cycles * nb
+        spectra = jnp.concatenate(
+            [inner[:, :run] + from_prev, inner[:, run:-run], inner[:, -run:] + from_next], axis=1
+        ).astype(jnp.bfloat16)
         spectra = spectra.reshape(2, n_tm, fl, cycles * sector * nb).transpose(1, 0, 2, 3)
         shared = lax.all_to_all(spectra, "tm", 0, 0, tiled=True)
         x = shared.reshape(n_tm, 2, fl, local_rows, nb).transpose(2, 3, 0, 1, 4)

time: 203 us -> 196 us (0.966)
  local copies, waits for them, and re-layouts: 28.1 us -> 24.7 us
  other arithmetic: 21.9 us -> 19.4 us
    convert_element_type x1 -> x0, other arithmetic: 2.54 us -> none  [shards(): spectra = (inner + edges.reshape(inner.shape)).astype(jnp.bfloat16)]
where the time goes in v10:
time: 196 us; the launch traced here: 195 us
  waiting for transfers between devices  97.4 us (50%)
  local copies, waits for them, and re-layouts  24.7 us (13%)
  matrix products  21.6 us (11%)
  other arithmetic  19.4 us (10%)
  blocking collectives  15.7 us (8%)
  between operations  13.6 us (7%)
  starting transfers between devices  3.02 us (2%)
    all_gather x1, waiting for transfers between devices, shards(): columns = lax.all_gather(rows, 'az', axis=1, tiled=True)  97.4 us
    all_to_all x1, blocking collectives, shards(): shared = lax.all_to_all(spectra, 'tm', 0, 0, tiled=True)  15.7 us
    dot_general x1, matrix products, shards(): jnp.einsum('fcqk,fpk->fcqp', lhs, columns, preferred_element_type=jnp.flo...  12.9 us
    dot_general x3, matrix products, transform(): lax.dot_general(table, rows, (((0,), (1,)), ((), ())), preferred_element_...  8.74 us
    convert_element_type x2, other arithmetic, transform(): rows = v.astype(jnp.bfloat16).reshape(-1, length)  8.66 us
    another operation x1, local copies, waits for them, and re-layouts, shards(): turned = jnp.stack([x[:, :, :, 1], -x[:, :, :, 0]], 3).reshape(rows.shape)  7.35 us
    transpose x1, local copies, waits for them, and re-layouts, shards(): x = shared.reshape(n_tm, 2, fl, local_rows, nb).transpose(2, 3, 0, 1, 4)  6.64 us
  transfers between devices with their start and end apart: 3, of which 1 were waited for; matrix products, arithmetic and copies ran while one was open for 16% of the time, Pallas kernels for 0%

profile of v10, /device:TPU:1, one launch (start us, length us, event | category | flops | bytes accessed | tf_op | source)
XLA Modules:
  0.0 195.4 jit_solution(15415249601952814517)
XLA Ops:
  6.5 0.0 all-gather.2.cloned.1.call-start
  6.5 0.1 fusion.27
  6.6 0.1 subtract_multiply_fusion
  6.7 0.3 fusion.23
  7.0 0.3 fusion.25
  7.3 0.7 select_add_fusion.2
  8.0 0.1 broadcast_in_dim.23
  8.1 0.2 copy.29
  8.3 0.1 broadcast_in_dim.27
  8.4 0.2 copy.31
  8.6 3.1 %multiply_convert_fusion.1 = (bf16[16,1,16,4096]{3,2,1,0:T(8,128)(2,1)S(1)}, bf16[16,1,16,4096]{3,2,1,0:T(8,128)(2,1)S(1)}) fusion(bf16[16,4,16,4096]{3,2,1,0:T(8,128)(2,1)} %param.3, f32[16,4096]{1,0:T(8,128)S(1)} %bitcast.52, f32[16,4096]{1,0:T(8,128)S(1)} %bitcast.54), kind=kLoop, calls=%fused_computation.11 | loop fusion | flops 6291456 | bytes 8912896 | tf_op jit(solution)/shard_map/convert_element_type | solution.py:59
  11.7 1.2 multiply_subtract_fusion
  12.9 2.2 %fusion.4 = (bf16[4096,256]{1,0:T(8,128)(2,1)S(1)}, bf16[4096,256]{1,0:T(8,128)(2,1)S(1)}) fusion(f32[64,64,256]{2,1,0:T(8,128)S(1)} %get-tuple-element.22, f32[4096]{0:T(1024)S(1)} %fusion.27, f32[64,64,256]{2,1,0:T(8,128)S(1)} %get-tuple-element.21, f32[4096]{0:T(1024)S(1)} %subtract_multiply_fusion), kind=kLoop, calls=%fused_computation.7 | loop fusion | flops 4194304 | bytes 12615680 | tf_op jit(solution)/shard_map/convert.8
  15.1 0.0 slice-start
  15.1 2.1 %fusion.9 = f32[512,256]{1,0:T(8,128)} fusion(bf16[256,4096]{1,0:T(8,128)(2,1)S(1)} %bitcast.57, bf16[4096,256]{1,0:T(8,128)(2,1)S(1)} %get-tuple-element.30, bf16[4096,256]{1,0:T(8,128)(2,1)S(1)} %get-tuple-element.31), kind=kOutput, calls=%fused_computation.18 | convolution fusion | flops 1082130432 | bytes 6815744 | tf_op jit(solution)/shard_map/dot_general | solution.py:60
  17.2 1.4 collective-permute-start.1
  18.6 0.0 slice-start.1
  18.6 2.1 %fusion.10 = f32[512,256]{1,0:T(8,128)} fusion(bf16[256,4096]{1,0:T(8,128)(2,1)S(1)} %bitcast.56, bf16[4096,256]{1,0:T(8,128)(2,1)S(1)} %get-tuple-element.30, bf16[4096,256]{1,0:T(8,128)(2,1)S(1)} %get-tuple-element.31), kind=kOutput, calls=%fused_computation.19 | convolution fusion | flops 1082130432 | bytes 6815744 | tf_op jit(solution)/shard_map/dot_general | solution.py:60
  20.7 1.6 collective-permute-start
  22.3 0.0 slice-done
  22.4 0.0 slice-done.1
  22.4 1.5 fusion.32
  23.9 0.1 broadcast_in_dim.25
  24.0 0.2 copy.30
  24.1 5.5 %add_convert_fusion = bf16[16,4,16,4096]{3,2,0,1:T(8,128)(2,1)S(1)} fusion(f32[16,4096]{1,0:T(8,128)S(1)} %bitcast.55, f32[16,4096]{1,0:T(8,128)S(1)} %bitcast.59, f32[16,4096]{1,0:T(8,128)S(1)} %bitcast.53, bf16[16,4,16,4096]{3,2,1,0:T(8,128)(2,1)S(1)} %bitcast.45, bf16[16,3,16,4096]{3,2,1,0:T(8,128)(2,1)S(1)} %get-tuple-element.15, ...), kind=kLoop, calls=%fused_computation.2 | loop fusion | flops 37748736 | bytes 30146560 | tf_op jit(solution)/shard_map/convert_element_type | solution.py:59
  29.6 4.5 %fusion.11 = f32[512,1024]{1,0:T(8,128)S(1)} fusion(bf16[1024,4096]{1,0:T(8,128)(2,1)S(1)} %bitcast.50, bf16[4096,256]{1,0:T(8,128)(2,1)S(1)} %get-tuple-element.30, bf16[4096,256]{1,0:T(8,128)(2,1)S(1)} %get-tuple-element.31), kind=kOutput, calls=%fused_computation.20 | convolution fusion | flops 4303355904 | bytes 14680064 | tf_op jit(solution)/shard_map/dot_general | solution.py:60
  34.2 0.1 slice.65
  34.3 0.0 collective-permute-done.1
  34.3 0.0 collective-permute-done
  34.3 0.2 fusion.13
  34.5 0.1 copy_bitcast_fusion
  34.6 15.7 %all_to_all.5 = bf16[8,2,32,1024]{3,2,1,0:T(8,128)(2,1)S(1)} all-to-all(bf16[8,2,32,1024]{3,2,1,0:T(8,128)(2,1)S(1)} %copy_bitcast_fusion), channel_id=1, replica_groups=mesh['az'=16,'tm'=8] {'tm'}, dimensions={0} | all-to-all | bytes 2097152 | tf_op jit(solution)/shard_map/all_to_all | solution.py:78
  50.3 3.1 %copy.21 = bf16[8,2,32,1024]{2,3,1,0:T(8,128)(2,1)} copy(bf16[8,2,32,1024]{3,2,1,0:T(8,128)(2,1)S(1)} %all_to_all.5) | data formatting | bytes 2097152 | tf_op jit(solution)/shard_map/all_to_all | solution.py:78
  53.4 6.6 %copy.22 = bf16[32,64,8,2,16]{1,4,3,2,0:T(8,128)(2,1)S(1)} copy(bf16[32,64,8,2,16]{0,4,1,3,2:T(8,128)(2,1)} %bitcast.46) | data formatting | bytes 2097152 | tf_op jit(solution)/shard_map/transpose | solution.py:79
  60.0 1.6 copy.27
  61.7 0.0 all-gather.2.cloned.1.call-update
  61.7 2.6 %fusion.33 = (bf16[32,64,8,1,16]{0,4,1,3,2:T(8,128)(2,1)S(1)}, bf16[32,64,8,1,16]{0,4,1,3,2:T(8,128)(2,1)S(1)}) fusion(bf16[32,64,8,2,16]{0,4,1,3,2:T(8,128)(2,1)} %bitcast.47), kind=kLoop, calls=%fused_computation.61 | loop fusion | flops 262144 | bytes 2097152 | tf_op jit(solution)/shard_map/slice | solution.py:82
  64.3 2.9 %pad_maximum_fusion.1 = bf16[32,64,8,2,16]{0,4,1,3,2:T(8,128)(2,1)} fusion(bf16[32,64,8,1,16]{0,4,1,3,2:T(8,128)(2,1)S(1)} %get-tuple-element.18, bf16[32,64,8,1,16]{0,4,1,3,2:T(8,128)(2,1)S(1)} %get-tuple-element.17), kind=kLoop, calls=%fused_computation.5 | loop fusion | flops 524288 | bytes 2097152 | tf_op jit(solution)/shard_map/stack | solution.py:82
  67.3 7.4 %copy.23 = bf16[32,64,8,2,16]{1,4,3,2,0:T(8,128)(2,1)} copy(bf16[32,64,8,2,16]{0,4,1,3,2:T(8,128)(2,1)} %pad_maximum_fusion.1) | data formatting | bytes 2097152 | tf_op jit(solution)/shard_map/stack | solution.py:82
  74.6 2.0 %copy.25 = bf16[32,1,64,256]{3,2,1,0:T(8,128)(2,1)S(1)} copy(bf16[32,1,64,256]{2,3,0,1:T(8,128)(2,1)} %bitcast.51) | data formatting | bytes 2097152 | tf_op jit(solution)/shard_map/stack;reshape | solution.py:83
  76.7 1.6 copy.24
  78.3 97.4 %all-gather.2.cloned.1.call-done = bf16[32,1024,256]{2,1,0:T(8,128)(2,1)} async-done(((bf16[32,64,256]{2,1,0:T(8,128)(2,1)}), bf16[32,1024,256]{2,1,0:T(8,128)(2,1)}) %all-gather.2.cloned.1.call-update) | async-done | bytes 16777232 | tf_op jit(solution)/shard_map/all_gather | solution.py:84
  175.7 12.9 %broadcast_multiply_fusion = f32[32,2,64,1024]{3,2,1,0:T(8,128)} fusion(bf16[32,1024,256]{2,1,0:T(8,128)(2,1)} %all-gather.2.cloned.1.call-done, bf16[32,1,64,256]{3,2,1,0:T(8,128)(2,1)S(1)} %copy.25, bf16[32,1,64,256]{3,2,1,0:T(8,128)(2,1)} %copy.24), kind=kOutput, calls=%fused_computation.3 | convolution fusion | flops 2152726528 | bytes 35651584 | tf_op jit(solution)/shard_map/fcqk,fpk->fcqp/dot_general | solution.py:85
  (3 shorter events, 0.0 us)
Async XLA Ops:
  6.5 169.2 %all-gather.2.cloned.1.call-start = ((), (), s32[]{:S(2)}) async-start(), calls=%async_computation.1 | async-start | bytes 17825792 | tf_op jit(solution)/shard_map/all_gather | solution.py:84
  15.1 7.2 %slice-start = ((s8[8388608]{0:T(1024)(128)(4,1)}), s8[4194304]{0:T(1024)(128)(4,1)S(1)}, s32[]{:S(2)}) async-start(s8[8388608]{0:T(1024)(128)(4,1)} %bitcast.44), calls=%async_computation.2 | async-start | bytes 8388608
  17.2 17.0 %collective-permute-start.1 = (f32[512,256]{1,0:T(8,128)}, f32[512,256]{1,0:T(8,128)S(1)}, u32[]{:S(2)}, u32[]{:S(2)}) collective-permute-start(f32[512,256]{1,0:T(8,128)} %fusion.9), channel_id=1, source_target_pairs={{8,0},{16,8},{24,16},{32,24},{40,32},{48,40},{56,48},{64,56},{72,6... | collective-permute-start | bytes 1572872 | tf_op jit(solution)/shard_map/ppermute | solution.py:67
  18.6 3.7 %slice-start.1 = ((s8[8388608]{0:T(1024)(128)(4,1)}), s8[4194304]{0:T(1024)(128)(4,1)S(1)}, s32[]{:S(2)}) async-start(s8[8388608]{0:T(1024)(128)(4,1)} %bitcast.44), calls=%async_computation.3 | async-start | bytes 8388608
  20.7 13.6 %collective-permute-start = (f32[512,256]{1,0:T(8,128)}, f32[512,256]{1,0:T(8,128)S(1)}, u32[]{:S(2)}, u32[]{:S(2)}) collective-permute-start(f32[512,256]{1,0:T(8,128)} %fusion.10), channel_id=1, source_target_pairs={{0,8},{8,16},{16,24},{24,32},{32,40},{40,48},{48,56},{56,64},{64,7... | collective-permute-start | bytes 1572872 | tf_op jit(solution)/shard_map/ppermute | solution.py:66
Sparse Core Ops, SparseCore 0:
  61.8 113.8 all-gather.1

commit v11 on v10

--- a/solution.py
+++ b/solution.py
@@ -3,10 +3,14 @@
 import jax
 import jax.numpy as jnp
 from jax import lax
+from jax.sharding import Mesh
 from jax.sharding import PartitionSpec as P
 
 FREQS = 256
 BLOCK_CHUNKS = 1
+AZ = ("xh", "z", "core")
+TM = ("xl", "y")
+CHIPS = ("xh", "z")
 
 
 def dft_table(length, freqs):
@@ -41,8 +45,8 @@
     cycles, sector, blocks, length = pressure.shape
     subs = offsets.shape[1]
     sub_len = length // subs
-    n_az = lax.axis_size("az")
-    n_tm = lax.axis_size("tm")
+    n_az = lax.axis_size(AZ)
+    n_tm = lax.axis_size(TM)
     forward = [(i, (i + 1) % n_az) for i in range(n_az)]
     backward = [((i + 1) % n_az, i) for i in range(n_az)]
     table = dft_table(length, FREQS)
@@ -63,8 +67,8 @@
 
         to_next = transform(weights[0] * block[:, sector - 1 :].astype(jnp.float32))
         to_prev = transform(weights[2] * block[:, :1].astype(jnp.float32))
-        from_prev = lax.ppermute(to_next, "az", forward)
-        from_next = lax.ppermute(to_prev, "az", backward)
+        from_prev = lax.ppermute(to_next, AZ, forward)
+        from_next = lax.ppermute(to_prev, AZ, backward)
         zero = jnp.zeros_like(block[:, :1])
         prev = jnp.concatenate([zero, block[:, :-1]], axis=1).astype(jnp.float32)
         nxt = jnp.concatenate([block[:, 1:], zero], axis=1).astype(jnp.float32)
@@ -75,23 +79,38 @@
             [inner[:, :run] + from_prev, inner[:, run:-run], inner[:, -run:] + from_next], axis=1
         ).astype(jnp.bfloat16)
         spectra = spectra.reshape(2, n_tm, fl, cycles * sector * nb).transpose(1, 0, 2, 3)
-        shared = lax.all_to_all(spectra, "tm", 0, 0, tiled=True)
+        shared = lax.all_to_all(spectra, TM, 0, 0, tiled=True)
         x = shared.reshape(n_tm, 2, fl, local_rows, nb).transpose(2, 3, 0, 1, 4)
         x = x.reshape(fl, local_rows, n_tm, 2, nb)
         rows = x.reshape(fl, local_rows, n_tm * 2 * nb)
         turned = jnp.stack([x[:, :, :, 1], -x[:, :, :, 0]], 3).reshape(rows.shape)
-        lhs = jnp.stack([rows, turned], 1)
-        columns = lax.all_gather(rows, "az", axis=1, tiled=True)
-        part = jnp.einsum("fcqk,fpk->fcqp", lhs, columns, preferred_element_type=jnp.float32)
+        lhs = jnp.stack([rows, turned], 1).reshape(fl, 2, local_rows, n_tm, 2, nb)
+        core = lax.axis_index("core")
+        swap = [(0, 1), (1, 0)]
+        x = x.reshape(fl, local_rows, n_tm, 2, nb)
+        mine = lax.dynamic_index_in_dim(x, core, 3, keepdims=False)
+        theirs = lax.ppermute(lax.dynamic_index_in_dim(x, 1 - core, 3, keepdims=False), "core", swap)
+        chip = jnp.where(
+            core == 0, jnp.concatenate([mine, theirs], 1), jnp.concatenate([theirs, mine], 1)
+        ).reshape(fl, 2 * local_rows, n_tm * nb)
+        own_cols = lax.all_gather(chip, CHIPS, axis=1, tiled=True)
+        other_cols = lax.ppermute(own_cols, "core", swap)
+        l_own = lax.dynamic_index_in_dim(lhs, core, 4, keepdims=False).reshape(fl, 2, local_rows, -1)
+        l_other = lax.dynamic_index_in_dim(lhs, 1 - core, 4, keepdims=False).reshape(fl, 2, local_rows, -1)
+        part = jnp.einsum(
+            "fcqk,fpk->fcqp", l_own, own_cols, preferred_element_type=jnp.float32
+        ) + jnp.einsum("fcqk,fpk->fcqp", l_other, other_cols, preferred_element_type=jnp.float32)
         result = part if result is None else result + part
     return result * (1.0 / (n_tm * blocks))
 
 
 def solution(mesh):
+    az, tm = mesh.devices.shape
+    fine = Mesh(mesh.devices.reshape(2, az // 4, 2, 2, tm // 2), ("xh", "z", "core", "xl", "y"))
     return jax.shard_map(
         shards,
-        mesh=mesh,
-        in_specs=(P(None, "az", "tm", None), P("tm", None), P("tm", None)),
-        out_specs=P("tm", None, "az", None),
+        mesh=fine,
+        in_specs=(P(None, AZ, TM, None), P(TM, None), P(TM, None)),
+        out_specs=P(TM, None, AZ, None),
         check_vma=False,
     )

time: 196 us -> 241 us (1.23)
  waiting for transfers between devices: 97.4 us -> 116 us
  blocking collectives: 15.7 us -> 0 us
  matrix products: 21.6 us -> 37.2 us
  starting transfers between devices: 3.02 us -> 15.4 us
  local copies, waits for them, and re-layouts: 24.7 us -> 34.4 us
  other arithmetic: 19.4 us -> 23.9 us
    dynamic_slice x0 -> x4, local copies, waits for them, and re-layouts: none -> 21.1 us  [the longest x1 7.39 us: shards(): lax.dynamic_index_in_dim(lhs, 1 - core, 4, keepdims=False)]
    all_to_all x1 -> x0, blocking collectives: 15.7 us -> none  [shards(): shared = lax.all_to_all(spectra, 'tm', 0, 0, tiled=True)]
    dot_general x1 -> x2, matrix products: 12.9 us -> 28.5 us  [the longest x1 16.6 us: shards(): jnp.einsum('fcqk,fpk->fcqp', l_other, other_cols, preferred_element_type=...]
    another operation x3 -> x0, local copies, waits for them, and re-layouts: 11 us -> none  [the longest x1 7.35 us: shards(): turned = jnp.stack([x[:, :, :, 1], -x[:, :, :, 0]], 3).reshape(rows.shape)]
    all_to_all x0 -> x1, waiting for transfers between devices: none -> 9.87 us  [shards(): shared = lax.all_to_all(spectra, TM, 0, 0, tiled=True)]
    all_gather x1, waiting for transfers between devices: 97.4 us -> 106 us  [shards(): own_cols = lax.all_gather(chip, CHIPS, axis=1, tiled=True)]
    ppermute x2 -> x4, starting transfers between devices: 3.02 us -> 10.3 us  [the longest x1 5.83 us: shards(): lax.ppermute(lax.dynamic_index_in_dim(x, 1 - core, 3, keepdims=False), 'c...]
    transpose x1 -> x0, local copies, waits for them, and re-layouts: 6.64 us -> none  [shards(): x = shared.reshape(n_tm, 2, fl, local_rows, nb).transpose(2, 3, 0, 1, 4)]
  transfers between devices with their start and end apart: 3 -> 6, of which waited for: 1 -> 2; matrix products, arithmetic and copies ran while one was open for 16% -> 21% of each run, Pallas kernels for 0% -> 0%
where the time goes in v11:
time: 241 us; the launch traced here: 240 us
  waiting for transfers between devices  116 us (48%)
  matrix products  37.2 us (15%)
  local copies, waits for them, and re-layouts  34.4 us (14%)
  other arithmetic  23.9 us (10%)
  starting transfers between devices  15.4 us (6%)
  between operations  13.6 us (6%)
    all_gather x1, waiting for transfers between devices, shards(): own_cols = lax.all_gather(chip, CHIPS, axis=1, tiled=True)  106 us
    dot_general x1, matrix products, shards(): jnp.einsum('fcqk,fpk->fcqp', l_other, other_cols, preferred_element_type=...  16.6 us
    dot_general x1, matrix products, shards(): jnp.einsum('fcqk,fpk->fcqp', l_own, own_cols, preferred_element_type=jnp....  11.9 us
    all_to_all x1, waiting for transfers between devices, shards(): shared = lax.all_to_all(spectra, TM, 0, 0, tiled=True)  9.87 us
    dot_general x3, matrix products, transform(): lax.dot_general(table, rows, (((0,), (1,)), ((), ())), preferred_element_...  8.76 us
    convert_element_type x2, other arithmetic, transform(): rows = v.astype(jnp.bfloat16).reshape(-1, length)  8.66 us
    dynamic_slice x1, local copies, waits for them, and re-layouts, shards(): lax.dynamic_index_in_dim(lhs, 1 - core, 4, keepdims=False)  7.39 us
    dynamic_slice x2, local copies, waits for them, and re-layouts, shards(): mine = lax.dynamic_index_in_dim(x, core, 3, keepdims=False)  7.04 us
  transfers between devices with their start and end apart: 6, of which 2 were waited for; matrix products, arithmetic and copies ran while one was open for 21% of the time, Pallas kernels for 0%

profile of v11, /device:TPU:1, one launch (start us, length us, event | category | flops | bytes accessed | tf_op | source)
XLA Modules:
  0.0 240.4 jit_solution(15624540245322104979)
XLA Ops:
  6.5 0.1 fusion.25
  6.6 0.1 subtract_multiply_fusion
  6.7 0.7 select_add_fusion.2
  7.4 0.1 broadcast_in_dim.23
  7.5 0.2 copy.43
  7.7 0.1 broadcast_in_dim.27
  7.8 0.2 copy.45
  8.0 0.3 fusion.21
  8.2 0.3 fusion.23
  8.6 3.1 %multiply_convert_fusion.1 = (bf16[16,1,16,4096]{3,2,1,0:T(8,128)(2,1)S(1)}, bf16[16,1,16,4096]{3,2,1,0:T(8,128)(2,1)S(1)}) fusion(bf16[16,4,16,4096]{3,2,1,0:T(8,128)(2,1)} %param.3, f32[16,4096]{1,0:T(8,128)S(1)} %bitcast.69, f32[16,4096]{1,0:T(8,128)S(1)} %bitcast.71), kind=kLoop, calls=%fused_computation.18 | loop fusion | flops 6291456 | bytes 8912896 | tf_op jit(solution)/shard_map/convert_element_type | solution.py:63
  11.7 1.2 multiply_subtract_fusion
  12.9 2.2 fusion.5
  15.1 0.0 slice-start
  15.1 2.1 fusion.8
  17.2 3.0 %collective-permute-start = (f32[512,256]{1,0:T(8,128)}, f32[512,256]{1,0:T(8,128)S(1)}, u32[]{:S(2)}, u32[]{:S(2)}) collective-permute-start(f32[512,256]{1,0:T(8,128)} %fusion.8), channel_id=1, source_target_pairs={{0,8},{8,16},{16,24},{24,32},{32,40},{40,48},{48,56},{56,64},{64,7... | collective-permute-start | bytes 1572872 | tf_op jit(solution)/shard_map/ppermute | solution.py:70
  20.3 0.0 slice-start.1
  20.3 2.1 fusion.7
  22.4 0.0 collective-permute-start.1
  22.4 0.0 slice-done
  22.4 0.1 slice-done.1
  22.4 1.5 fusion.29
  24.0 0.1 broadcast_in_dim.25
  24.1 0.2 copy.44
  24.2 5.5 %add_convert_fusion = bf16[16,4,16,4096]{3,2,0,1:T(8,128)(2,1)S(1)} fusion(f32[16,4096]{1,0:T(8,128)S(1)} %bitcast.72, f32[16,4096]{1,0:T(8,128)S(1)} %bitcast.76, f32[16,4096]{1,0:T(8,128)S(1)} %bitcast.70, bf16[16,4,16,4096]{3,2,1,0:T(8,128)(2,1)S(1)} %bitcast.61, bf16[16,3,16,4096]{3,2,1,0:T(8,128)(2,1)S(1)} %get-tuple-element.17, ...), kind=kLoop, calls=%fused_computation.1 | loop fusion | flops 37748736 | bytes 30146560 | tf_op jit(solution)/shard_map/convert_element_type | solution.py:63
  29.7 4.5 %fusion.9 = f32[512,1024]{1,0:T(8,128)S(1)} fusion(bf16[1024,4096]{1,0:T(8,128)(2,1)S(1)} %bitcast.65, bf16[4096,256]{1,0:T(8,128)(2,1)S(1)} %get-tuple-element.34, bf16[4096,256]{1,0:T(8,128)(2,1)S(1)} %get-tuple-element.35), kind=kOutput, calls=%fused_computation.26 | convolution fusion | flops 4303355904 | bytes 14680064 | tf_op jit(solution)/shard_map/dot_general | solution.py:64
  34.3 0.1 slice.65
  34.4 0.0 collective-permute-done
  34.4 0.0 collective-permute-done.1
  34.4 0.2 fusion.11
  34.6 1.1 copy_bitcast_fusion
  35.7 5.1 %all-to-all-start = ((bf16[8,2,32,1024]{3,2,1,0:T(8,128)(2,1)}), bf16[8,2,32,1024]{3,2,1,0:T(8,128)(2,1)S(1)}, u32[]{:S(2)}, u32[]{:S(2)}) async-start(bf16[8,2,32,1024]{3,2,1,0:T(8,128)(2,1)} %copy_bitcast_fusion), calls=%async_computation | async-start | bytes 2097152 | tf_op jit(solution)/shard_map/all_to_all | solution.py:82
  40.8 0.0 all-gather.2.cloned.1.call-start
  40.8 9.9 %all-to-all-done = bf16[8,2,32,1024]{3,2,1,0:T(8,128)(2,1)S(1)} async-done(((bf16[8,2,32,1024]{3,2,1,0:T(8,128)(2,1)}), bf16[8,2,32,1024]{3,2,1,0:T(8,128)(2,1)S(1)}, u32[]{:S(2)}, u32[]{:S(2)}) %all-to-all-start) | async-done | bytes 1048608 | tf_op jit(solution)/shard_map/all_to_all | solution.py:82
  50.7 3.1 %copy.28 = bf16[8,2,32,1024]{2,3,1,0:T(8,128)(2,1)} copy(bf16[8,2,32,1024]{3,2,1,0:T(8,128)(2,1)S(1)} %all-to-all-done) | data formatting | bytes 2097152 | tf_op jit(solution)/shard_map/all_to_all | solution.py:82
  53.8 4.4 %dynamic-slice_bitcast_fusion.1 = (bf16[32,64,8,1,16]{0,4,1,3,2:T(8,128)(2,1)S(1)}, bf16[32,64,8,16]{0,3,1,2:T(8,128)(2,1)}) fusion(bf16[8,2,32,64,16]{2,4,3,1,0:T(8,128)(2,1)} %bitcast.62, s32[]{:T(128)S(6)} %select_n.58, s32[]{:T(128)S(6)} %select_n.60), kind=kLoop, calls=%fused_computation.23 | loop fusion | bytes 2097160 | tf_op jit(solution)/shard_map/jit(dynamic_index_in_dim)/dynamic_slice | solution.py:91
  58.2 4.6 %copy.31 = bf16[32,64,8,16]{1,3,2,0:T(8,128)(2,1)} copy(bf16[32,64,8,16]{0,3,1,2:T(8,128)(2,1)} %get-tuple-element.20) | data formatting | bytes 1048576 | tf_op jit(solution)/shard_map/jit(dynamic_index_in_dim)/squeeze | solution.py:92
  62.8 5.8 %collective-permute-start.2 = (bf16[32,64,8,16]{1,3,2,0:T(8,128)(2,1)}, bf16[32,64,8,16]{1,3,2,0:T(8,128)(2,1)}, u32[]{:S(2)}, u32[]{:S(2)}) collective-permute-start(bf16[32,64,8,16]{1,3,2,0:T(8,128)(2,1)} %copy.31), channel_id=1, source_target_pairs={{0,8},{8,0},{1,9},{9,1},{2,10},{10,2},{3,11},{11,3},{4,12},{12,4},... | collective-permute-start | bytes 1572872 | tf_op jit(solution)/shard_map/ppermute | solution.py:92
  68.7 2.6 %copy.30 = bf16[32,64,8,1,16]{1,4,2,0,3:T(8,128)(2,1)S(1)} copy(bf16[32,64,8,1,16]{0,4,1,3,2:T(8,128)(2,1)S(1)} %get-tuple-element.19) | data formatting | bytes 1048576 | tf_op jit(solution)/shard_map/jit(dynamic_index_in_dim)/dynamic_slice | solution.py:91
  71.3 0.4 copy.32
  71.7 0.0 collective-permute-done.2
  71.7 1.6 copy.33
  73.3 1.4 maximum_select_fusion
  74.7 0.0 all-gather.2.cloned.1.call-update
  74.8 105.9 %all-gather.2.cloned.1.call-done = bf16[32,1024,128]{2,1,0:T(8,128)(2,1)} async-done(((bf16[32,128,128]{2,1,0:T(8,128)(2,1)}), bf16[32,1024,128]{2,1,0:T(8,128)(2,1)}) %all-gather.2.cloned.1.call-update) | async-done | bytes 8388624 | tf_op jit(solution)/shard_map/all_gather | solution.py:96
  180.7 1.4 collective-permute-start.3
  182.1 2.6 %fusion.30 = (bf16[32,64,8,1,16]{0,4,1,3,2:T(8,128)(2,1)S(1)}, bf16[32,64,8,1,16]{0,4,1,3,2:T(8,128)(2,1)S(1)}) fusion(bf16[32,64,8,2,16]{0,4,1,3,2:T(8,128)(2,1)} %bitcast.63), kind=kLoop, calls=%fused_computation.67 | loop fusion | flops 262144 | bytes 2097152 | tf_op jit(solution)/shard_map/slice | solution.py:86
  184.7 0.0 copy-start
  184.7 0.9 maximum_bitcast_fusion
  185.7 1.3 copy-done
  186.9 4.2 %fusion.3 = (bf16[32,2,64,8,1,16]{0,5,2,4,3,1:T(8,128)(2,1)}, bf16[32,2,64,8,1,16]{0,5,2,4,3,1:T(8,128)(2,1)}) fusion(s32[]{:T(128)S(6)} %select_n.60, bf16[32,1,64,8,2,16]{0,5,2,4,3,1:T(8,128)(2,1)S(1)} %bitcast.64, bf16[32,1,64,8,2,16]{0,5,2,4,3,1:T(8,128)(2,1)S(1)} %maximum_bitcast_fusion, s32[]{:T(128)S(6)} %select_n.58), kind=kLoop, calls=%fused_computation.9 | loop fusion | flops 1048576 | bytes 4194312 | tf_op jit(solution)/shard_map/stack | solution.py:87
  191.1 6.7 %copy.29 = bf16[32,2,64,8,1,16]{2,5,3,1,0,4:T(8,128)(2,1)S(1)} copy(bf16[32,2,64,8,1,16]{0,5,2,4,3,1:T(8,128)(2,1)} %get-tuple-element.14) | data formatting | bytes 2097152 | tf_op jit(solution)/shard_map/jit(dynamic_index_in_dim)/dynamic_slice | solution.py:98
  197.7 7.4 %copy.37 = bf16[32,2,64,8,1,16]{2,5,3,1,0,4:T(8,128)(2,1)} copy(bf16[32,2,64,8,1,16]{0,5,2,4,3,1:T(8,128)(2,1)} %get-tuple-element.13) | data formatting | bytes 2097152 | tf_op jit(solution)/shard_map/jit(dynamic_index_in_dim)/dynamic_slice | solution.py:99
  205.1 11.9 %fusion.1 = f32[32,2,64,1024]{3,2,1,0:T(8,128)} fusion(bf16[32,2,64,128]{2,3,1,0:T(8,128)(2,1)S(1)} %bitcast.66, bf16[32,1024,128]{2,1,0:T(8,128)(2,1)} %all-gather.2.cloned.1.call-done), kind=kOutput, calls=%fused_computation.7 | convolution fusion | flops 1073741824 | bytes 26214400 | tf_op jit(solution)/shard_map/fcqk,fpk->fcqp/dot_general | solution.py:100
  217.0 0.0 collective-permute-done.3
  217.0 16.6 %add_multiply_fusion = f32[32,2,64,1024]{3,2,1,0:T(8,128)} fusion(f32[32,2,64,1024]{3,2,1,0:T(8,128)} %fusion.1, bf16[32,2,64,128]{2,3,1,0:T(8,128)(2,1)} %bitcast.67, bf16[32,1024,128]{2,1,0:T(8,128)(2,1)} %collective-permute-done.3), kind=kOutput, calls=%fused_computation | convolution fusion | flops 1082130432 | bytes 42991616 | tf_op jit(solution)/shard_map/fcqk,fpk->fcqp/dot_general | solution.py:102
  (3 shorter events, 0.0 us)
Async XLA Ops:
  15.1 7.3 %slice-start = ((s8[8388608]{0:T(1024)(128)(4,1)}), s8[4194304]{0:T(1024)(128)(4,1)S(1)}, s32[]{:S(2)}) async-start(s8[8388608]{0:T(1024)(128)(4,1)} %bitcast.60), calls=%async_computation.2 | async-start | bytes 8388608
  17.2 17.1 %collective-permute-start = (f32[512,256]{1,0:T(8,128)}, f32[512,256]{1,0:T(8,128)S(1)}, u32[]{:S(2)}, u32[]{:S(2)}) collective-permute-start(f32[512,256]{1,0:T(8,128)} %fusion.8), channel_id=1, source_target_pairs={{0,8},{8,16},{16,24},{24,32},{32,40},{40,48},{48,56},{56,64},{64,7... | collective-permute-start | bytes 1572872 | tf_op jit(solution)/shard_map/ppermute | solution.py:70
  20.3 2.2 slice-start.1
  22.4 12.0 %collective-permute-start.1 = (f32[512,256]{1,0:T(8,128)}, f32[512,256]{1,0:T(8,128)S(1)}, u32[]{:S(2)}, u32[]{:S(2)}) collective-permute-start(f32[512,256]{1,0:T(8,128)} %fusion.7), channel_id=1, source_target_pairs={{8,0},{16,8},{24,16},{32,24},{40,32},{48,40},{56,48},{64,56},{72,6... | collective-permute-start | bytes 1572872 | tf_op jit(solution)/shard_map/ppermute | solution.py:71
  35.7 15.0 %all-to-all-start = ((bf16[8,2,32,1024]{3,2,1,0:T(8,128)(2,1)}), bf16[8,2,32,1024]{3,2,1,0:T(8,128)(2,1)S(1)}, u32[]{:S(2)}, u32[]{:S(2)}) async-start(bf16[8,2,32,1024]{3,2,1,0:T(8,128)(2,1)} %copy_bitcast_fusion), calls=%async_computation | async-start | bytes 2097152 | tf_op jit(solution)/shard_map/all_to_all | solution.py:82
  40.8 139.9 %all-gather.2.cloned.1.call-start = ((), (), s32[]{:S(2)}) async-start(), calls=%async_computation.1 | async-start | bytes 9437184 | tf_op jit(solution)/shard_map/all_gather | solution.py:96
  62.8 8.9 %collective-permute-start.2 = (bf16[32,64,8,16]{1,3,2,0:T(8,128)(2,1)}, bf16[32,64,8,16]{1,3,2,0:T(8,128)(2,1)}, u32[]{:S(2)}, u32[]{:S(2)}) collective-permute-start(bf16[32,64,8,16]{1,3,2,0:T(8,128)(2,1)} %copy.31), channel_id=1, source_target_pairs={{0,8},{8,0},{1,9},{9,1},{2,10},{10,2},{3,11},{11,3},{4,12},{12,4},... | collective-permute-start | bytes 1572872 | tf_op jit(solution)/shard_map/ppermute | solution.py:92
  180.7 36.4 %collective-permute-start.3 = (bf16[32,1024,128]{2,1,0:T(8,128)(2,1)}, bf16[32,1024,128]{2,1,0:T(8,128)(2,1)}, u32[]{:S(2)}, u32[]{:S(2)}) collective-permute-start(bf16[32,1024,128]{2,1,0:T(8,128)(2,1)} %all-gather.2.cloned.1.call-done), channel_id=1, source_target_pairs={{0,8},{8,0},{1,9},{9,1},{2,10},{10,2},{3,11},{11,3},{4,12},{12,4},... | collective-permute-start | bytes 25165832 | tf_op jit(solution)/shard_map/ppermute | solution.py:97
  184.7 2.2 copy-start
Sparse Core Ops, SparseCore 0:
  74.9 105.7 all-gather.1

commit v12 on v10

--- a/solution.py
+++ b/solution.py
@@ -1,8 +1,11 @@
+import functools
 import math
 
 import jax
 import jax.numpy as jnp
 from jax import lax
+from jax.experimental import pallas as pl
+from jax.experimental.pallas import tpu as pltpu
 from jax.sharding import PartitionSpec as P
 
 FREQS = 256
@@ -35,6 +38,31 @@
         high = (offsets + 1 == shift).astype(frac.dtype)
         rows.append((1.0 - frac) * low + frac * high)
     return jnp.stack(rows, 0)
+
+
+def csm_kernel(lhs_ref, rhs_ref, out_ref, *, scale):
+    for i in range(lhs_ref.shape[0]):
+        prod = lax.dot_general(
+            lhs_ref[i], rhs_ref[i], (((1,), (1,)), ((), ())), preferred_element_type=jnp.float32
+        )
+        out_ref[i] = (prod * scale).reshape(out_ref.shape[1:])
+
+
+def cross_terms(lhs, columns, scale):
+    freqs, rows, width = lhs.shape
+    mics = columns.shape[1]
+    step = 4
+    return pl.pallas_call(
+        functools.partial(csm_kernel, scale=scale),
+        grid=(freqs // step,),
+        in_specs=[
+            pl.BlockSpec((step, rows, width), lambda i: (i, 0, 0)),
+            pl.BlockSpec((step, mics, width), lambda i: (i, 0, 0)),
+        ],
+        out_specs=pl.BlockSpec((step, 2, rows // 2, mics), lambda i: (i, 0, 0, 0)),
+        out_shape=jax.ShapeDtypeStruct((freqs, 2, rows // 2, mics), jnp.float32),
+        compiler_params=pltpu.CompilerParams(vmem_limit_bytes=48 * 1024 * 1024),
+    )(lhs, columns)
 
 
 def shards(pressure, offsets, frac):
@@ -82,9 +110,9 @@
         turned = jnp.stack([x[:, :, :, 1], -x[:, :, :, 0]], 3).reshape(rows.shape)
         lhs = jnp.stack([rows, turned], 1)
         columns = lax.all_gather(rows, "az", axis=1, tiled=True)
-        part = jnp.einsum("fcqk,fpk->fcqp", lhs, columns, preferred_element_type=jnp.float32)
+        part = cross_terms(lhs.reshape(fl, 2 * local_rows, -1), columns, 1.0 / (n_tm * blocks))
         result = part if result is None else result + part
-    return result * (1.0 / (n_tm * blocks))
+    return result
 
 
 def solution(mesh):

time: 196 us -> 199 us (1.015)
  Pallas kernels: 0 us -> 16.3 us
  matrix products: 21.6 us -> 8.74 us
  other arithmetic: 19.4 us -> 24.1 us
  waiting for transfers between devices: 97.4 us -> 92.9 us
    pallas_call x0 -> x1, Pallas kernels: none -> 16.3 us  [cross_terms(): pl.pallas_call(functools.partial(csm_kernel, scale=scale), grid=(freqs //...]
    dot_general x1 -> x0, matrix products: 12.9 us -> none  [shards(): jnp.einsum('fcqk,fpk->fcqp', lhs, columns, preferred_element_type=jnp.flo...]
    another operation x2 -> x3, other arithmetic: 2.34 us -> 7.03 us  [the longest x1 4.69 us: shards(): lhs = jnp.stack([rows, turned], 1)]
    all_gather x1, waiting for transfers between devices: 97.4 us -> 92.8 us  [shards(): columns = lax.all_gather(rows, 'az', axis=1, tiled=True)]
  transfers between devices with their start and end apart: 3 -> 3, of which waited for: 1 -> 1; matrix products, arithmetic and copies ran while one was open for 16% -> 18% of each run, Pallas kernels for 0% -> 0%
where the time goes in v12:
time: 199 us
  waiting for transfers between devices  92.9 us (47%)
  local copies, waits for them, and re-layouts  24.6 us (12%)
  other arithmetic  24.1 us (12%)
  Pallas kernels  16.3 us (8%)
  blocking collectives  15.7 us (8%)
  between operations  13.6 us (7%)
  matrix products  8.74 us (4%)
  starting transfers between devices  3.02 us (2%)
    all_gather x1, waiting for transfers between devices, shards(): columns = lax.all_gather(rows, 'az', axis=1, tiled=True)  92.8 us
    pallas_call x1, Pallas kernels, cross_terms(): pl.pallas_call(functools.partial(csm_kernel, scale=scale), grid=(freqs //...  16.3 us
    all_to_all x1, blocking collectives, shards(): shared = lax.all_to_all(spectra, 'tm', 0, 0, tiled=True)  15.7 us
    dot_general x3, matrix products, transform(): lax.dot_general(table, rows, (((0,), (1,)), ((), ())), preferred_element_...  8.74 us
    convert_element_type x2, other arithmetic, transform(): rows = v.astype(jnp.bfloat16).reshape(-1, length)  8.66 us
    another operation x1, local copies, waits for them, and re-layouts, shards(): turned = jnp.stack([x[:, :, :, 1], -x[:, :, :, 0]], 3).reshape(rows.shape)  7.35 us
    transpose x1, local copies, waits for them, and re-layouts, shards(): x = shared.reshape(n_tm, 2, fl, local_rows, nb).transpose(2, 3, 0, 1, 4)  6.64 us
    another operation x1, other arithmetic, shards(): lhs = jnp.stack([rows, turned], 1)  4.69 us
  transfers between devices with their start and end apart: 3, of which 1 were waited for; matrix products, arithmetic and copies ran while one was open for 18% of the time, Pallas kernels for 0%

profile of v12, /device:TPU:1, one launch (start us, length us, event | category | flops | bytes accessed | tf_op | source)
XLA Modules:
  0.0 198.9 jit_solution(12324835755361000034)
XLA Ops:
  6.5 0.0 all-gather.2.cloned.1.call-start
  6.5 0.1 fusion.20
  6.6 0.1 subtract_multiply_fusion
  6.7 0.3 fusion.16
  7.0 0.3 fusion.18
  7.3 0.7 select_add_fusion.2
  8.0 0.1 broadcast_in_dim.23
  8.1 0.2 copy.27
  8.3 0.1 broadcast_in_dim.27
  8.4 0.2 copy.29
  8.6 3.1 %multiply_convert_fusion.1 = (bf16[16,1,16,4096]{3,2,1,0:T(8,128)(2,1)S(1)}, bf16[16,1,16,4096]{3,2,1,0:T(8,128)(2,1)S(1)}) fusion(bf16[16,4,16,4096]{3,2,1,0:T(8,128)(2,1)} %param.3, f32[16,4096]{1,0:T(8,128)S(1)} %bitcast.47, f32[16,4096]{1,0:T(8,128)S(1)} %bitcast.49), kind=kLoop, calls=%fused_computation.9 | loop fusion | flops 6291456 | bytes 8912896 | tf_op jit(solution)/shard_map/convert_element_type | solution.py:87
  11.7 1.2 multiply_subtract_fusion
  12.9 2.2 %fusion = (bf16[4096,256]{1,0:T(8,128)(2,1)S(1)}, bf16[4096,256]{1,0:T(8,128)(2,1)S(1)}) fusion(f32[64,64,256]{2,1,0:T(8,128)S(1)} %get-tuple-element.22, f32[4096]{0:T(1024)S(1)} %fusion.20, f32[64,64,256]{2,1,0:T(8,128)S(1)} %get-tuple-element.21, f32[4096]{0:T(1024)S(1)} %subtract_multiply_fusion), kind=kLoop, calls=%fused_computation.5 | loop fusion | flops 4194304 | bytes 12615680 | tf_op jit(solution)/shard_map/convert.8
  15.1 0.0 slice-start
  15.1 2.1 %fusion.2 = f32[512,256]{1,0:T(8,128)} fusion(bf16[256,4096]{1,0:T(8,128)(2,1)S(1)} %bitcast.52, bf16[4096,256]{1,0:T(8,128)(2,1)S(1)} %get-tuple-element.30, bf16[4096,256]{1,0:T(8,128)(2,1)S(1)} %get-tuple-element.31), kind=kOutput, calls=%fused_computation.13 | convolution fusion | flops 1082130432 | bytes 6815744 | tf_op jit(solution)/shard_map/dot_general | solution.py:88
  17.2 1.4 collective-permute-start.1
  18.6 0.0 slice-start.1
  18.6 2.1 %fusion.3 = f32[512,256]{1,0:T(8,128)} fusion(bf16[256,4096]{1,0:T(8,128)(2,1)S(1)} %bitcast.51, bf16[4096,256]{1,0:T(8,128)(2,1)S(1)} %get-tuple-element.30, bf16[4096,256]{1,0:T(8,128)(2,1)S(1)} %get-tuple-element.31), kind=kOutput, calls=%fused_computation.14 | convolution fusion | flops 1082130432 | bytes 6815744 | tf_op jit(solution)/shard_map/dot_general | solution.py:88
  20.7 1.6 collective-permute-start
  22.3 0.0 slice-done
  22.4 0.0 slice-done.1
  22.4 1.5 fusion.24
  23.9 0.1 broadcast_in_dim.25
  24.0 0.2 copy.28
  24.1 5.5 %add_convert_fusion = bf16[16,4,16,4096]{3,2,0,1:T(8,128)(2,1)S(1)} fusion(f32[16,4096]{1,0:T(8,128)S(1)} %bitcast.50, f32[16,4096]{1,0:T(8,128)S(1)} %bitcast.54, f32[16,4096]{1,0:T(8,128)S(1)} %bitcast.48, bf16[16,4,16,4096]{3,2,1,0:T(8,128)(2,1)S(1)} %bitcast.40, bf16[16,3,16,4096]{3,2,1,0:T(8,128)(2,1)S(1)} %get-tuple-element.15, ...), kind=kLoop, calls=%fused_computation | loop fusion | flops 37748736 | bytes 30146560 | tf_op jit(solution)/shard_map/convert_element_type | solution.py:87
  29.6 4.5 %fusion.4 = f32[512,1024]{1,0:T(8,128)S(1)} fusion(bf16[1024,4096]{1,0:T(8,128)(2,1)S(1)} %bitcast.45, bf16[4096,256]{1,0:T(8,128)(2,1)S(1)} %get-tuple-element.30, bf16[4096,256]{1,0:T(8,128)(2,1)S(1)} %get-tuple-element.31), kind=kOutput, calls=%fused_computation.15 | convolution fusion | flops 4303355904 | bytes 14680064 | tf_op jit(solution)/shard_map/dot_general | solution.py:88
  34.2 0.1 slice.65
  34.3 0.0 collective-permute-done.1
  34.3 0.0 collective-permute-done
  34.3 0.2 fusion.6
  34.5 0.1 copy_bitcast_fusion
  34.6 15.7 %all_to_all.5 = bf16[8,2,32,1024]{3,2,1,0:T(8,128)(2,1)S(1)} all-to-all(bf16[8,2,32,1024]{3,2,1,0:T(8,128)(2,1)S(1)} %copy_bitcast_fusion), channel_id=1, replica_groups=mesh['az'=16,'tm'=8] {'tm'}, dimensions={0} | all-to-all | bytes 2097152 | tf_op jit(solution)/shard_map/all_to_all | solution.py:106
  50.3 3.1 %copy.21 = bf16[8,2,32,1024]{2,3,1,0:T(8,128)(2,1)} copy(bf16[8,2,32,1024]{3,2,1,0:T(8,128)(2,1)S(1)} %all_to_all.5) | data formatting | bytes 2097152 | tf_op jit(solution)/shard_map/all_to_all | solution.py:106
  53.4 6.6 %copy.22 = bf16[32,64,8,2,16]{1,4,3,2,0:T(8,128)(2,1)S(1)} copy(bf16[32,64,8,2,16]{0,4,1,3,2:T(8,128)(2,1)} %bitcast.41) | data formatting | bytes 2097152 | tf_op jit(solution)/shard_map/transpose | solution.py:107
  60.0 1.6 copy.26
  61.7 0.0 all-gather.2.cloned.1.call-update
  61.7 2.6 %fusion.25 = (bf16[32,64,8,1,16]{0,4,1,3,2:T(8,128)(2,1)S(1)}, bf16[32,64,8,1,16]{0,4,1,3,2:T(8,128)(2,1)S(1)}) fusion(bf16[32,64,8,2,16]{0,4,1,3,2:T(8,128)(2,1)} %bitcast.42), kind=kLoop, calls=%fused_computation.55 | loop fusion | flops 262144 | bytes 2097152 | tf_op jit(solution)/shard_map/slice | solution.py:110
  64.3 2.9 %pad_maximum_fusion.1 = bf16[32,64,8,2,16]{0,4,1,3,2:T(8,128)(2,1)} fusion(bf16[32,64,8,1,16]{0,4,1,3,2:T(8,128)(2,1)S(1)} %get-tuple-element.18, bf16[32,64,8,1,16]{0,4,1,3,2:T(8,128)(2,1)S(1)} %get-tuple-element.17), kind=kLoop, calls=%fused_computation.2 | loop fusion | flops 524288 | bytes 2097152 | tf_op jit(solution)/shard_map/stack | solution.py:110
  67.3 7.4 %copy.23 = bf16[32,64,8,2,16]{1,4,3,2,0:T(8,128)(2,1)} copy(bf16[32,64,8,2,16]{0,4,1,3,2:T(8,128)(2,1)} %pad_maximum_fusion.1) | data formatting | bytes 2097152 | tf_op jit(solution)/shard_map/stack | solution.py:110
  74.6 4.7 %pad_maximum_fusion.2 = bf16[32,2,64,256]{2,3,0,1:T(8,128)(2,1)} fusion(bf16[32,1,64,256]{2,3,0,1:T(8,128)(2,1)} %bitcast.46, bf16[32,1,64,256]{2,3,0,1:T(8,128)(2,1)S(1)} %bitcast.44), kind=kLoop, calls=%fused_computation.3 | loop fusion | flops 1048576 | bytes 4194304 | tf_op jit(solution)/shard_map/stack | solution.py:111
  79.3 3.5 %copy.24 = bf16[32,2,64,256]{3,2,1,0:T(8,128)(2,1)S(1)} copy(bf16[32,2,64,256]{2,3,0,1:T(8,128)(2,1)} %pad_maximum_fusion.2) | data formatting | bytes 4194304 | tf_op jit(solution)/shard_map/stack | solution.py:111
  82.9 92.8 %all-gather.2.cloned.1.call-done.rhs_ref = bf16[32,1024,256]{2,1,0:T(8,128)(2,1)} async-done(((bf16[32,64,256]{2,1,0:T(8,128)(2,1)}), bf16[32,1024,256]{2,1,0:T(8,128)(2,1)}) %all-gather.2.cloned.1.call-update) | async-done | bytes 16777232 | tf_op jit(solution)/shard_map/all_gather | solution.py:112
  175.7 16.3 %shard_map.37 = f32[32,2,64,1024]{3,2,1,0:T(8,128)} custom-call(bf16[32,128,256]{2,1,0:T(8,128)(2,1)S(1)} %bitcast.38, bf16[32,1024,256]{2,1,0:T(8,128)(2,1)} %all-gather.2.cloned.1.call-done.rhs_ref), custom_call_target="tpu_custom_call" | custom-call | tf_op jit(solution)/shard_map/pallas_call | solution.py:55
  (3 shorter events, 0.0 us)
Async XLA Ops:
  6.5 169.2 %all-gather.2.cloned.1.call-start = ((), (), s32[]{:S(2)}) async-start(), calls=%async_computation.1 | async-start | bytes 17825792 | tf_op jit(solution)/shard_map/all_gather | solution.py:112
  15.1 7.2 %slice-start = ((s8[8388608]{0:T(1024)(128)(4,1)}), s8[4194304]{0:T(1024)(128)(4,1)S(1)}, s32[]{:S(2)}) async-start(s8[8388608]{0:T(1024)(128)(4,1)} %bitcast.39), calls=%async_computation.2 | async-start | bytes 8388608
  17.2 17.0 %collective-permute-start.1 = (f32[512,256]{1,0:T(8,128)}, f32[512,256]{1,0:T(8,128)S(1)}, u32[]{:S(2)}, u32[]{:S(2)}) collective-permute-start(f32[512,256]{1,0:T(8,128)} %fusion.2), channel_id=1, source_target_pairs={{8,0},{16,8},{24,16},{32,24},{40,32},{48,40},{56,48},{64,56},{72,6... | collective-permute-start | bytes 1572872 | tf_op jit(solution)/shard_map/ppermute | solution.py:95
  18.6 3.7 %slice-start.1 = ((s8[8388608]{0:T(1024)(128)(4,1)}), s8[4194304]{0:T(1024)(128)(4,1)S(1)}, s32[]{:S(2)}) async-start(s8[8388608]{0:T(1024)(128)(4,1)} %bitcast.39), calls=%async_computation.3 | async-start | bytes 8388608
  20.7 13.6 %collective-permute-start = (f32[512,256]{1,0:T(8,128)}, f32[512,256]{1,0:T(8,128)S(1)}, u32[]{:S(2)}, u32[]{:S(2)}) collective-permute-start(f32[512,256]{1,0:T(8,128)} %fusion.3), channel_id=1, source_target_pairs={{0,8},{8,16},{16,24},{24,32},{32,40},{40,48},{48,56},{56,64},{64,7... | collective-permute-start | bytes 1572872 | tf_op jit(solution)/shard_map/ppermute | solution.py:94
Sparse Core Ops, SparseCore 0:
  61.8 113.8 all-gather.1

commit v13 on v11

--- a/solution.py
+++ b/solution.py
@@ -10,7 +10,6 @@
 BLOCK_CHUNKS = 1
 AZ = ("xh", "z", "core")
 TM = ("xl", "y")
-CHIPS = ("xh", "z")
 
 
 def dft_table(length, freqs):
@@ -79,27 +78,16 @@
             [inner[:, :run] + from_prev, inner[:, run:-run], inner[:, -run:] + from_next], axis=1
         ).astype(jnp.bfloat16)
         spectra = spectra.reshape(2, n_tm, fl, cycles * sector * nb).transpose(1, 0, 2, 3)
-        shared = lax.all_to_all(spectra, TM, 0, 0, tiled=True)
+        shared = spectra.reshape(2, n_tm // 2, *spectra.shape[1:])
+        shared = lax.all_to_all(shared, "y", 1, 1, tiled=True)
+        shared = lax.all_to_all(shared, "xl", 0, 0, tiled=True).reshape(spectra.shape)
         x = shared.reshape(n_tm, 2, fl, local_rows, nb).transpose(2, 3, 0, 1, 4)
         x = x.reshape(fl, local_rows, n_tm, 2, nb)
         rows = x.reshape(fl, local_rows, n_tm * 2 * nb)
         turned = jnp.stack([x[:, :, :, 1], -x[:, :, :, 0]], 3).reshape(rows.shape)
-        lhs = jnp.stack([rows, turned], 1).reshape(fl, 2, local_rows, n_tm, 2, nb)
-        core = lax.axis_index("core")
-        swap = [(0, 1), (1, 0)]
-        x = x.reshape(fl, local_rows, n_tm, 2, nb)
-        mine = lax.dynamic_index_in_dim(x, core, 3, keepdims=False)
-        theirs = lax.ppermute(lax.dynamic_index_in_dim(x, 1 - core, 3, keepdims=False), "core", swap)
-        chip = jnp.where(
-            core == 0, jnp.concatenate([mine, theirs], 1), jnp.concatenate([theirs, mine], 1)
-        ).reshape(fl, 2 * local_rows, n_tm * nb)
-        own_cols = lax.all_gather(chip, CHIPS, axis=1, tiled=True)
-        other_cols = lax.ppermute(own_cols, "core", swap)
-        l_own = lax.dynamic_index_in_dim(lhs, core, 4, keepdims=False).reshape(fl, 2, local_rows, -1)
-        l_other = lax.dynamic_index_in_dim(lhs, 1 - core, 4, keepdims=False).reshape(fl, 2, local_rows, -1)
-        part = jnp.einsum(
-            "fcqk,fpk->fcqp", l_own, own_cols, preferred_element_type=jnp.float32
-        ) + jnp.einsum("fcqk,fpk->fcqp", l_other, other_cols, preferred_element_type=jnp.float32)
+        lhs = jnp.stack([rows, turned], 1)
+        columns = lax.all_gather(rows, AZ, axis=1, tiled=True)
+        part = jnp.einsum("fcqk,fpk->fcqp", lhs, columns, preferred_element_type=jnp.float32)
         result = part if result is None else result + part
     return result * (1.0 / (n_tm * blocks))
 

time: 241 us -> 212 us (0.88)
  blocking collectives: 0 us -> 25.3 us
  matrix products: 37.2 us -> 21.6 us
  starting transfers between devices: 15.4 us -> 3.02 us
  waiting for transfers between devices: 116 us -> 104 us
  local copies, waits for them, and re-layouts: 34.4 us -> 24.7 us
  other arithmetic: 23.9 us -> 19.4 us
    all_to_all x0 -> x2, blocking collectives: none -> 25.3 us  [the longest x1 13.7 us: shards(): shared = lax.all_to_all(shared, 'y', 1, 1, tiled=True)]
    dynamic_slice x4 -> x0, local copies, waits for them, and re-layouts: 21.1 us -> none  [the longest x1 7.39 us: shards(): lax.dynamic_index_in_dim(lhs, 1 - core, 4, keepdims=False)]
    dot_general x2 -> x1, matrix products: 28.5 us -> 12.9 us  [shards(): jnp.einsum('fcqk,fpk->fcqp', lhs, columns, preferred_element_type=jnp.flo...]
    another operation x0 -> x3, local copies, waits for them, and re-layouts: none -> 10.9 us  [the longest x1 7.35 us: shards(): turned = jnp.stack([x[:, :, :, 1], -x[:, :, :, 0]], 3).reshape(rows.shape)]
    all_to_all x1 -> x0, waiting for transfers between devices: 9.87 us -> none  [shards(): shared = lax.all_to_all(spectra, TM, 0, 0, tiled=True)]
    ppermute x2 -> x0, starting transfers between devices: 7.23 us -> none  [the longest x1 5.83 us: shards(): lax.ppermute(lax.dynamic_index_in_dim(x, 1 - core, 3, keepdims=False), 'c...]
    transpose x0 -> x1, local copies, waits for them, and re-layouts: none -> 6.64 us  [shards(): x = shared.reshape(n_tm, 2, fl, local_rows, nb).transpose(2, 3, 0, 1, 4)]
    all_to_all x1 -> x0, starting transfers between devices: 5.12 us -> none  [shards(): shared = lax.all_to_all(spectra, TM, 0, 0, tiled=True)]
  transfers between devices with their start and end apart: 6 -> 3, of which waited for: 2 -> 1; matrix products, arithmetic and copies ran while one was open for 21% -> 14% of each run, Pallas kernels for 0% -> 0%
where the time goes in v13:
time: 212 us; the launch traced here: 211 us
  waiting for transfers between devices  104 us (49%)
  blocking collectives  25.3 us (12%)
  local copies, waits for them, and re-layouts  24.7 us (12%)
  matrix products  21.6 us (10%)
  other arithmetic  19.4 us (9%)
  between operations  13.6 us (6%)
  starting transfers between devices  3.02 us (1%)
    all_gather x1, waiting for transfers between devices, shards(): columns = lax.all_gather(rows, AZ, axis=1, tiled=True)  104 us
    all_to_all x1, blocking collectives, shards(): shared = lax.all_to_all(shared, 'y', 1, 1, tiled=True)  13.7 us
    dot_general x1, matrix products, shards(): jnp.einsum('fcqk,fpk->fcqp', lhs, columns, preferred_element_type=jnp.flo...  12.9 us
    all_to_all x1, blocking collectives, shards(): lax.all_to_all(shared, 'xl', 0, 0, tiled=True).reshape(spectra.shape)  11.6 us
    dot_general x3, matrix products, transform(): lax.dot_general(table, rows, (((0,), (1,)), ((), ())), preferred_element_...  8.74 us
    convert_element_type x2, other arithmetic, transform(): rows = v.astype(jnp.bfloat16).reshape(-1, length)  8.66 us
    another operation x1, local copies, waits for them, and re-layouts, shards(): turned = jnp.stack([x[:, :, :, 1], -x[:, :, :, 0]], 3).reshape(rows.shape)  7.35 us
    transpose x1, local copies, waits for them, and re-layouts, shards(): x = shared.reshape(n_tm, 2, fl, local_rows, nb).transpose(2, 3, 0, 1, 4)  6.64 us
  transfers between devices with their start and end apart: 3, of which 1 were waited for; matrix products, arithmetic and copies ran while one was open for 14% of the time, Pallas kernels for 0%

profile of v13, /device:TPU:1, one launch (start us, length us, event | category | flops | bytes accessed | tf_op | source)
XLA Modules:
  0.0 211.2 jit_solution(13463029156152683097)
XLA Ops:
  6.5 0.0 all-gather.2.cloned.1.call-start
  6.5 0.1 fusion.27
  6.6 0.1 subtract_multiply_fusion
  6.7 0.3 fusion.23
  7.0 0.3 fusion.25
  7.3 0.7 select_add_fusion.2
  8.0 0.1 broadcast_in_dim.23
  8.1 0.2 copy.43
  8.3 0.1 broadcast_in_dim.27
  8.4 0.2 copy.45
  8.6 3.1 %multiply_convert_fusion.1 = (bf16[16,1,16,4096]{3,2,1,0:T(8,128)(2,1)S(1)}, bf16[16,1,16,4096]{3,2,1,0:T(8,128)(2,1)S(1)}) fusion(bf16[16,4,16,4096]{3,2,1,0:T(8,128)(2,1)} %param.3, f32[16,4096]{1,0:T(8,128)S(1)} %bitcast.54, f32[16,4096]{1,0:T(8,128)S(1)} %bitcast.56), kind=kLoop, calls=%fused_computation.11 | loop fusion | flops 6291456 | bytes 8912896 | tf_op jit(solution)/shard_map/convert_element_type | solution.py:62
  11.7 1.2 multiply_subtract_fusion
  12.9 2.2 %fusion.4 = (bf16[4096,256]{1,0:T(8,128)(2,1)S(1)}, bf16[4096,256]{1,0:T(8,128)(2,1)S(1)}) fusion(f32[64,64,256]{2,1,0:T(8,128)S(1)} %get-tuple-element.22, f32[4096]{0:T(1024)S(1)} %fusion.27, f32[64,64,256]{2,1,0:T(8,128)S(1)} %get-tuple-element.21, f32[4096]{0:T(1024)S(1)} %subtract_multiply_fusion), kind=kLoop, calls=%fused_computation.7 | loop fusion | flops 4194304 | bytes 12615680 | tf_op jit(solution)/shard_map/convert.8
  15.1 0.0 slice-start
  15.1 2.1 fusion.9
  17.2 1.4 collective-permute-start.1
  18.6 0.0 slice-start.1
  18.6 2.1 fusion.10
  20.7 1.6 collective-permute-start
  22.3 0.0 slice-done
  22.4 0.0 slice-done.1
  22.4 1.5 fusion.32
  23.9 0.1 broadcast_in_dim.25
  24.0 0.2 copy.44
  24.1 5.5 %add_convert_fusion = bf16[16,4,16,4096]{3,2,0,1:T(8,128)(2,1)S(1)} fusion(f32[16,4096]{1,0:T(8,128)S(1)} %bitcast.57, f32[16,4096]{1,0:T(8,128)S(1)} %bitcast.61, f32[16,4096]{1,0:T(8,128)S(1)} %bitcast.55, bf16[16,4,16,4096]{3,2,1,0:T(8,128)(2,1)S(1)} %bitcast.46, bf16[16,3,16,4096]{3,2,1,0:T(8,128)(2,1)S(1)} %get-tuple-element.15, ...), kind=kLoop, calls=%fused_computation.2 | loop fusion | flops 37748736 | bytes 30146560 | tf_op jit(solution)/shard_map/convert_element_type | solution.py:62
  29.6 4.5 %fusion.11 = f32[512,1024]{1,0:T(8,128)S(1)} fusion(bf16[1024,4096]{1,0:T(8,128)(2,1)S(1)} %bitcast.51, bf16[4096,256]{1,0:T(8,128)(2,1)S(1)} %get-tuple-element.30, bf16[4096,256]{1,0:T(8,128)(2,1)S(1)} %get-tuple-element.31), kind=kOutput, calls=%fused_computation.20 | convolution fusion | flops 4303355904 | bytes 14680064 | tf_op jit(solution)/shard_map/dot_general | solution.py:63
  34.2 0.1 slice.65
  34.3 0.0 collective-permute-done.1
  34.3 0.0 collective-permute-done
  34.3 0.2 fusion.13
  34.5 0.1 pad_maximum_fusion.5
  34.6 0.1 copy.31
  34.7 13.7 %all_to_all.10 = bf16[2,4,2,32,1024]{4,3,2,0,1:T(8,128)(2,1)S(1)} all-to-all(bf16[2,4,2,32,1024]{4,3,2,0,1:T(8,128)(2,1)S(1)} %copy.31), channel_id=1, replica_groups=mesh['xh'=2,'z'=4,'core'=2,'xl'=2,'y'=4] {'y'}, dimensions={1} | all-to-all | bytes 2097152 | tf_op jit(solution)/shard_map/all_to_all | solution.py:82
  48.4 0.1 copy.32
  48.5 11.6 %all_to_all.11 = bf16[2,4,2,32,1024]{4,3,2,1,0:T(8,128)(2,1)S(1)} all-to-all(bf16[2,4,2,32,1024]{4,3,2,1,0:T(8,128)(2,1)S(1)} %copy.32), channel_id=1, replica_groups=mesh['xh'=2,'z'=4,'core'=2,'xl'=2,'y'=4] {'xl'}, dimensions={0} | all-to-all | bytes 2097152 | tf_op jit(solution)/shard_map/all_to_all | solution.py:83
  60.1 3.1 %copy.33 = bf16[2,4,2,32,1024]{3,4,2,1,0:T(8,128)(2,1)} copy(bf16[2,4,2,32,1024]{4,3,2,1,0:T(8,128)(2,1)S(1)} %all_to_all.11) | data formatting | bytes 2097152 | tf_op jit(solution)/shard_map/all_to_all | solution.py:83
  63.1 6.6 %copy.34 = bf16[32,64,8,2,16]{1,4,3,2,0:T(8,128)(2,1)S(1)} copy(bf16[32,64,8,2,16]{0,4,1,3,2:T(8,128)(2,1)} %bitcast.47) | data formatting | bytes 2097152 | tf_op jit(solution)/shard_map/transpose | solution.py:84
  69.8 1.6 copy.39
  71.4 0.0 all-gather.2.cloned.1.call-update
  71.4 2.6 %fusion.33 = (bf16[32,64,8,1,16]{0,4,1,3,2:T(8,128)(2,1)S(1)}, bf16[32,64,8,1,16]{0,4,1,3,2:T(8,128)(2,1)S(1)}) fusion(bf16[32,64,8,2,16]{0,4,1,3,2:T(8,128)(2,1)} %bitcast.48), kind=kLoop, calls=%fused_computation.60 | loop fusion | flops 262144 | bytes 2097152 | tf_op jit(solution)/shard_map/slice | solution.py:87
  74.1 2.9 %pad_maximum_fusion.1 = bf16[32,64,8,2,16]{0,4,1,3,2:T(8,128)(2,1)} fusion(bf16[32,64,8,1,16]{0,4,1,3,2:T(8,128)(2,1)S(1)} %get-tuple-element.18, bf16[32,64,8,1,16]{0,4,1,3,2:T(8,128)(2,1)S(1)} %get-tuple-element.17), kind=kLoop, calls=%fused_computation.5 | loop fusion | flops 524288 | bytes 2097152 | tf_op jit(solution)/shard_map/stack | solution.py:87
  77.0 7.4 %copy.35 = bf16[32,64,8,2,16]{1,4,3,2,0:T(8,128)(2,1)} copy(bf16[32,64,8,2,16]{0,4,1,3,2:T(8,128)(2,1)} %pad_maximum_fusion.1) | data formatting | bytes 2097152 | tf_op jit(solution)/shard_map/stack | solution.py:87
  84.4 1.9 copy.37
  86.3 1.6 copy.36
  87.9 103.5 %all-gather.2.cloned.1.call-done = bf16[32,1024,256]{2,1,0:T(8,128)(2,1)} async-done(((bf16[32,64,256]{2,1,0:T(8,128)(2,1)}), bf16[32,1024,256]{2,1,0:T(8,128)(2,1)}) %all-gather.2.cloned.1.call-update) | async-done | bytes 16777232 | tf_op jit(solution)/shard_map/all_gather | solution.py:89
  191.4 12.9 %broadcast_multiply_fusion = f32[32,2,64,1024]{3,2,1,0:T(8,128)} fusion(bf16[32,1024,256]{2,1,0:T(8,128)(2,1)} %all-gather.2.cloned.1.call-done, bf16[32,1,64,256]{3,2,1,0:T(8,128)(2,1)S(1)} %copy.37, bf16[32,1,64,256]{3,2,1,0:T(8,128)(2,1)} %copy.36), kind=kOutput, calls=%fused_computation.3 | convolution fusion | flops 2152726528 | bytes 35651584 | tf_op jit(solution)/shard_map/fcqk,fpk->fcqp/dot_general | solution.py:90
  (3 shorter events, 0.0 us)
Async XLA Ops:
  6.5 184.9 %all-gather.2.cloned.1.call-start = ((), (), s32[]{:S(2)}) async-start(), calls=%async_computation.2 | async-start | bytes 17825792 | tf_op jit(solution)/shard_map/all_gather | solution.py:89
  15.1 7.2 %slice-start = ((s8[8388608]{0:T(1024)(128)(4,1)}), s8[4194304]{0:T(1024)(128)(4,1)S(1)}, s32[]{:S(2)}) async-start(s8[8388608]{0:T(1024)(128)(4,1)} %bitcast.45), calls=%async_computation.3 | async-start | bytes 8388608
  17.2 17.0 %collective-permute-start.1 = (f32[512,256]{1,0:T(8,128)}, f32[512,256]{1,0:T(8,128)S(1)}, u32[]{:S(2)}, u32[]{:S(2)}) collective-permute-start(f32[512,256]{1,0:T(8,128)} %fusion.9), channel_id=1, source_target_pairs={{8,0},{16,8},{24,16},{32,24},{40,32},{48,40},{56,48},{64,56},{72,6... | collective-permute-start | bytes 1572872 | tf_op jit(solution)/shard_map/ppermute | solution.py:70
  18.6 3.7 %slice-start.1 = ((s8[8388608]{0:T(1024)(128)(4,1)}), s8[4194304]{0:T(1024)(128)(4,1)S(1)}, s32[]{:S(2)}) async-start(s8[8388608]{0:T(1024)(128)(4,1)} %bitcast.45), calls=%async_computation.4 | async-start | bytes 8388608
  20.7 13.6 %collective-permute-start = (f32[512,256]{1,0:T(8,128)}, f32[512,256]{1,0:T(8,128)S(1)}, u32[]{:S(2)}, u32[]{:S(2)}) collective-permute-start(f32[512,256]{1,0:T(8,128)} %fusion.10), channel_id=1, source_target_pairs={{0,8},{8,16},{16,24},{24,32},{32,40},{40,48},{48,56},{56,64},{64,7... | collective-permute-start | bytes 1572872 | tf_op jit(solution)/shard_map/ppermute | solution.py:69
Sparse Core Ops, SparseCore 0:
  71.6 119.8 all-gather.1

commit v14 on v10

--- a/solution.py
+++ b/solution.py
@@ -55,24 +55,42 @@
         block = pressure[:, :, j * nb : (j + 1) * nb]
         weights = all_weights[:, :, :, j * nb : (j + 1) * nb]
 
-        def transform(v):
-            rows = v.astype(jnp.bfloat16).reshape(-1, length)
+        def transform(rows):
             return lax.dot_general(
-                table, rows, (((0,), (1,)), ((), ())), preferred_element_type=jnp.float32
+                table, rows.reshape(-1, length), (((0,), (1,)), ((), ())),
+                preferred_element_type=jnp.float32,
             )
 
-        to_next = transform(weights[0] * block[:, sector - 1 :].astype(jnp.float32))
-        to_prev = transform(weights[2] * block[:, :1].astype(jnp.float32))
+        def split(v):
+            hi = v.astype(jnp.bfloat16)
+            return hi, (v - hi.astype(jnp.float32)).astype(jnp.bfloat16)
+
+        def edge(v):
+            hi, lo = split(v)
+            both = transform(jnp.concatenate([hi, lo], 0))
+            return both[:, : both.shape[1] // 2] + both[:, both.shape[1] // 2 :]
+
+        to_next = edge(weights[0] * block[:, sector - 1 :].astype(jnp.float32))
+        to_prev = edge(weights[2] * block[:, :1].astype(jnp.float32))
         from_prev = lax.ppermute(to_next, "az", forward)
         from_next = lax.ppermute(to_prev, "az", backward)
         zero = jnp.zeros_like(block[:, :1])
         prev = jnp.concatenate([zero, block[:, :-1]], axis=1).astype(jnp.float32)
         nxt = jnp.concatenate([block[:, 1:], zero], axis=1).astype(jnp.float32)
         total = weights[0] * prev + weights[1] * block.astype(jnp.float32) + weights[2] * nxt
-        inner = lax.optimization_barrier(transform(total.transpose(1, 0, 2, 3)))
+        total = total.transpose(1, 0, 2, 3)
+        hi, lo = split(total)
+        rest = jnp.concatenate([lo[:1], lo[-1:]], 0)
+        inner = lax.optimization_barrier(transform(jnp.concatenate([hi, rest], 0)))
         run = cycles * nb
+        body = sector * run
         spectra = jnp.concatenate(
-            [inner[:, :run] + from_prev, inner[:, run:-run], inner[:, -run:] + from_next], axis=1
+            [
+                inner[:, :run] + inner[:, body : body + run] + from_prev,
+                inner[:, run : body - run],
+                inner[:, body - run : body] + inner[:, body + run :] + from_next,
+            ],
+            axis=1,
         ).astype(jnp.bfloat16)
         spectra = spectra.reshape(2, n_tm, fl, cycles * sector * nb).transpose(1, 0, 2, 3)
         shared = lax.all_to_all(spectra, "tm", 0, 0, tiled=True)

time: 196 us -> 224 us (1.14)
  other arithmetic: 19.4 us -> 39.1 us
  matrix products: 21.6 us -> 27.2 us
  local copies, waits for them, and re-layouts: 24.7 us -> 27.4 us
    concatenate x0 -> x2, other arithmetic: none -> 10.3 us  [the longest x1 9.52 us: shards(): inner = lax.optimization_barrier(transform(jnp.concatenate([hi, rest], 0)))]
    convert_element_type x2 -> x3, other arithmetic: 8.66 us -> 15.1 us  [the longest x2 8.51 us: split(): hi = v.astype(jnp.bfloat16)]
    dot_general x3, matrix products: 8.74 us -> 14.4 us  [transform(): lax.dot_general(table, rows.reshape(-1, length), (((0,), (1,)), ((), ()))...]
    slice x1 -> x2, local copies, waits for them, and re-layouts: 0.07 us -> 2.77 us  [the longest x1 2.71 us: shards(): rest = jnp.concatenate([lo[:1], lo[-1:]], 0)]
  transfers between devices with their start and end apart: 3 -> 3, of which waited for: 1 -> 1; matrix products, arithmetic and copies ran while one was open for 16% -> 25% of each run, Pallas kernels for 0% -> 0%
where the time goes in v14:
time: 224 us; the launch traced here: 223 us
  waiting for transfers between devices  97 us (43%)
  other arithmetic  39.1 us (17%)
  local copies, waits for them, and re-layouts  27.4 us (12%)
  matrix products  27.2 us (12%)
  blocking collectives  16.1 us (7%)
  between operations  13.6 us (6%)
  starting transfers between devices  3.02 us (1%)
    all_gather x1, waiting for transfers between devices, shards(): columns = lax.all_gather(rows, 'az', axis=1, tiled=True)  96.9 us
    all_to_all x1, blocking collectives, shards(): shared = lax.all_to_all(spectra, 'tm', 0, 0, tiled=True)  16.1 us
    dot_general x3, matrix products, transform(): lax.dot_general(table, rows.reshape(-1, length), (((0,), (1,)), ((), ()))...  14.4 us
    dot_general x1, matrix products, shards(): jnp.einsum('fcqk,fpk->fcqp', lhs, columns, preferred_element_type=jnp.flo...  12.9 us
    concatenate x1, other arithmetic, shards(): inner = lax.optimization_barrier(transform(jnp.concatenate([hi, rest], 0)))  9.52 us
    convert_element_type x2, other arithmetic, split(): hi = v.astype(jnp.bfloat16)  8.51 us
    another operation x1, local copies, waits for them, and re-layouts, shards(): turned = jnp.stack([x[:, :, :, 1], -x[:, :, :, 0]], 3).reshape(rows.shape)  7.36 us
    transpose x1, local copies, waits for them, and re-layouts, shards(): x = shared.reshape(n_tm, 2, fl, local_rows, nb).transpose(2, 3, 0, 1, 4)  6.64 us
  transfers between devices with their start and end apart: 3, of which 1 were waited for; matrix products, arithmetic and copies ran while one was open for 25% of the time, Pallas kernels for 0%

profile of v14, /device:TPU:1, one launch (start us, length us, event | category | flops | bytes accessed | tf_op | source)
XLA Modules:
  0.0 223.5 jit_solution(2959138935023782733)
XLA Ops:
  6.5 0.0 all-gather.2.cloned.1.call-start
  6.5 0.1 fusion.32
  6.6 0.1 subtract_multiply_fusion
  6.7 0.3 fusion.28
  7.0 0.3 fusion.30
  7.3 0.7 select_add_fusion.2
  8.0 0.1 broadcast_in_dim.23
  8.1 0.2 copy.29
  8.3 0.1 broadcast_in_dim.27
  8.4 0.2 copy.31
  8.6 3.0 %fusion.8 = (bf16[16,1,16,4096]{3,2,1,0:T(8,128)(2,1)S(1)}, bf16[16,1,16,4096]{3,2,1,0:T(8,128)(2,1)S(1)}, bf16[16,1,16,4096]{3,2,1,0:T(8,128)(2,1)S(1)}, bf16[16,1,16,4096]{3,2,1,0:T(8,128)(2,1)S(1)}) fusion(f32[16,4096]{1,0:T(8,128)S(1)} %bitcast.57, bf16[16,4,16,4096]{3,2,1,0:T(8,128)(2,1)} %param.3, f32[16,4096]{1,0:T(8,128)S(1)} %bitcast.60), kind=kLoop, calls=%fused_computation.21 | loop fusion | flops 12582912 | bytes 13107200 | tf_op jit(solution)/shard_map/convert_element_type | solution.py:65
  11.6 1.2 multiply_subtract_fusion
  12.8 2.2 fusion.5
  15.0 0.0 copy-start
  15.0 0.8 pad_maximum_fusion.2
  15.8 2.4 %fusion.12 = f32[512,512]{1,0:T(8,128)S(1)} fusion(bf16[512,4096]{1,0:T(8,128)(2,1)S(1)} %bitcast.64, bf16[4096,256]{1,0:T(8,128)(2,1)S(1)} %get-tuple-element.38, bf16[4096,256]{1,0:T(8,128)(2,1)S(1)} %get-tuple-element.39), kind=kOutput, calls=%fused_computation.28 | convolution fusion | flops 2155872256 | bytes 9437184 | tf_op jit(solution)/shard_map/dot_general | solution.py:59
  18.2 0.9 slice_add_fusion
  19.1 1.4 collective-permute-start.1
  20.4 0.0 slice-start
  20.4 0.0 copy-done
  20.4 0.0 slice-start.1
  20.4 2.4 %fusion.13 = f32[512,512]{1,0:T(8,128)S(1)} fusion(bf16[512,4096]{1,0:T(8,128)(2,1)S(1)} %bitcast.63, bf16[4096,256]{1,0:T(8,128)(2,1)S(1)} %get-tuple-element.38, bf16[4096,256]{1,0:T(8,128)(2,1)S(1)} %get-tuple-element.39), kind=kOutput, calls=%fused_computation.29 | convolution fusion | flops 2155872256 | bytes 9437184 | tf_op jit(solution)/shard_map/dot_general | solution.py:59
  22.9 0.9 slice_add_fusion.2
  23.7 1.6 collective-permute-start
  25.4 0.0 slice-done
  25.4 0.0 slice-done.1
  25.4 1.5 fusion.38
  26.9 0.1 broadcast_in_dim.25
  27.0 0.2 copy.30
  27.1 5.5 %bitcast_convert_fusion = bf16[4,16,16,4096]{3,2,1,0:T(8,128)(2,1)S(1)} fusion(f32[16,4096]{1,0:T(8,128)S(1)} %bitcast.61, f32[16,4096]{1,0:T(8,128)S(1)} %bitcast.65, f32[16,4096]{1,0:T(8,128)S(1)} %bitcast.58, bf16[16,4,16,4096]{3,2,1,0:T(8,128)(2,1)S(1)} %bitcast.50, bf16[16,3,16,4096]{3,2,1,0:T(8,128)(2,1)S(1)} %get-tuple-element.21, ...), kind=kLoop, calls=%fused_computation.3 | loop fusion | flops 37748736 | bytes 30146560 | tf_op jit(solution)/shard_map/convert_element_type | solution.py:65
  32.7 6.6 %fusion.2 = bf16[4,16,16,4096]{3,2,1,0:T(8,128)(2,1)} fusion(f32[16,4096]{1,0:T(8,128)S(1)} %bitcast.62, f32[16,4096]{1,0:T(8,128)S(1)} %bitcast.66, f32[16,4096]{1,0:T(8,128)S(1)} %bitcast.59, bf16[16,4,16,4096]{3,2,1,0:T(8,128)(2,1)S(1)} %bitcast.50, bf16[16,3,16,4096]{3,2,1,0:T(8,128)(2,1)S(1)} %get-tuple-element.21, ...), kind=kLoop, calls=%fused_computation.4 | loop fusion | flops 50331648 | bytes 30146560 | tf_op jit(solution)/shard_map/convert_element_type | solution.py:66
  39.3 2.7 %fusion.37 = (bf16[1,16,16,4096]{3,2,1,0:T(8,128)(2,1)S(1)}, bf16[1,16,16,4096]{3,2,1,0:T(8,128)(2,1)S(1)}) fusion(bf16[4,16,16,4096]{3,2,1,0:T(8,128)(2,1)} %fusion.2), kind=kLoop, calls=%fused_computation.74 | loop fusion | bytes 8388608 | tf_op jit(solution)/shard_map/slice | solution.py:83
  42.0 0.0 copy-start.1
  42.0 9.5 %pad_maximum_fusion = bf16[6,16,16,4096]{3,2,1,0:T(8,128)(2,1)} fusion(bf16[1,16,16,4096]{3,2,1,0:T(8,128)(2,1)S(1)} %get-tuple-element.20, bf16[1,16,16,4096]{3,2,1,0:T(8,128)(2,1)S(1)} %get-tuple-element.19, bf16[4,16,16,4096]{3,2,1,0:T(8,128)(2,1)S(1)} %bitcast_convert_fusion), kind=kLoop, calls=%fused_computation.6 | loop fusion | flops 12582912 | bytes 25165824 | tf_op jit(solution)/shard_map/concatenate | solution.py:84
  51.5 0.0 copy-done.1
  51.5 9.5 %fusion.14 = f32[512,1536]{1,0:T(8,128)S(1)} fusion(bf16[1536,4096]{1,0:T(8,128)(2,1)} %bitcast.55, bf16[4096,256]{1,0:T(8,128)(2,1)S(1)} %get-tuple-element.38, bf16[4096,256]{1,0:T(8,128)(2,1)S(1)} %copy-done.1), kind=kOutput, calls=%fused_computation.30 | convolution fusion | flops 6450839552 | bytes 19922944 | tf_op jit(solution)/shard_map/dot_general | solution.py:59
  61.0 0.1 slice.121
  61.1 0.0 collective-permute-done.1
  61.1 0.0 collective-permute-done
  61.1 1.4 fusion.18
  62.5 0.1 copy_bitcast_fusion
  62.7 16.1 %all_to_all.5 = bf16[8,2,32,1024]{3,2,1,0:T(8,128)(2,1)S(1)} all-to-all(bf16[8,2,32,1024]{3,2,1,0:T(8,128)(2,1)S(1)} %copy_bitcast_fusion), channel_id=1, replica_groups=mesh['az'=16,'tm'=8] {'tm'}, dimensions={0} | all-to-all | bytes 2097152 | tf_op jit(solution)/shard_map/all_to_all | solution.py:96
  78.8 3.1 %copy.21 = bf16[8,2,32,1024]{2,3,1,0:T(8,128)(2,1)} copy(bf16[8,2,32,1024]{3,2,1,0:T(8,128)(2,1)S(1)} %all_to_all.5) | data formatting | bytes 2097152 | tf_op jit(solution)/shard_map/all_to_all | solution.py:96
  81.9 6.6 %copy.22 = bf16[32,64,8,2,16]{1,4,3,2,0:T(8,128)(2,1)S(1)} copy(bf16[32,64,8,2,16]{0,4,1,3,2:T(8,128)(2,1)} %bitcast.51) | data formatting | bytes 2097152 | tf_op jit(solution)/shard_map/transpose | solution.py:97
  88.5 1.6 copy.27
  90.1 0.0 all-gather.2.cloned.1.call-update
  90.2 2.6 %fusion.39 = (bf16[32,64,8,1,16]{0,4,1,3,2:T(8,128)(2,1)S(1)}, bf16[32,64,8,1,16]{0,4,1,3,2:T(8,128)(2,1)S(1)}) fusion(bf16[32,64,8,2,16]{0,4,1,3,2:T(8,128)(2,1)} %bitcast.52), kind=kLoop, calls=%fused_computation.76 | loop fusion | flops 262144 | bytes 2097152 | tf_op jit(solution)/shard_map/slice | solution.py:100
  92.8 2.9 %pad_maximum_fusion.4 = bf16[32,64,8,2,16]{0,4,1,3,2:T(8,128)(2,1)} fusion(bf16[32,64,8,1,16]{0,4,1,3,2:T(8,128)(2,1)S(1)} %get-tuple-element.24, bf16[32,64,8,1,16]{0,4,1,3,2:T(8,128)(2,1)S(1)} %get-tuple-element.23), kind=kLoop, calls=%fused_computation.11 | loop fusion | flops 524288 | bytes 2097152 | tf_op jit(solution)/shard_map/stack | solution.py:100
  95.7 7.4 %copy.23 = bf16[32,64,8,2,16]{1,4,3,2,0:T(8,128)(2,1)} copy(bf16[32,64,8,2,16]{0,4,1,3,2:T(8,128)(2,1)} %pad_maximum_fusion.4) | data formatting | bytes 2097152 | tf_op jit(solution)/shard_map/stack | solution.py:100
  103.1 2.1 copy.25
  105.2 1.6 copy.24
  106.8 96.9 %all-gather.2.cloned.1.call-done = bf16[32,1024,256]{2,1,0:T(8,128)(2,1)} async-done(((bf16[32,64,256]{2,1,0:T(8,128)(2,1)}), bf16[32,1024,256]{2,1,0:T(8,128)(2,1)}) %all-gather.2.cloned.1.call-update) | async-done | bytes 16777232 | tf_op jit(solution)/shard_map/all_gather | solution.py:102
  203.8 12.9 %broadcast_multiply_fusion = f32[32,2,64,1024]{3,2,1,0:T(8,128)} fusion(bf16[32,1024,256]{2,1,0:T(8,128)(2,1)} %all-gather.2.cloned.1.call-done, bf16[32,1,64,256]{3,2,1,0:T(8,128)(2,1)S(1)} %copy.25, bf16[32,1,64,256]{3,2,1,0:T(8,128)(2,1)} %copy.24), kind=kOutput, calls=%fused_computation.7 | convolution fusion | flops 2152726528 | bytes 35651584 | tf_op jit(solution)/shard_map/fcqk,fpk->fcqp/dot_general | solution.py:103
  (3 shorter events, 0.0 us)
Async XLA Ops:
  6.5 197.2 %all-gather.2.cloned.1.call-start = ((), (), s32[]{:S(2)}) async-start(), calls=%async_computation.1 | async-start | bytes 17825792 | tf_op jit(solution)/shard_map/all_gather | solution.py:102
  15.0 5.5 %copy-start = (bf16[4096,256]{1,0:T(8,128)(2,1)}, bf16[4096,256]{1,0:T(8,128)(2,1)S(1)}, u32[]{:S(2)}) copy-start(bf16[4096,256]{1,0:T(8,128)(2,1)S(1)} %get-tuple-element.39) | copy-start | bytes 6291460
  19.1 42.1 %collective-permute-start.1 = (f32[512,256]{1,0:T(8,128)}, f32[512,256]{1,0:T(8,128)}, u32[]{:S(2)}, u32[]{:S(2)}) collective-permute-start(f32[512,256]{1,0:T(8,128)} %slice_add_fusion), channel_id=1, source_target_pairs={{8,0},{16,8},{24,16},{32,24},{40,32},{48,40},{56,48},{64,56},{72,6... | collective-permute-start | bytes 1572872 | tf_op jit(solution)/shard_map/ppermute | solution.py:76
  20.4 4.9 %slice-start = ((s8[8388608]{0:T(1024)(128)(4,1)}), s8[4194304]{0:T(1024)(128)(4,1)S(1)}, s32[]{:S(2)}) async-start(s8[8388608]{0:T(1024)(128)(4,1)} %bitcast.49), calls=%async_computation.2 | async-start | bytes 8388608
  20.4 4.9 %slice-start.1 = ((s8[8388608]{0:T(1024)(128)(4,1)}), s8[4194304]{0:T(1024)(128)(4,1)S(1)}, s32[]{:S(2)}) async-start(s8[8388608]{0:T(1024)(128)(4,1)} %bitcast.49), calls=%async_computation.3 | async-start | bytes 8388608
  23.7 37.4 %collective-permute-start = (f32[512,256]{1,0:T(8,128)}, f32[512,256]{1,0:T(8,128)}, u32[]{:S(2)}, u32[]{:S(2)}) collective-permute-start(f32[512,256]{1,0:T(8,128)} %slice_add_fusion.2), channel_id=1, source_target_pairs={{0,8},{8,16},{16,24},{24,32},{32,40},{40,48},{48,56},{56,64},{64,7... | collective-permute-start | bytes 1572872 | tf_op jit(solution)/shard_map/ppermute | solution.py:75
  42.0 9.5 %copy-start.1 = (bf16[4096,256]{1,0:T(8,128)(2,1)S(1)}, bf16[4096,256]{1,0:T(8,128)(2,1)}, u32[]{:S(2)}) copy-start(bf16[4096,256]{1,0:T(8,128)(2,1)} %copy-done) | copy-start | bytes 6291460
Sparse Core Ops, SparseCore 0:
  90.3 113.4 all-gather.1

commit v15 on v14

--- a/solution.py
+++ b/solution.py
@@ -79,17 +79,15 @@
         nxt = jnp.concatenate([block[:, 1:], zero], axis=1).astype(jnp.float32)
         total = weights[0] * prev + weights[1] * block.astype(jnp.float32) + weights[2] * nxt
         total = total.transpose(1, 0, 2, 3)
-        hi, lo = split(total)
-        rest = jnp.concatenate([lo[:1], lo[-1:]], 0)
-        inner = lax.optimization_barrier(transform(jnp.concatenate([hi, rest], 0)))
+        hi = total.astype(jnp.bfloat16)
+        first = split(total[:1])[1]
+        last = split(total[-1:])[1]
+        inner, low_first, low_last = lax.optimization_barrier(
+            (transform(hi), transform(first), transform(last))
+        )
         run = cycles * nb
-        body = sector * run
         spectra = jnp.concatenate(
-            [
-                inner[:, :run] + inner[:, body : body + run] + from_prev,
-                inner[:, run : body - run],
-                inner[:, body - run : body] + inner[:, body + run :] + from_next,
-            ],
+            [inner[:, :run] + low_first + from_prev, inner[:, run:-run], inner[:, -run:] + low_last + from_next],
             axis=1,
         ).astype(jnp.bfloat16)
         spectra = spectra.reshape(2, n_tm, fl, cycles * sector * nb).transpose(1, 0, 2, 3)

time: 224 us -> 216 us (0.964)
  other arithmetic: 39.1 us -> 29.4 us
    concatenate x1 -> x0, other arithmetic: 9.52 us -> none  [shards(): inner = lax.optimization_barrier(transform(jnp.concatenate([hi, rest], 0)))]
    convert_element_type x0 -> x1, other arithmetic: none -> 8.89 us  [shards(): hi = total.astype(jnp.bfloat16)]
    convert_element_type x2 -> x1, other arithmetic: 8.51 us -> 3 us  [split(): hi = v.astype(jnp.bfloat16)]
    convert_element_type x1, other arithmetic: 6.62 us -> 2.98 us  [split(): return (hi, (v - hi.astype(jnp.float32)).astype(jnp.bfloat16))]
    slice x2 -> x1, local copies, waits for them, and re-layouts: 2.77 us -> 0.07 us  [shards(): inner[:, run:-run]]
    dot_general x3 -> x5, matrix products: 14.4 us -> 15.8 us  [transform(): lax.dot_general(table, rows.reshape(-1, length), (((0,), (1,)), ((), ()))...]
  transfers between devices with their start and end apart: 3 -> 3, of which waited for: 1 -> 1; matrix products, arithmetic and copies ran while one was open for 25% -> 22% of each run, Pallas kernels for 0% -> 0%
where the time goes in v15:
time: 216 us; the launch traced here: 215 us
  waiting for transfers between devices  96.9 us (45%)
  other arithmetic  29.4 us (14%)
  matrix products  28.7 us (13%)
  local copies, waits for them, and re-layouts  27.7 us (13%)
  blocking collectives  16.1 us (7%)
  between operations  13.6 us (6%)
  starting transfers between devices  3.03 us (1%)
    all_gather x1, waiting for transfers between devices, shards(): columns = lax.all_gather(rows, 'az', axis=1, tiled=True)  96.9 us
    all_to_all x1, blocking collectives, shards(): shared = lax.all_to_all(spectra, 'tm', 0, 0, tiled=True)  16.1 us
    dot_general x5, matrix products, transform(): lax.dot_general(table, rows.reshape(-1, length), (((0,), (1,)), ((), ()))...  15.8 us
    dot_general x1, matrix products, shards(): jnp.einsum('fcqk,fpk->fcqp', lhs, columns, preferred_element_type=jnp.flo...  12.9 us
    convert_element_type x1, other arithmetic, shards(): hi = total.astype(jnp.bfloat16)  8.89 us
    another operation x1, local copies, waits for them, and re-layouts, shards(): turned = jnp.stack([x[:, :, :, 1], -x[:, :, :, 0]], 3).reshape(rows.shape)  7.41 us
    transpose x1, local copies, waits for them, and re-layouts, shards(): x = shared.reshape(n_tm, 2, fl, local_rows, nb).transpose(2, 3, 0, 1, 4)  6.64 us
  transfers between devices with their start and end apart: 3, of which 1 were waited for; matrix products, arithmetic and copies ran while one was open for 22% of the time, Pallas kernels for 0%

profile of v15, /device:TPU:1, one launch (start us, length us, event | category | flops | bytes accessed | tf_op | source)
XLA Modules:
  0.0 215.5 jit_solution(16596662808704839972)
XLA Ops:
  6.5 0.0 all-gather.2.cloned.1.call-start
  6.5 0.1 fusion.24
  6.6 0.1 subtract_multiply_fusion
  6.7 0.3 fusion.20
  7.0 0.3 fusion.22
  7.3 0.7 select_add_fusion.2
  8.0 0.1 broadcast_in_dim.23
  8.1 0.2 copy.29
  8.3 0.1 broadcast_in_dim.27
  8.4 0.2 copy.31
  8.6 3.0 %fusion.7 = (bf16[16,1,16,4096]{3,2,1,0:T(8,128)(2,1)S(1)}, bf16[16,1,16,4096]{3,2,1,0:T(8,128)(2,1)S(1)}, bf16[16,1,16,4096]{3,2,1,0:T(8,128)(2,1)S(1)}, bf16[16,1,16,4096]{3,2,1,0:T(8,128)(2,1)S(1)}) fusion(f32[16,4096]{1,0:T(8,128)S(1)} %bitcast.59, bf16[16,4,16,4096]{3,2,1,0:T(8,128)(2,1)} %param.3, f32[16,4096]{1,0:T(8,128)S(1)} %bitcast.61), kind=kLoop, calls=%fused_computation.17 | loop fusion | flops 12582912 | bytes 13107200 | tf_op jit(solution)/shard_map/convert_element_type | solution.py:65
  11.6 1.2 multiply_subtract_fusion
  12.8 2.2 %fusion.4 = (bf16[4096,256]{1,0:T(8,128)(2,1)S(1)}, bf16[4096,256]{1,0:T(8,128)(2,1)S(1)}) fusion(f32[64,64,256]{2,1,0:T(8,128)S(1)} %get-tuple-element.36, f32[4096]{0:T(1024)S(1)} %fusion.24, f32[64,64,256]{2,1,0:T(8,128)S(1)} %get-tuple-element.35, f32[4096]{0:T(1024)S(1)} %subtract_multiply_fusion), kind=kLoop, calls=%fused_computation.9 | loop fusion | flops 4194304 | bytes 12615680 | tf_op jit(solution)/shard_map/convert.8
  15.0 0.0 copy-start
  15.0 0.0 copy-start.2
  15.0 0.8 pad_maximum_fusion.1
  15.8 2.4 %fusion.26 = f32[512,512]{1,0:T(8,128)S(1)} fusion(bf16[512,4096]{1,0:T(8,128)(2,1)S(1)} %bitcast.58, bf16[4096,256]{1,0:T(8,128)(2,1)S(1)} %get-tuple-element.46, bf16[4096,256]{1,0:T(8,128)(2,1)S(1)} %get-tuple-element.47), kind=kOutput, calls=%fused_computation.64 | convolution fusion | flops 2155872256 | bytes 9437184 | tf_op jit(solution)/shard_map/dot_general | solution.py:59
  18.2 0.9 slice_add_fusion
  19.0 1.4 collective-permute-start.1
  20.4 0.0 slice-start
  20.4 0.0 copy-done
  20.4 0.0 copy-done.2
  20.4 0.0 slice-start.1
  20.4 2.4 %fusion.27 = f32[512,512]{1,0:T(8,128)S(1)} fusion(bf16[512,4096]{1,0:T(8,128)(2,1)S(1)} %bitcast.57, bf16[4096,256]{1,0:T(8,128)(2,1)S(1)} %get-tuple-element.46, bf16[4096,256]{1,0:T(8,128)(2,1)S(1)} %get-tuple-element.47), kind=kOutput, calls=%fused_computation.65 | convolution fusion | flops 2155872256 | bytes 9437184 | tf_op jit(solution)/shard_map/dot_general | solution.py:59
  22.8 0.9 slice_add_fusion.1
  23.7 1.6 collective-permute-start
  25.3 0.0 slice-done
  25.3 0.0 slice-done.1
  25.3 3.4 %fusion.32 = (bf16[16,3,16,4096]{3,2,1,0:T(8,128)(2,1)S(1)}, bf16[16,3,16,4096]{3,2,1,0:T(8,128)(2,1)}) fusion(bf16[16,4,16,4096]{3,2,1,0:T(8,128)(2,1)S(1)} %bitcast.50), kind=kLoop, calls=%fused_computation.70 | loop fusion | bytes 25165824 | tf_op jit(solution)/shard_map/slice | solution.py:78
  28.7 0.1 broadcast_in_dim.25
  28.8 0.9 copy.30
  29.7 8.9 %fusion.31 = (bf16[4,16,16,4096]{3,2,1,0:T(8,128)(2,1)}, f32[4,16,16,4096]{3,2,1,0:T(8,128)S(1)}) fusion(f32[16,4096]{1,0:T(8,128)S(1)} %bitcast.62, bf16[16,4,16,4096]{3,2,1,0:T(8,128)(2,1)S(1)} %bitcast.50, f32[16,4096]{1,0:T(8,128)} %bitcast.66, f32[16,4096]{1,0:T(8,128)S(1)} %bitcast.60, bf16[16,3,16,4096]{3,2,1,0:T(8,128)(2,1)S(1)} %get-tuple-element.29, ...), kind=kLoop, calls=%fused_computation.69 | loop fusion | flops 37748736 | bytes 46923776 | tf_op jit(solution)/shard_map/convert_element_type | solution.py:82
  38.6 3.0 %subtract_convert_fusion.2 = (bf16[1,16,16,4096]{3,2,1,0:T(8,128)(2,1)}, bf16[1,16,16,4096]{3,2,1,0:T(8,128)(2,1)}) fusion(f32[4,16,16,4096]{3,2,1,0:T(8,128)S(1)} %get-tuple-element.20), kind=kLoop, calls=%fused_computation.18 | loop fusion | flops 8388608 | bytes 12582912 | tf_op jit(solution)/shard_map/convert_element_type | solution.py:66
  41.6 0.0 copy-start.1
  41.6 0.0 copy-start.3
  41.6 0.0 copy-start.5
  41.6 8.4 %fusion.30 = f32[512,1024]{1,0:T(8,128)S(1)} fusion(bf16[1024,4096]{1,0:T(8,128)(2,1)} %bitcast.56, bf16[4096,256]{1,0:T(8,128)(2,1)} %copy-done, bf16[4096,256]{1,0:T(8,128)(2,1)} %copy-done.2), kind=kOutput, calls=%fused_computation.68 | convolution fusion | flops 4303355904 | bytes 14680064 | tf_op jit(solution)/shard_map/dot_general | solution.py:59
  50.0 0.0 copy-done.1
  50.0 0.0 copy-done.3
  50.0 0.0 copy-done.5
  50.0 0.0 copy-start.4
  50.0 1.3 fusion.28
  51.3 0.3 copy-done.4
  51.6 1.3 fusion.29
  53.0 0.1 slice.107
  53.0 0.0 collective-permute-done.1
  53.0 0.0 collective-permute-done
  53.1 1.4 add_convert_fusion.1
  54.5 0.1 copy_bitcast_fusion
  54.6 16.1 %all_to_all.5 = bf16[8,2,32,1024]{3,2,1,0:T(8,128)(2,1)S(1)} all-to-all(bf16[8,2,32,1024]{3,2,1,0:T(8,128)(2,1)S(1)} %copy_bitcast_fusion), channel_id=1, replica_groups=mesh['az'=16,'tm'=8] {'tm'}, dimensions={0} | all-to-all | bytes 2097152 | tf_op jit(solution)/shard_map/all_to_all | solution.py:94
  70.8 3.1 %copy.21 = bf16[8,2,32,1024]{2,3,1,0:T(8,128)(2,1)} copy(bf16[8,2,32,1024]{3,2,1,0:T(8,128)(2,1)S(1)} %all_to_all.5) | data formatting | bytes 2097152 | tf_op jit(solution)/shard_map/all_to_all | solution.py:94
  73.8 6.6 %copy.22 = bf16[32,64,8,2,16]{1,4,3,2,0:T(8,128)(2,1)S(1)} copy(bf16[32,64,8,2,16]{0,4,1,3,2:T(8,128)(2,1)} %bitcast.51) | data formatting | bytes 2097152 | tf_op jit(solution)/shard_map/transpose | solution.py:95
  80.5 1.6 copy.27
  82.1 0.0 all-gather.2.cloned.1.call-update
  82.1 2.6 %fusion.33 = (bf16[32,64,8,1,16]{0,4,1,3,2:T(8,128)(2,1)S(1)}, bf16[32,64,8,1,16]{0,4,1,3,2:T(8,128)(2,1)S(1)}) fusion(bf16[32,64,8,2,16]{0,4,1,3,2:T(8,128)(2,1)} %bitcast.52), kind=kLoop, calls=%fused_computation.71 | loop fusion | flops 262144 | bytes 2097152 | tf_op jit(solution)/shard_map/slice | solution.py:98
  84.7 2.9 %pad_maximum_fusion.3 = bf16[32,64,8,2,16]{0,4,1,3,2:T(8,128)(2,1)} fusion(bf16[32,64,8,1,16]{0,4,1,3,2:T(8,128)(2,1)S(1)} %get-tuple-element.32, bf16[32,64,8,1,16]{0,4,1,3,2:T(8,128)(2,1)S(1)} %get-tuple-element.31), kind=kLoop, calls=%fused_computation.7 | loop fusion | flops 524288 | bytes 2097152 | tf_op jit(solution)/shard_map/stack | solution.py:98
  87.7 7.4 %copy.23 = bf16[32,64,8,2,16]{1,4,3,2,0:T(8,128)(2,1)} copy(bf16[32,64,8,2,16]{0,4,1,3,2:T(8,128)(2,1)} %pad_maximum_fusion.3) | data formatting | bytes 2097152 | tf_op jit(solution)/shard_map/stack | solution.py:98
  95.1 2.1 copy.25
  97.2 1.6 copy.24
  98.8 96.9 %all-gather.2.cloned.1.call-done = bf16[32,1024,256]{2,1,0:T(8,128)(2,1)} async-done(((bf16[32,64,256]{2,1,0:T(8,128)(2,1)}), bf16[32,1024,256]{2,1,0:T(8,128)(2,1)}) %all-gather.2.cloned.1.call-update) | async-done | bytes 16777232 | tf_op jit(solution)/shard_map/all_gather | solution.py:100
  195.7 12.9 %broadcast_multiply_fusion = f32[32,2,64,1024]{3,2,1,0:T(8,128)} fusion(bf16[32,1024,256]{2,1,0:T(8,128)(2,1)} %all-gather.2.cloned.1.call-done, bf16[32,1,64,256]{3,2,1,0:T(8,128)(2,1)S(1)} %copy.25, bf16[32,1,64,256]{3,2,1,0:T(8,128)(2,1)} %copy.24), kind=kOutput, calls=%fused_computation.3 | convolution fusion | flops 2152726528 | bytes 35651584 | tf_op jit(solution)/shard_map/fcqk,fpk->fcqp/dot_general | solution.py:101
  (3 shorter events, 0.0 us)
Async XLA Ops:
  6.5 189.2 %all-gather.2.cloned.1.call-start = ((), (), s32[]{:S(2)}) async-start(), calls=%async_computation.1 | async-start | bytes 17825792 | tf_op jit(solution)/shard_map/all_gather | solution.py:100
  15.0 5.4 %copy-start = (bf16[4096,256]{1,0:T(8,128)(2,1)}, bf16[4096,256]{1,0:T(8,128)(2,1)S(1)}, u32[]{:S(2)}) copy-start(bf16[4096,256]{1,0:T(8,128)(2,1)S(1)} %get-tuple-element.46) | copy-start | bytes 6291460
  15.0 5.4 %copy-start.2 = (bf16[4096,256]{1,0:T(8,128)(2,1)}, bf16[4096,256]{1,0:T(8,128)(2,1)S(1)}, u32[]{:S(2)}) copy-start(bf16[4096,256]{1,0:T(8,128)(2,1)S(1)} %get-tuple-element.47) | copy-start | bytes 6291460
  19.0 34.0 %collective-permute-start.1 = (f32[512,256]{1,0:T(8,128)}, f32[512,256]{1,0:T(8,128)}, u32[]{:S(2)}, u32[]{:S(2)}) collective-permute-start(f32[512,256]{1,0:T(8,128)} %slice_add_fusion), channel_id=1, source_target_pairs={{8,0},{16,8},{24,16},{32,24},{40,32},{48,40},{56,48},{64,56},{72,6... | collective-permute-start | bytes 1572872 | tf_op jit(solution)/shard_map/ppermute | solution.py:76
  20.4 4.9 %slice-start = ((s8[8388608]{0:T(1024)(128)(4,1)}), s8[4194304]{0:T(1024)(128)(4,1)S(1)}, s32[]{:S(2)}) async-start(s8[8388608]{0:T(1024)(128)(4,1)} %bitcast.49), calls=%async_computation.2 | async-start | bytes 8388608
  20.4 4.9 %slice-start.1 = ((s8[8388608]{0:T(1024)(128)(4,1)}), s8[4194304]{0:T(1024)(128)(4,1)S(1)}, s32[]{:S(2)}) async-start(s8[8388608]{0:T(1024)(128)(4,1)} %bitcast.49), calls=%async_computation.3 | async-start | bytes 8388608
  23.7 29.4 %collective-permute-start = (f32[512,256]{1,0:T(8,128)}, f32[512,256]{1,0:T(8,128)}, u32[]{:S(2)}, u32[]{:S(2)}) collective-permute-start(f32[512,256]{1,0:T(8,128)} %slice_add_fusion.1), channel_id=1, source_target_pairs={{0,8},{8,16},{16,24},{24,32},{32,40},{40,48},{48,56},{56,64},{64,7... | collective-permute-start | bytes 1572872 | tf_op jit(solution)/shard_map/ppermute | solution.py:75
  41.6 8.4 %copy-start.1 = (bf16[4096,256]{1,0:T(8,128)(2,1)S(1)}, bf16[4096,256]{1,0:T(8,128)(2,1)}, u32[]{:S(2)}) copy-start(bf16[4096,256]{1,0:T(8,128)(2,1)} %copy-done) | copy-start | bytes 6291460
  41.6 8.4 %copy-start.3 = (bf16[4096,256]{1,0:T(8,128)(2,1)S(1)}, bf16[4096,256]{1,0:T(8,128)(2,1)}, u32[]{:S(2)}) copy-start(bf16[4096,256]{1,0:T(8,128)(2,1)} %copy-done.2) | copy-start | bytes 6291460
  41.6 8.4 %copy-start.5 = (bf16[1,16,16,4096]{3,2,1,0:T(8,128)(2,1)S(1)}, bf16[1,16,16,4096]{3,2,1,0:T(8,128)(2,1)}, u32[]{:S(2)}) copy-start(bf16[1,16,16,4096]{3,2,1,0:T(8,128)(2,1)} %get-tuple-element.21) | copy-start | bytes 6291460
  50.0 1.6 copy-start.4
Sparse Core Ops, SparseCore 0:
  82.2 113.4 all-gather.1

commit v16 on v5

--- a/solution.py
+++ b/solution.py
@@ -59,13 +59,13 @@
         prev = jnp.concatenate([left, block[:, :-1]], axis=1).astype(jnp.float32)
         nxt = jnp.concatenate([block[:, 1:], right], axis=1).astype(jnp.float32)
         total = weights[0] * prev + weights[1] * block.astype(jnp.float32) + weights[2] * nxt
-        virtual = total.astype(jnp.bfloat16).reshape(cycles * sector * nb, length)
+        virtual = total.astype(jnp.bfloat16).transpose(1, 0, 2, 3).reshape(cycles * sector * nb, length)
         spectra = lax.dot_general(
             table, virtual, (((0,), (1,)), ((), ())), preferred_element_type=jnp.float32
         ).astype(jnp.bfloat16)
         spectra = spectra.reshape(2, n_tm, fl, cycles * sector * nb).transpose(1, 0, 2, 3)
         shared = lax.all_to_all(spectra, "tm", 0, 0, tiled=True)
-        x = shared.reshape(n_tm, 2, fl, cycles, sector, nb).transpose(2, 4, 3, 0, 1, 5)
+        x = shared.reshape(n_tm, 2, fl, local_rows, nb).transpose(2, 3, 0, 1, 4)
         x = x.reshape(fl, local_rows, n_tm, 2, nb)
         rows = x.reshape(fl, local_rows, n_tm * 2 * nb)
         turned = jnp.stack([x[:, :, :, 1], -x[:, :, :, 0]], 3).reshape(rows.shape)

time: 214 us -> 213 us (level)
  waiting for transfers between devices: 116 us -> 110 us
  blocking collectives: 15.2 us -> 17.8 us
    ppermute x1, waiting for transfers between devices: 0.01 us -> 12.9 us  [shards(): left = lax.ppermute(block[:, sector - 1:], 'az', forward)]
    ppermute x1, waiting for transfers between devices: 14.1 us -> 2.99 us  [shards(): right = lax.ppermute(block[:, :1], 'az', backward)]
    all_gather x1, waiting for transfers between devices: 102 us -> 93.8 us  [shards(): columns = lax.all_gather(rows, 'az', axis=1, tiled=True)]
    another operation x2, local copies, waits for them, and re-layouts: 7.81 us -> 3.75 us  [shards(): lhs = jnp.stack([rows, turned], 1)]
    all_to_all x1, blocking collectives: 15.2 us -> 17.8 us  [shards(): shared = lax.all_to_all(spectra, 'tm', 0, 0, tiled=True)]
    another operation x1, local copies, waits for them, and re-layouts: 4.85 us -> 7.45 us  [shards(): turned = jnp.stack([x[:, :, :, 1], -x[:, :, :, 0]], 3).reshape(rows.shape)]
  transfers between devices with their start and end apart: 3 -> 3, of which waited for: 2 -> 3; matrix products, arithmetic and copies ran while one was open for 11% -> 12% of each run, Pallas kernels for 0% -> 0%
where the time goes in v16:
time: 213 us; the launch traced here: 212 us
  waiting for transfers between devices  110 us (52%)
  local copies, waits for them, and re-layouts  30.5 us (14%)
  matrix products  19.7 us (9%)
  other arithmetic  17.8 us (8%)
  blocking collectives  17.8 us (8%)
  between operations  13.6 us (6%)
  starting transfers between devices  3.16 us (1%)
    all_gather x1, waiting for transfers between devices, shards(): columns = lax.all_gather(rows, 'az', axis=1, tiled=True)  93.8 us
    all_to_all x1, blocking collectives, shards(): shared = lax.all_to_all(spectra, 'tm', 0, 0, tiled=True)  17.8 us
    dot_general x1, matrix products, shards(): jnp.einsum('fcqk,fpk->fcqp', lhs, columns, preferred_element_type=jnp.flo...  12.9 us
    ppermute x1, waiting for transfers between devices, shards(): left = lax.ppermute(block[:, sector - 1:], 'az', forward)  12.9 us
    another operation x1, local copies, waits for them, and re-layouts, shards(): turned = jnp.stack([x[:, :, :, 1], -x[:, :, :, 0]], 3).reshape(rows.shape)  7.45 us
    convert_element_type x1, other arithmetic, shards(): total.astype(jnp.bfloat16).transpose(1, 0, 2, 3)  7.4 us
    dot_general x1, matrix products, shards(): lax.dot_general(table, virtual, (((0,), (1,)), ((), ())), preferred_eleme...  6.81 us
    transpose x1, local copies, waits for them, and re-layouts, shards(): x = shared.reshape(n_tm, 2, fl, local_rows, nb).transpose(2, 3, 0, 1, 4)  6.64 us
  transfers between devices with their start and end apart: 3, of which 3 were waited for; matrix products, arithmetic and copies ran while one was open for 12% of the time, Pallas kernels for 0%

profile of v16, /device:TPU:1, one launch (start us, length us, event | category | flops | bytes accessed | tf_op | source)
XLA Modules:
  0.0 212.3 jit_solution(4386814092186905587)
XLA Ops:
  6.5 0.0 all-gather.2.cloned.1.call-start
  6.5 2.7 %fusion.33 = (bf16[16,1,16,4096]{3,2,1,0:T(8,128)(2,1)S(1)}, bf16[16,1,16,4096]{3,2,1,0:T(8,128)(2,1)S(1)}) fusion(bf16[16,4,16,4096]{3,2,1,0:T(8,128)(2,1)} %param.3), kind=kLoop, calls=%fused_computation.52 | loop fusion | bytes 8388608 | tf_op jit(solution)/shard_map/slice | solution.py:57
  9.3 0.0 copy-start
  9.3 0.0 copy-start.1
  9.3 0.1 copy.37
  9.4 3.1 %collective-permute-start = (bf16[16,1,16,4096]{3,2,0,1:T(8,128)(2,1)S(1)}, bf16[16,1,16,4096]{3,2,0,1:T(8,128)(2,1)S(1)}, u32[]{:S(2)}, u32[]{:S(2)}) collective-permute-start(bf16[16,1,16,4096]{3,2,0,1:T(8,128)(2,1)S(1)} %copy.37), channel_id=1, source_target_pairs={{0,8},{8,16},{16,24},{24,32},{32,40},{40,48},{48,56},{56,64},{64,7... | collective-permute-start | bytes 6291464 | tf_op jit(solution)/shard_map/ppermute | solution.py:56
  12.5 0.1 copy.38
  12.7 0.1 collective-permute-start.1
  12.8 0.1 fusion.29
  12.8 0.1 subtract_multiply_fusion
  12.9 0.3 fusion.25
  13.2 0.3 fusion.27
  13.5 0.0 copy-done
  13.5 0.0 copy-done.1
  13.6 0.1 broadcast_in_dim.22
  13.7 0.9 copy.31
  14.6 0.1 broadcast_in_dim.26
  14.7 0.9 copy.33
  15.5 0.1 broadcast_in_dim.24
  15.6 0.9 copy.32
  16.5 0.0 slice-start
  16.5 0.9 multiply_subtract_fusion
  17.4 0.0 slice-start.1
  17.4 3.2 %fusion.8 = (bf16[4096,256]{1,0:T(8,128)(2,1)}, bf16[4096,256]{1,0:T(8,128)(2,1)}) fusion(f32[64,64,256]{2,1,0:T(8,128)S(1)} %get-tuple-element.20, f32[4096]{0:T(1024)S(1)} %fusion.29, f32[64,64,256]{2,1,0:T(8,128)S(1)} %get-tuple-element.19, f32[4096]{0:T(1024)S(1)} %subtract_multiply_fusion), kind=kLoop, calls=%fused_computation.10 | loop fusion | flops 4194304 | bytes 12615680 | tf_op jit(solution)/shard_map/convert.1
  20.6 0.0 slice-done
  20.6 0.5 slice-done.1
  21.1 1.5 fusion.32
  22.6 12.9 %collective-permute-done = bf16[16,1,16,4096]{3,2,0,1:T(8,128)(2,1)S(1)} collective-permute-done((bf16[16,1,16,4096]{3,2,0,1:T(8,128)(2,1)S(1)}, bf16[16,1,16,4096]{3,2,0,1:T(8,128)(2,1)S(1)}, u32[]{:S(2)}, u32[]{:S(2)}) %collective-permute-start) | collective-permute-done | bytes 2097184 | tf_op jit(solution)/shard_map/ppermute | solution.py:56
  35.5 3.0 %collective-permute-done.1 = bf16[16,1,16,4096]{3,2,0,1:T(8,128)(2,1)S(1)} collective-permute-done((bf16[16,1,16,4096]{3,2,0,1:T(8,128)(2,1)S(1)}, bf16[16,1,16,4096]{3,2,0,1:T(8,128)(2,1)S(1)}, u32[]{:S(2)}, u32[]{:S(2)}) %collective-permute-start.1) | collective-permute-done | bytes 2097184 | tf_op jit(solution)/shard_map/ppermute | solution.py:57
  38.5 7.4 %add_convert_fusion = bf16[16,4,16,4096]{3,2,0,1:T(8,128)(2,1)S(1)} fusion(bf16[16,1,16,4096]{3,2,0,1:T(8,128)(2,1)S(1)} %collective-permute-done, bf16[16,1,16,4096]{3,2,0,1:T(8,128)(2,1)S(1)} %collective-permute-done.1, f32[16,4096]{1,0:T(8,128)} %bitcast.49, f32[16,4096]{1,0:T(8,128)} %bitcast.50, f32[16,4096]{1,0:T(8,128)} %bitcast.48, ...), kind=kLoop, calls=%fused_computation.2 | loop fusion | flops 62914560 | bytes 34340864 | tf_op jit(solution)/shard_map/convert_element_type | solution.py:62
  45.9 6.8 %fusion.13 = bf16[512,1024]{1,0:T(8,128)(2,1)S(1)} fusion(bf16[1024,4096]{1,0:T(8,128)(2,1)S(1)} %bitcast.46, bf16[4096,256]{1,0:T(8,128)(2,1)} %get-tuple-element.28, bf16[4096,256]{1,0:T(8,128)(2,1)} %get-tuple-element.29), kind=kOutput, calls=%fused_computation.19 | convolution fusion | flops 4303880192 | bytes 13631488 | tf_op jit(solution)/shard_map/dot_general | solution.py:63
  52.7 0.1 copy.44
  52.8 17.8 %all_to_all.5 = bf16[8,2,32,1024]{3,2,1,0:T(8,128)(2,1)S(1)} all-to-all(bf16[8,2,32,1024]{3,2,1,0:T(8,128)(2,1)S(1)} %bitcast.47), channel_id=1, replica_groups=mesh['az'=16,'tm'=8] {'tm'}, dimensions={0} | all-to-all | bytes 2097152 | tf_op jit(solution)/shard_map/all_to_all | solution.py:67
  70.6 3.1 %copy.23 = bf16[8,2,32,1024]{2,3,1,0:T(8,128)(2,1)} copy(bf16[8,2,32,1024]{3,2,1,0:T(8,128)(2,1)S(1)} %all_to_all.5) | data formatting | bytes 2097152 | tf_op jit(solution)/shard_map/all_to_all | solution.py:67
  73.7 6.6 %copy.24 = bf16[32,64,8,2,16]{1,4,3,2,0:T(8,128)(2,1)S(1)} copy(bf16[32,64,8,2,16]{0,4,1,3,2:T(8,128)(2,1)} %bitcast.41) | data formatting | bytes 2097152 | tf_op jit(solution)/shard_map/transpose | solution.py:68
  80.3 1.6 copy.29
  81.9 0.0 all-gather.2.cloned.1.call-update
  82.0 2.6 %fusion.34 = (bf16[32,64,8,1,16]{0,4,1,3,2:T(8,128)(2,1)S(1)}, bf16[32,64,8,1,16]{0,4,1,3,2:T(8,128)(2,1)S(1)}) fusion(bf16[32,64,8,2,16]{0,4,1,3,2:T(8,128)(2,1)} %bitcast.42), kind=kLoop, calls=%fused_computation.53 | loop fusion | flops 262144 | bytes 2097152 | tf_op jit(solution)/shard_map/slice | solution.py:71
  84.6 2.9 %pad_maximum_fusion = bf16[32,64,8,2,16]{0,4,1,3,2:T(8,128)(2,1)} fusion(bf16[32,64,8,1,16]{0,4,1,3,2:T(8,128)(2,1)S(1)} %get-tuple-element.18, bf16[32,64,8,1,16]{0,4,1,3,2:T(8,128)(2,1)S(1)} %get-tuple-element.17), kind=kLoop, calls=%fused_computation.8 | loop fusion | flops 524288 | bytes 2097152 | tf_op jit(solution)/shard_map/stack | solution.py:71
  87.5 7.5 %copy.25 = bf16[32,64,8,2,16]{1,4,3,2,0:T(8,128)(2,1)} copy(bf16[32,64,8,2,16]{0,4,1,3,2:T(8,128)(2,1)} %pad_maximum_fusion) | data formatting | bytes 2097152 | tf_op jit(solution)/shard_map/stack | solution.py:71
  95.0 2.1 %copy.27 = bf16[32,1,64,256]{3,2,1,0:T(8,128)(2,1)S(1)} copy(bf16[32,1,64,256]{2,3,0,1:T(8,128)(2,1)} %bitcast.45) | data formatting | bytes 2097152 | tf_op jit(solution)/shard_map/stack;reshape | solution.py:72
  97.1 1.6 copy.26
  98.8 93.8 %all-gather.2.cloned.1.call-done = bf16[32,1024,256]{2,1,0:T(8,128)(2,1)} async-done(((bf16[32,64,256]{2,1,0:T(8,128)(2,1)}), bf16[32,1024,256]{2,1,0:T(8,128)(2,1)}) %all-gather.2.cloned.1.call-update) | async-done | bytes 16777232 | tf_op jit(solution)/shard_map/all_gather | solution.py:73
  192.5 12.9 %broadcast_multiply_fusion = f32[32,2,64,1024]{3,2,1,0:T(8,128)} fusion(bf16[32,1024,256]{2,1,0:T(8,128)(2,1)} %all-gather.2.cloned.1.call-done, bf16[32,1,64,256]{3,2,1,0:T(8,128)(2,1)S(1)} %copy.27, bf16[32,1,64,256]{3,2,1,0:T(8,128)(2,1)} %copy.26), kind=kOutput, calls=%fused_computation.3 | convolution fusion | flops 2152726528 | bytes 35651584 | tf_op jit(solution)/shard_map/fcqk,fpk->fcqp/dot_general | solution.py:74
  (4 shorter events, 0.0 us)
Async XLA Ops:
  6.5 186.0 %all-gather.2.cloned.1.call-start = ((), (), s32[]{:S(2)}) async-start(), calls=%async_computation.1 | async-start | bytes 17825792 | tf_op jit(solution)/shard_map/all_gather | solution.py:73
  9.3 4.3 %copy-start = (f32[16,16]{1,0:T(8,128)S(1)}, f32[16,16]{1,0:T(8,128)}, u32[]{:S(2)}) copy-start(f32[16,16]{1,0:T(8,128)} %param.5) | copy-start | bytes 3076
  9.3 4.3 %copy-start.1 = (s32[16,16]{1,0:T(8,128)S(1)}, s32[16,16]{1,0:T(8,128)}, u32[]{:S(2)}) copy-start(s32[16,16]{1,0:T(8,128)} %param.4) | copy-start | bytes 3076
  9.4 26.1 %collective-permute-start = (bf16[16,1,16,4096]{3,2,0,1:T(8,128)(2,1)S(1)}, bf16[16,1,16,4096]{3,2,0,1:T(8,128)(2,1)S(1)}, u32[]{:S(2)}, u32[]{:S(2)}) collective-permute-start(bf16[16,1,16,4096]{3,2,0,1:T(8,128)(2,1)S(1)} %copy.37), channel_id=1, source_target_pairs={{0,8},{8,16},{16,24},{24,32},{32,40},{40,48},{48,56},{56,64},{64,7... | collective-permute-start | bytes 6291464 | tf_op jit(solution)/shard_map/ppermute | solution.py:56
  12.7 25.8 %collective-permute-start.1 = (bf16[16,1,16,4096]{3,2,0,1:T(8,128)(2,1)S(1)}, bf16[16,1,16,4096]{3,2,0,1:T(8,128)(2,1)S(1)}, u32[]{:S(2)}, u32[]{:S(2)}) collective-permute-start(bf16[16,1,16,4096]{3,2,0,1:T(8,128)(2,1)S(1)} %copy.38), channel_id=1, source_target_pairs={{8,0},{16,8},{24,16},{32,24},{40,32},{48,40},{56,48},{64,56},{72,6... | collective-permute-start | bytes 6291464 | tf_op jit(solution)/shard_map/ppermute | solution.py:57
  16.5 4.1 %slice-start = ((s8[8388608]{0:T(1024)(128)(4,1)}), s8[4194304]{0:T(1024)(128)(4,1)S(1)}, s32[]{:S(2)}) async-start(s8[8388608]{0:T(1024)(128)(4,1)} %bitcast.39), calls=%async_computation.2 | async-start | bytes 8388608
  17.4 3.7 %slice-start.1 = ((s8[8388608]{0:T(1024)(128)(4,1)}), s8[4194304]{0:T(1024)(128)(4,1)S(1)}, s32[]{:S(2)}) async-start(s8[8388608]{0:T(1024)(128)(4,1)} %bitcast.39), calls=%async_computation.3 | async-start | bytes 8388608
Sparse Core Ops, SparseCore 0:
  82.1 110.3 all-gather.1

commit v17 on v16

--- a/solution.py
+++ b/solution.py
@@ -56,13 +56,24 @@
         left = lax.ppermute(block[:, sector - 1 :], "az", forward)
         right = lax.ppermute(block[:, :1], "az", backward)
         weights = all_weights[:, :, :, j * nb : (j + 1) * nb]
-        prev = jnp.concatenate([left, block[:, :-1]], axis=1).astype(jnp.float32)
-        nxt = jnp.concatenate([block[:, 1:], right], axis=1).astype(jnp.float32)
-        total = weights[0] * prev + weights[1] * block.astype(jnp.float32) + weights[2] * nxt
-        virtual = total.astype(jnp.bfloat16).transpose(1, 0, 2, 3).reshape(cycles * sector * nb, length)
-        spectra = lax.dot_general(
-            table, virtual, (((0,), (1,)), ((), ())), preferred_element_type=jnp.float32
-        ).astype(jnp.bfloat16)
+
+        def transform(total):
+            rows = total.astype(jnp.bfloat16).transpose(1, 0, 2, 3).reshape(-1, length)
+            return lax.dot_general(
+                table, rows, (((0,), (1,)), ((), ())), preferred_element_type=jnp.float32
+            )
+
+        def virtual(prev, mid, nxt):
+            return (
+                weights[0] * prev.astype(jnp.float32)
+                + weights[1] * mid.astype(jnp.float32)
+                + weights[2] * nxt.astype(jnp.float32)
+            )
+
+        inner = transform(virtual(block[:, :-2], block[:, 1:-1], block[:, 2:]))
+        first = transform(virtual(left, block[:, :1], block[:, 1:2]))
+        last = transform(virtual(block[:, -2:-1], block[:, -1:], right))
+        spectra = jnp.concatenate([first, inner, last], axis=1).astype(jnp.bfloat16)
         spectra = spectra.reshape(2, n_tm, fl, cycles * sector * nb).transpose(1, 0, 2, 3)
         shared = lax.all_to_all(spectra, "tm", 0, 0, tiled=True)
         x = shared.reshape(n_tm, 2, fl, local_rows, nb).transpose(2, 3, 0, 1, 4)

time: 213 us -> 210 us (0.986)
  waiting for transfers between devices: 110 us -> 97.2 us
  local copies, waits for them, and re-layouts: 30.5 us -> 40.4 us
  other arithmetic: 17.8 us -> 21.8 us
    ppermute x1, waiting for transfers between devices: 12.9 us -> 0.01 us  [shards(): left = lax.ppermute(block[:, sector - 1:], 'az', forward)]
    dot_general x0 -> x1, local copies, waits for them, and re-layouts: none -> 6.38 us  [transform(): lax.dot_general(table, rows, (((0,), (1,)), ((), ())), preferred_element_...]
    slice x2, local copies, waits for them, and re-layouts: 4.21 us -> 9.72 us  [the longest x1 5.01 us: shards(): left = lax.ppermute(block[:, sector - 1:], 'az', forward)]
    all_gather x1, waiting for transfers between devices: 93.8 us -> 97.2 us  [shards(): columns = lax.all_gather(rows, 'az', axis=1, tiled=True)]
    ppermute x1, waiting for transfers between devices: 2.99 us -> 0.01 us  [shards(): right = lax.ppermute(block[:, :1], 'az', backward)]
    dot_general x0 -> x1, other arithmetic: none -> 2.35 us  [transform(): lax.dot_general(table, rows, (((0,), (1,)), ((), ())), preferred_element_...]
    convert_element_type x1 -> x2, other arithmetic: 7.4 us -> 9.63 us  [transform(): rows = total.astype(jnp.bfloat16).transpose(1, 0, 2, 3).reshape(-1, length)]
    dot_general x1 -> x3, matrix products: 6.81 us -> 4.93 us  [transform(): lax.dot_general(table, rows, (((0,), (1,)), ((), ())), preferred_element_...]
  transfers between devices with their start and end apart: 3 -> 3, of which waited for: 3 -> 1; matrix products, arithmetic and copies ran while one was open for 12% -> 21% of each run, Pallas kernels for 0% -> 0%
where the time goes in v17:
time: 210 us
  waiting for transfers between devices  97.2 us (46%)
  local copies, waits for them, and re-layouts  40.4 us (19%)
  other arithmetic  21.8 us (10%)
  matrix products  17.8 us (8%)
  blocking collectives  15.9 us (8%)
  between operations  13.6 us (6%)
  starting transfers between devices  3.02 us (1%)
    all_gather x1, waiting for transfers between devices, shards(): columns = lax.all_gather(rows, 'az', axis=1, tiled=True)  97.2 us
    all_to_all x1, blocking collectives, shards(): shared = lax.all_to_all(spectra, 'tm', 0, 0, tiled=True)  15.9 us
    dot_general x1, matrix products, shards(): jnp.einsum('fcqk,fpk->fcqp', lhs, columns, preferred_element_type=jnp.flo...  12.9 us
    convert_element_type x2, other arithmetic, transform(): rows = total.astype(jnp.bfloat16).transpose(1, 0, 2, 3).reshape(-1, length)  9.63 us
    another operation x1, local copies, waits for them, and re-layouts, shards(): turned = jnp.stack([x[:, :, :, 1], -x[:, :, :, 0]], 3).reshape(rows.shape)  7.36 us
    transpose x1, local copies, waits for them, and re-layouts, shards(): x = shared.reshape(n_tm, 2, fl, local_rows, nb).transpose(2, 3, 0, 1, 4)  6.64 us
    dot_general x1, local copies, waits for them, and re-layouts, transform(): lax.dot_general(table, rows, (((0,), (1,)), ((), ())), preferred_element_...  6.38 us
    slice x1, local copies, waits for them, and re-layouts, shards(): left = lax.ppermute(block[:, sector - 1:], 'az', forward)  5.01 us
  transfers between devices with their start and end apart: 3, of which 1 were waited for; matrix products, arithmetic and copies ran while one was open for 21% of the time, Pallas kernels for 0%

profile of v17, /device:TPU:1, one launch (start us, length us, event | category | flops | bytes accessed | tf_op | source)
XLA Modules:
  0.0 209.8 jit_solution(10048177513454176142)
XLA Ops:
  6.5 0.0 all-gather.2.cloned.1.call-start
  6.5 0.0 copy-start
  6.5 5.0 %fusion.24 = (bf16[16,1,16,4096]{3,2,1,0:T(8,128)(2,1)}, bf16[16,1,16,4096]{3,2,1,0:T(8,128)(2,1)}) fusion(bf16[16,4,16,4096]{3,2,1,0:T(8,128)(2,1)} %param.3), kind=kLoop, calls=%fused_computation.51 | loop fusion | bytes 8388608 | tf_op jit(solution)/shard_map/slice | solution.py:56
  11.5 3.0 %collective-permute-start = (bf16[16,1,16,4096]{3,2,1,0:T(8,128)(2,1)}, bf16[16,1,16,4096]{3,2,1,0:T(8,128)(2,1)S(1)}, u32[]{:S(2)}, u32[]{:S(2)}) collective-permute-start(bf16[16,1,16,4096]{3,2,1,0:T(8,128)(2,1)} %get-tuple-element.15), channel_id=1, source_target_pairs={{0,8},{8,16},{16,24},{24,32},{32,40},{40,48},{48,56},{56,64},{64,7... | collective-permute-start | bytes 6291464 | tf_op jit(solution)/shard_map/ppermute | solution.py:56
  14.6 0.0 collective-permute-start.1
  14.6 0.1 fusion.22
  14.7 0.1 subtract_multiply_fusion
  14.7 0.0 copy-done
  14.7 0.0 copy-start.2
  14.8 0.0 copy-start.3
  14.8 4.7 %fusion.25 = (bf16[16,2,16,4096]{3,2,1,0:T(8,128)(2,1)}, bf16[16,2,16,4096]{3,2,1,0:T(8,128)(2,1)}, bf16[16,2,16,4096]{3,2,1,0:T(8,128)(2,1)}) fusion(bf16[16,4,16,4096]{3,2,1,0:T(8,128)(2,1)S(1)} %copy-done), kind=kLoop, calls=%fused_computation.52 | loop fusion | bytes 25165824 | tf_op jit(solution)/shard_map/slice | solution.py:73
  19.5 0.3 fusion.18
  19.7 0.3 fusion.20
  20.1 0.0 copy-done.2
  20.1 0.0 copy-done.3
  20.1 0.1 broadcast_in_dim.22
  20.2 0.2 copy.37
  20.4 0.1 broadcast_in_dim.26
  20.5 0.2 copy.39
  20.7 0.1 broadcast_in_dim.24
  20.8 0.2 copy.38
  20.9 1.2 multiply_subtract_fusion
  22.1 2.2 %fusion.4 = (bf16[4096,256]{1,0:T(8,128)(2,1)S(1)}, bf16[4096,256]{1,0:T(8,128)(2,1)S(1)}) fusion(f32[64,64,256]{2,1,0:T(8,128)S(1)} %get-tuple-element.23, f32[4096]{0:T(1024)S(1)} %fusion.22, f32[64,64,256]{2,1,0:T(8,128)S(1)} %get-tuple-element.22, f32[4096]{0:T(1024)S(1)} %subtract_multiply_fusion), kind=kLoop, calls=%fused_computation.7 | loop fusion | flops 4194304 | bytes 12615680 | tf_op jit(solution)/shard_map/convert.4
  24.3 2.3 %maximum_bitcast_fusion = bf16[512,4096]{0,1:T(8,128)(2,1)} fusion(bf16[4096,256]{1,0:T(8,128)(2,1)S(1)} %get-tuple-element.31, bf16[4096,256]{1,0:T(8,128)(2,1)S(1)} %get-tuple-element.32), kind=kLoop, calls=%fused_computation.4 | loop fusion | flops 8388608 | bytes 8388608 | tf_op jit(solution)/shard_map/dot_general | solution.py:62
  26.7 6.4 %copy.18 = bf16[512,4096]{1,0:T(8,128)(2,1)} copy(bf16[512,4096]{0,1:T(8,128)(2,1)} %maximum_bitcast_fusion) | data formatting | bytes 8388608 | tf_op jit(solution)/shard_map/dot_general | solution.py:62
  33.0 0.0 copy-start.1
  33.0 6.0 %add_convert_fusion = bf16[16,2,16,4096]{3,2,0,1:T(8,128)(2,1)S(1)} fusion(bf16[16,2,16,4096]{3,2,1,0:T(8,128)(2,1)} %get-tuple-element.19, bf16[16,2,16,4096]{3,2,1,0:T(8,128)(2,1)} %get-tuple-element.18, bf16[16,2,16,4096]{3,2,1,0:T(8,128)(2,1)} %get-tuple-element.17, f32[16,4096]{1,0:T(8,128)S(1)} %bitcast.72, f32[16,4096]{1,0:T(8,128)S(1)} %bitcast.74, ...), kind=kLoop, calls=%fused_computation.3 | loop fusion | flops 18874368 | bytes 17563648 | tf_op jit(solution)/shard_map/convert_element_type | solution.py:61
  39.1 0.0 slice-start
  39.1 0.0 copy-done.1
  39.1 0.0 slice-start.1
  39.1 2.4 %convolution_convert_fusion = bf16[2,8,32,512]{3,2,1,0:T(8,128)(2,1)S(1)} fusion(bf16[2,8,32,4096]{3,2,1,0:T(8,128)(2,1)S(1)} %bitcast.66, bf16[512,4096,1,1]{1,0,3,2:T(8,128)(2,1)S(1)} %bitcast.69), kind=kOutput, calls=%fused_computation.18 | convolution fusion | flops 2147745792 | bytes 8912896 | tf_op jit(solution)/shard_map/dot_general | solution.py:62
  41.4 0.0 collective-permute-done
  41.5 0.0 collective-permute-done.1
  41.5 0.0 slice-done
  41.5 1.0 slice-done.1
  42.5 3.6 %add_convert_fusion.2 = (bf16[16,1,16,4096]{3,2,1,0:T(8,128)(2,1)S(1)}, bf16[16,1,16,4096]{3,2,1,0:T(8,128)(2,1)S(1)}) fusion(bf16[16,1,16,4096]{3,2,1,0:T(8,128)(2,1)S(1)} %collective-permute-done, bf16[16,4,16,4096]{3,2,1,0:T(8,128)(2,1)S(1)} %bitcast.60, f32[16,4096]{1,0:T(8,128)S(1)} %bitcast.73, f32[16,4096]{1,0:T(8,128)S(1)} %bitcast.75, ...), kind=kLoop, calls=%fused_computation.11 | loop fusion | flops 18874368 | bytes 17563648 | tf_op jit(solution)/shard_map/convert_element_type | solution.py:61
  46.2 1.3 convolution_convert_fusion.1
  47.5 1.3 convolution_convert_fusion.2
  48.8 0.1 maximum_bitcast_fusion.1
  48.9 0.1 copy.22
  49.0 15.9 %all_to_all.5 = bf16[8,2,32,1024]{3,2,1,0:T(8,128)(2,1)S(1)} all-to-all(bf16[8,2,32,1024]{3,2,1,0:T(8,128)(2,1)S(1)} %copy.22), channel_id=1, replica_groups=mesh['az'=16,'tm'=8] {'tm'}, dimensions={0} | all-to-all | bytes 2097152 | tf_op jit(solution)/shard_map/all_to_all | solution.py:78
  64.9 3.1 %copy.23 = bf16[8,2,32,1024]{2,3,1,0:T(8,128)(2,1)} copy(bf16[8,2,32,1024]{3,2,1,0:T(8,128)(2,1)S(1)} %all_to_all.5) | data formatting | bytes 2097152 | tf_op jit(solution)/shard_map/all_to_all | solution.py:78
  68.0 6.6 %copy.24 = bf16[32,64,8,2,16]{1,4,3,2,0:T(8,128)(2,1)S(1)} copy(bf16[32,64,8,2,16]{0,4,1,3,2:T(8,128)(2,1)} %bitcast.61) | data formatting | bytes 2097152 | tf_op jit(solution)/shard_map/transpose | solution.py:79
  74.6 1.6 copy.29
  76.2 0.0 all-gather.2.cloned.1.call-update
  76.3 2.6 %fusion.26 = (bf16[32,64,8,1,16]{0,4,1,3,2:T(8,128)(2,1)S(1)}, bf16[32,64,8,1,16]{0,4,1,3,2:T(8,128)(2,1)S(1)}) fusion(bf16[32,64,8,2,16]{0,4,1,3,2:T(8,128)(2,1)} %bitcast.62), kind=kLoop, calls=%fused_computation.53 | loop fusion | flops 262144 | bytes 2097152 | tf_op jit(solution)/shard_map/slice | solution.py:82
  78.9 2.9 %pad_maximum_fusion = bf16[32,64,8,2,16]{0,4,1,3,2:T(8,128)(2,1)} fusion(bf16[32,64,8,1,16]{0,4,1,3,2:T(8,128)(2,1)S(1)} %get-tuple-element.21, bf16[32,64,8,1,16]{0,4,1,3,2:T(8,128)(2,1)S(1)} %get-tuple-element.20), kind=kLoop, calls=%fused_computation.5 | loop fusion | flops 524288 | bytes 2097152 | tf_op jit(solution)/shard_map/stack | solution.py:82
  81.8 7.4 %copy.25 = bf16[32,64,8,2,16]{1,4,3,2,0:T(8,128)(2,1)} copy(bf16[32,64,8,2,16]{0,4,1,3,2:T(8,128)(2,1)} %pad_maximum_fusion) | data formatting | bytes 2097152 | tf_op jit(solution)/shard_map/stack | solution.py:82
  89.2 2.1 %copy.27 = bf16[32,1,64,256]{3,2,1,0:T(8,128)(2,1)S(1)} copy(bf16[32,1,64,256]{2,3,0,1:T(8,128)(2,1)} %bitcast.65) | data formatting | bytes 2097152 | tf_op jit(solution)/shard_map/stack;reshape | solution.py:83
  91.3 1.6 copy.26
  92.9 97.2 %all-gather.2.cloned.1.call-done = bf16[32,1024,256]{2,1,0:T(8,128)(2,1)} async-done(((bf16[32,64,256]{2,1,0:T(8,128)(2,1)}), bf16[32,1024,256]{2,1,0:T(8,128)(2,1)}) %all-gather.2.cloned.1.call-update) | async-done | bytes 16777232 | tf_op jit(solution)/shard_map/all_gather | solution.py:84
  190.1 12.9 %broadcast_multiply_fusion = f32[32,2,64,1024]{3,2,1,0:T(8,128)} fusion(bf16[32,1024,256]{2,1,0:T(8,128)(2,1)} %all-gather.2.cloned.1.call-done, bf16[32,1,64,256]{3,2,1,0:T(8,128)(2,1)S(1)} %copy.27, bf16[32,1,64,256]{3,2,1,0:T(8,128)(2,1)} %copy.26), kind=kOutput, calls=%fused_computation.2 | convolution fusion | flops 2152726528 | bytes 35651584 | tf_op jit(solution)/shard_map/fcqk,fpk->fcqp/dot_general | solution.py:85
  (4 shorter events, 0.0 us)
Async XLA Ops:
  6.5 183.5 %all-gather.2.cloned.1.call-start = ((), (), s32[]{:S(2)}) async-start(), calls=%async_computation.1 | async-start | bytes 17825792 | tf_op jit(solution)/shard_map/all_gather | solution.py:84
  6.5 8.2 %copy-start = (bf16[16,4,16,4096]{3,2,1,0:T(8,128)(2,1)S(1)}, bf16[16,4,16,4096]{3,2,1,0:T(8,128)(2,1)}, u32[]{:S(2)}) copy-start(bf16[16,4,16,4096]{3,2,1,0:T(8,128)(2,1)} %param.3) | copy-start | bytes 25165828
  11.5 29.9 %collective-permute-start = (bf16[16,1,16,4096]{3,2,1,0:T(8,128)(2,1)}, bf16[16,1,16,4096]{3,2,1,0:T(8,128)(2,1)S(1)}, u32[]{:S(2)}, u32[]{:S(2)}) collective-permute-start(bf16[16,1,16,4096]{3,2,1,0:T(8,128)(2,1)} %get-tuple-element.15), channel_id=1, source_target_pairs={{0,8},{8,16},{16,24},{24,32},{32,40},{40,48},{48,56},{56,64},{64,7... | collective-permute-start | bytes 6291464 | tf_op jit(solution)/shard_map/ppermute | solution.py:56
  14.6 26.9 %collective-permute-start.1 = (bf16[16,1,16,4096]{3,2,1,0:T(8,128)(2,1)}, bf16[16,1,16,4096]{3,2,1,0:T(8,128)(2,1)}, u32[]{:S(2)}, u32[]{:S(2)}) collective-permute-start(bf16[16,1,16,4096]{3,2,1,0:T(8,128)(2,1)} %get-tuple-element.16), channel_id=1, source_target_pairs={{8,0},{16,8},{24,16},{32,24},{40,32},{48,40},{56,48},{64,56},{72,6... | collective-permute-start | bytes 6291464 | tf_op jit(solution)/shard_map/ppermute | solution.py:57
  14.7 5.4 %copy-start.2 = (f32[16,16]{1,0:T(8,128)S(1)}, f32[16,16]{1,0:T(8,128)}, u32[]{:S(2)}) copy-start(f32[16,16]{1,0:T(8,128)} %param.5) | copy-start | bytes 3076
  14.8 5.4 %copy-start.3 = (s32[16,16]{1,0:T(8,128)S(1)}, s32[16,16]{1,0:T(8,128)}, u32[]{:S(2)}) copy-start(s32[16,16]{1,0:T(8,128)} %param.4) | copy-start | bytes 3076
  33.0 6.0 %copy-start.1 = (bf16[512,4096]{1,0:T(8,128)(2,1)S(1)}, bf16[512,4096]{1,0:T(8,128)(2,1)}, u32[]{:S(2)}) copy-start(bf16[512,4096]{1,0:T(8,128)(2,1)} %copy.18) | copy-start | bytes 12582916
  39.1 2.4 %slice-start = ((s8[8388608]{0:T(1024)(128)(4,1)}), s8[4194304]{0:T(1024)(128)(4,1)S(1)}, s32[]{:S(2)}) async-start(s8[8388608]{0:T(1024)(128)(4,1)} %bitcast.59), calls=%async_computation.2 | async-start | bytes 8388608
  39.1 3.5 %slice-start.1 = ((s8[8388608]{0:T(1024)(128)(4,1)}), s8[4194304]{0:T(1024)(128)(4,1)S(1)}, s32[]{:S(2)}) async-start(s8[8388608]{0:T(1024)(128)(4,1)} %bitcast.59), calls=%async_computation.3 | async-start | bytes 8388608
Sparse Core Ops, SparseCore 0:
  76.4 113.6 all-gather.1
